TPU v7x, 512 devices: a whole 4x8x8 slice. The times are simulated.
512 devices in a mesh: req: 64 (over z, y_lo, x), tp: 8 (over y_hi, core).
Axes of the slice: x: 4, y: 8 (y_hi: 4, y_lo: 2; y = y_hi * 2 + y_lo), z: 8, core: 2. Of those that a mesh axis runs over, the one named last changes fastest.
Arguments:
- queries: bfloat16 [8192, 4096], P('req', 'tp'), may hold values from -48 to 48
- suffix_kv: bfloat16 [8192, 2, 2048], P('req', None, 'tp'), may hold values from -6 to 6
- window_kv: bfloat16 [2, 4096, 2, 2048], P(None, 'req', None, 'tp'), may hold values from -6 to 6
- sink_kv: bfloat16 [2, 4, 2, 2048], P(None, None, None, 'tp'), may hold values from -16 to 16
- lengths: int32 [64], P('req'), may hold values from 1 to 128, 4096 in all
- group_ids: int32 [64], replicated, may hold values from 0 to 1
- hidden_in: bfloat16 [8192, 2048], P('req', 'tp'), may hold values from -6 to 6
- router: bfloat16 [2048, 8], P('tp'), may hold values from -0.125 to 0.125
- picks: int32 [8192, 2], P('req'), may hold values from 0 to 7, all different within a row
Outputs:
- mixed: bfloat16 [8192, 4096], P('req', 'tp')
All inputs are finite; a program needn't handle non-finite values. No bound on the sum of `lengths` on one device may be relied on, other than what follows from the above.
Results may differ from a plain program's by a relative error of at most 0.0024.
Values may be sent and summed in bfloat16 or wider, within the bound.
No kernel may reach another device: no remote copies, remote signals or barrier semaphores. Data moves between devices by JAX's collectives and lax.ppermute only.
A program may use at most 64 MiB of HBM per device.

v0:
```python
import math

import jax
import jax.numpy as jnp
from jax import lax
from jax.sharding import PartitionSpec as P

HEAD_DIM = 128
PICKS = 2


def absorb(soft_state, query_heads, key_rows, value_rows, visible_of, tile_count, tile_rows):
    score_scale = 1.0 / math.sqrt(query_heads.shape[3])

    def one_tile(tile_index, carried):
        running_max, running_sum, weighted = carried
        first_row = tile_index * tile_rows
        scores = (
            jnp.einsum("qhpd,khd->qhpk", query_heads, key_rows, preferred_element_type=jnp.float32)
            * score_scale
        )
        query_pos = first_row + jnp.arange(tile_rows, dtype=jnp.int32)
        visible = visible_of(query_pos)[:, None, None, :]
        old_max = running_max
        old_sum = running_sum
        old_weighted = weighted
        new_max = jnp.maximum(old_max, jnp.max(jnp.where(visible, scores, -jnp.inf), axis=3))
        exponentials = jnp.where(visible, jnp.exp(scores - new_max[..., None]), 0.0)
        factor = jnp.exp(old_max - new_max)
        new_sum = old_sum * factor + jnp.sum(exponentials, axis=3)
        product = jnp.einsum(
            "qhpk,khd->qhpd",
            exponentials.astype(jnp.bfloat16),
            value_rows,
            preferred_element_type=jnp.float32,
        )
        new_weighted = old_weighted * factor[..., None] + product
        running_max = new_max
        running_sum = new_sum
        weighted = new_weighted
        return (running_max, running_sum, weighted)

    return lax.fori_loop(0, tile_count, one_tile, soft_state)


def keyed_blocks(soft_state, query_heads, kv_part, first_pos, rule, tile_count, tile_rows):
    part_rows = kv_part.shape[0]
    block_rows = math.gcd(part_rows, 512)
    head_count = query_heads.shape[1]
    head_dim = query_heads.shape[3]

    def one_block(block_index, carried):
        offset = block_index * block_rows
        kv_block = lax.dynamic_slice_in_dim(kv_part, offset, block_rows, 0)
        key_rows = kv_block[:, 0].reshape(block_rows, head_count, head_dim)
        value_rows = kv_block[:, 1].reshape(block_rows, head_count, head_dim)
        key_pos = first_pos + offset + jnp.arange(block_rows, dtype=jnp.int32)

        def visible_of(query_pos):
            if rule == "window":
                return key_pos[None, :] > query_pos[:, None]
            return key_pos[None, :] <= query_pos[:, None]

        return absorb(carried, query_heads, key_rows, value_rows, visible_of, tile_count, tile_rows)

    return lax.fori_loop(0, part_rows // block_rows, one_block, soft_state)


def body(queries, suffix_kv, window_kv, sink_kv, lengths, group_ids, hidden_in, router, picks):
    row_count = queries.shape[0]
    head_count = suffix_kv.shape[2] // HEAD_DIM
    query_heads = queries.reshape(row_count, head_count, PICKS, HEAD_DIM)
    partial_value = jnp.dot(hidden_in, router, preferred_element_type=jnp.float32)
    logits = lax.psum(partial_value, "tp")
    experts = jnp.arange(logits.shape[1], dtype=jnp.int32)
    chosen = jnp.sum(
        jnp.where(picks[:, :, None] == experts[None, None, :], logits[:, None, :], 0.0), axis=2
    )
    gate_values = jax.nn.sigmoid(chosen - chosen[:, ::-1])
    my_group = group_ids[lax.axis_index("req")]
    length = lengths[0]
    tile_rows = math.gcd(row_count, 128)
    tile_count = row_count // tile_rows
    running_max = jnp.full((row_count, head_count, PICKS), -jnp.inf, jnp.float32)
    running_sum = jnp.zeros((row_count, head_count, PICKS), jnp.float32)
    weighted = jnp.zeros((row_count, head_count, PICKS, HEAD_DIM), jnp.float32)
    soft_state = (running_max, running_sum, weighted)
    sink_rows = lax.dynamic_index_in_dim(sink_kv, my_group, 0, keepdims=False)
    sink_count = sink_rows.shape[0]
    sink_keys = sink_rows[:, 0].reshape(sink_count, head_count, HEAD_DIM)
    sink_values = sink_rows[:, 1].reshape(sink_count, head_count, HEAD_DIM)

    def sink_visible(query_pos):
        return jnp.ones((query_pos.shape[0], sink_count), jnp.bool_)

    soft_state = absorb(
        soft_state, query_heads, sink_keys, sink_values, sink_visible, tile_count, tile_rows
    )
    soft_state = keyed_blocks(
        soft_state, query_heads, suffix_kv, 0, "suffix", tile_count, tile_rows
    )
    outgoing = jnp.take(window_kv, group_ids, axis=0)
    received = lax.all_to_all(outgoing, "req", split_axis=0, concat_axis=0, tiled=True)
    gathered = received.reshape(-1, received.shape[2], received.shape[3])
    soft_state = keyed_blocks(soft_state, query_heads, gathered, 0, "window", tile_count, tile_rows)
    running_max, running_sum, weighted = soft_state
    attended = weighted / running_sum[..., None]
    positions = jnp.arange(row_count, dtype=jnp.int32)
    is_live = positions < length
    mixed_out = jnp.where(
        is_live[:, None, None, None], attended * gate_values[:, None, :, None], 0.0
    )
    return mixed_out.astype(jnp.bfloat16).reshape(row_count, head_count * PICKS * HEAD_DIM)


def solution(mesh):
    return jax.shard_map(
        body,
        mesh=mesh,
        in_specs=(
            P("req", "tp"),
            P("req", None, "tp"),
            P(None, "req", None, "tp"),
            P(None, None, None, "tp"),
            P("req"),
            P(),
            P("req", "tp"),
            P("tp", None),
            P("req", None),
        ),
        out_specs=P("req", "tp"),
        check_vma=False,
    )
```

profile of v0, /device:TPU:40, one launch (start us, length us, event | category | flops | bytes accessed | tf_op | source)
XLA Modules:
  0.0 170.9 jit_solution(7163152850505933909)
XLA Ops:
  0.0 0.7 compare_select_fusion
  0.7 0.7 compare_and_fusion
  1.4 10.6 %gather_fusion = bf16[64,64,2,256]{3,2,1,0:T(2,128)(2,1)} fusion(bf16[2,64,2,256]{3,2,1,0:T(2,128)(2,1)S(1)} %copy-done, s32[1024]{0:T(1024)S(1)} %pad_clamp_fusion), kind=kCustom, calls=%fused_computation | custom fusion | bytes 8388864 | tf_op jit(solution)/shard_map/jit(_take)/gather | solution.py:102
  11.9 7.9 %broadcast_select_fusion = bf16[64,64,2,256]{3,2,1,0:T(2,128)(2,1)} fusion(bf16[64,64,2,256]{3,2,1,0:T(2,128)(2,1)} %gather_fusion, pred[64]{0:T(512)(128)(4,1)S(1)} %compare_and_fusion), kind=kLoop, calls=%fused_computation.19 | loop fusion | flops 2097152 | bytes 8388672 | tf_op jit(solution)/shard_map/jit(_take)/select_n | solution.py:102
  19.9 15.1 %all-to-all-start = ((bf16[64,64,2,256]{3,2,1,0:T(2,128)(2,1)}), bf16[64,64,2,256]{3,2,1,0:T(2,128)(2,1)}, u32[]{:S(2)}, u32[]{:S(2)}) async-start(bf16[64,64,2,256]{3,2,1,0:T(2,128)(2,1)} %broadcast_select_fusion), calls=%async_computation | async-start | bytes 8388608 | tf_op jit(solution)/shard_map/all_to_all | solution.py:103
  35.0 0.6 dynamic_slice.16
  36.9 0.2 fusion.29
  37.2 0.1 copy.90
  37.7 67.2 %psum.7 = f32[128,8]{0,1:T(8,128)S(1)} all-reduce(f32[128,8]{0,1:T(8,128)S(1)} %fusion.32), channel_id=1, replica_groups=mesh['req'=64,'tp'=8] {'tp'}, use_global_device_ids=true, to_apply=%region_8.9 | all-reduce | flops 1024 | bytes 8192 | tf_op jit(solution)/shard_map/psum | solution.py:74
  106.2 0.1 fusion.31
  106.3 0.2 select_reduce_fusion.1
  106.7 0.2 fusion.12
  106.9 0.2 fusion.11
  107.2 26.1 %all-to-all-done = bf16[64,64,2,256]{3,2,1,0:T(2,128)(2,1)} async-done(((bf16[64,64,2,256]{3,2,1,0:T(2,128)(2,1)}), bf16[64,64,2,256]{3,2,1,0:T(2,128)(2,1)}, u32[]{:S(2)}, u32[]{:S(2)}) %all-to-all-start) | async-done | bytes 4194336 | tf_op jit(solution)/shard_map/all_to_all | solution.py:103
  133.3 36.8 %while.29 = (s32[]{:T(128)}, f32[128,2,2]{0,2,1:T(2,128)S(1)}, f32[128,2,2]{0,2,1:T(2,128)S(1)}, f32[128,2,2,128]{0,3,2,1:T(8,128)S(1)}, bf16[4096,2,256]{2,1,0:...) while((s32[]{:T(128)}, f32[128,2,2]{0,2,1:T(2,128)S(1)}, ...), condition=%wide.region_7.8_spmd, body=%wide.region_4.0_spmd.sunk | while | flops 136775168 | bytes 6721715 | solution.py:66
  133.3 2.0 %constant_dynamic-slice_fusion.3 = (bf16[512,1,256]{2,1,0:T(2,128)(2,1)S(1)}, bf16[512,1,256]{2,1,0:T(2,128)(2,1)S(1)}) fusion(bf16[4096,2,256]{2,1,0:T(2,128)(2,1)} %get-tuple-element.362, s32[]{:T(128)S(6)} %select_n.101, s32[]{:T(128)S(6)} %add.173), kind=kLoop, calls=%fused_computation.17.clone.1 | loop fusion | bytes 1048584 | tf_op jit(solution)/shard_map/while/body/eval_jaxpr/slice | solution.py:56
  135.3 0.7 copy.105
  136.2 0.4 select_reduce_fusion.4
  136.5 0.2 fusion.52
  136.8 0.7 copy.106
  137.5 0.4 fusion.53
  137.9 2.1 %constant_dynamic-slice_fusion.3 = (bf16[512,1,256]{2,1,0:T(2,128)(2,1)S(1)}, bf16[512,1,256]{2,1,0:T(2,128)(2,1)S(1)}) fusion(bf16[4096,2,256]{2,1,0:T(2,128)(2,1)} %get-tuple-element.362, s32[]{:T(128)S(6)} %select_n.101, s32[]{:T(128)S(6)} %add.173), kind=kLoop, calls=%fused_computation.17.clone.1 | loop fusion | bytes 1048584 | tf_op jit(solution)/shard_map/while/body/eval_jaxpr/slice | solution.py:56
  139.9 0.7 copy.105
  140.8 0.4 select_reduce_fusion.4
  141.1 0.2 fusion.52
  141.4 0.7 copy.106
  142.1 0.4 fusion.53
  142.5 2.1 %constant_dynamic-slice_fusion.3 = (bf16[512,1,256]{2,1,0:T(2,128)(2,1)S(1)}, bf16[512,1,256]{2,1,0:T(2,128)(2,1)S(1)}) fusion(bf16[4096,2,256]{2,1,0:T(2,128)(2,1)} %get-tuple-element.362, s32[]{:T(128)S(6)} %select_n.101, s32[]{:T(128)S(6)} %add.173), kind=kLoop, calls=%fused_computation.17.clone.1 | loop fusion | bytes 1048584 | tf_op jit(solution)/shard_map/while/body/eval_jaxpr/slice | solution.py:56
  144.5 0.7 copy.105
  145.4 0.4 select_reduce_fusion.4
  145.7 0.2 fusion.52
  146.0 0.7 copy.106
  146.6 0.4 fusion.53
  147.1 2.1 %constant_dynamic-slice_fusion.3 = (bf16[512,1,256]{2,1,0:T(2,128)(2,1)S(1)}, bf16[512,1,256]{2,1,0:T(2,128)(2,1)S(1)}) fusion(bf16[4096,2,256]{2,1,0:T(2,128)(2,1)} %get-tuple-element.362, s32[]{:T(128)S(6)} %select_n.101, s32[]{:T(128)S(6)} %add.173), kind=kLoop, calls=%fused_computation.17.clone.1 | loop fusion | bytes 1048584 | tf_op jit(solution)/shard_map/while/body/eval_jaxpr/slice | solution.py:56
  149.2 0.7 copy.105
  150.0 0.4 select_reduce_fusion.4
  150.4 0.2 fusion.52
  150.6 0.7 copy.106
  151.3 0.4 fusion.53
  151.7 2.1 %constant_dynamic-slice_fusion.3 = (bf16[512,1,256]{2,1,0:T(2,128)(2,1)S(1)}, bf16[512,1,256]{2,1,0:T(2,128)(2,1)S(1)}) fusion(bf16[4096,2,256]{2,1,0:T(2,128)(2,1)} %get-tuple-element.362, s32[]{:T(128)S(6)} %select_n.101, s32[]{:T(128)S(6)} %add.173), kind=kLoop, calls=%fused_computation.17.clone.1 | loop fusion | bytes 1048584 | tf_op jit(solution)/shard_map/while/body/eval_jaxpr/slice | solution.py:56
  153.8 0.7 copy.105
  154.6 0.4 select_reduce_fusion.4
  155.0 0.2 fusion.52
  155.2 0.7 copy.106
  155.9 0.4 fusion.53
  156.3 2.1 %constant_dynamic-slice_fusion.3 = (bf16[512,1,256]{2,1,0:T(2,128)(2,1)S(1)}, bf16[512,1,256]{2,1,0:T(2,128)(2,1)S(1)}) fusion(bf16[4096,2,256]{2,1,0:T(2,128)(2,1)} %get-tuple-element.362, s32[]{:T(128)S(6)} %select_n.101, s32[]{:T(128)S(6)} %add.173), kind=kLoop, calls=%fused_computation.17.clone.1 | loop fusion | bytes 1048584 | tf_op jit(solution)/shard_map/while/body/eval_jaxpr/slice | solution.py:56
  158.4 0.7 copy.105
  159.2 0.4 select_reduce_fusion.4
  159.6 0.2 fusion.52
  159.8 0.7 copy.106
  160.5 0.4 fusion.53
  160.9 2.1 %constant_dynamic-slice_fusion.3 = (bf16[512,1,256]{2,1,0:T(2,128)(2,1)S(1)}, bf16[512,1,256]{2,1,0:T(2,128)(2,1)S(1)}) fusion(bf16[4096,2,256]{2,1,0:T(2,128)(2,1)} %get-tuple-element.362, s32[]{:T(128)S(6)} %select_n.101, s32[]{:T(128)S(6)} %add.173), kind=kLoop, calls=%fused_computation.17.clone.1 | loop fusion | bytes 1048584 | tf_op jit(solution)/shard_map/while/body/eval_jaxpr/slice | solution.py:56
  163.0 0.7 copy.105
  163.8 0.4 select_reduce_fusion.4
  164.2 0.2 fusion.52
  164.4 0.7 copy.106
  165.1 0.4 fusion.53
  165.5 2.1 %constant_dynamic-slice_fusion.3 = (bf16[512,1,256]{2,1,0:T(2,128)(2,1)S(1)}, bf16[512,1,256]{2,1,0:T(2,128)(2,1)S(1)}) fusion(bf16[4096,2,256]{2,1,0:T(2,128)(2,1)} %get-tuple-element.362, s32[]{:T(128)S(6)} %select_n.101, s32[]{:T(128)S(6)} %add.173), kind=kLoop, calls=%fused_computation.17.clone.1 | loop fusion | bytes 1048584 | tf_op jit(solution)/shard_map/while/body/eval_jaxpr/slice | solution.py:56
  167.6 0.7 copy.105
  168.4 0.4 select_reduce_fusion.4
  168.8 0.2 fusion.52
  169.0 0.7 copy.106
  169.7 0.4 fusion.53
  170.2 0.8 copy.68
  (73 shorter events, 2.1 us)
Async XLA Ops:
  0.0 1.4 copy-start
  19.8 15.2 %copy-start.7 = (s32[64]{0:T(128)S(1)}, s32[64]{0:T(128)}, u32[]{:S(2)}) copy-start(s32[64]{0:T(128)} %param.16) | copy-start | bytes 772
  19.8 16.9 %copy-start.2 = (bf16[128,512]{1,0:T(8,128)(2,1)S(1)}, bf16[128,512]{1,0:T(8,128)(2,1)}, u32[]{:S(2)}) copy-start(bf16[128,512]{1,0:T(8,128)(2,1)} %param.11) | copy-start | bytes 393220
  19.8 17.0 %copy-start.1 = (bf16[128,2,256]{2,1,0:T(2,128)(2,1)S(1)}, bf16[128,2,256]{2,1,0:T(2,128)(2,1)}, u32[]{:S(2)}) copy-start(bf16[128,2,256]{2,1,0:T(2,128)(2,1)} %param.12) | copy-start | bytes 393220
  19.9 17.7 %copy-start.3 = (bf16[128,256]{1,0:T(8,128)(2,1)S(1)}, bf16[128,256]{1,0:T(8,128)(2,1)}, u32[]{:S(2)}) copy-start(bf16[128,256]{1,0:T(8,128)(2,1)} %param.17) | copy-start | bytes 196612
  19.9 17.7 %copy-start.4 = (bf16[256,8]{0,1:T(8,128)(2,1)S(1)}, bf16[256,8]{0,1:T(8,128)(2,1)}, u32[]{:S(2)}) copy-start(bf16[256,8]{0,1:T(8,128)(2,1)} %param.18) | copy-start | bytes 12292
  19.9 84.9 %copy-start.6 = (s32[128,2]{0,1:T(2,128)S(1)}, s32[128,2]{0,1:T(2,128)}, u32[]{:S(2)}) copy-start(s32[128,2]{0,1:T(2,128)} %param.19) | copy-start | bytes 3076
  19.9 86.2 %copy-start.5 = (bf16[2,4,2,256]{3,2,1,0:T(2,128)(2,1)S(1)}, bf16[2,4,2,256]{3,2,1,0:T(2,128)(2,1)}, u32[]{:S(2)}) copy-start(bf16[2,4,2,256]{3,2,1,0:T(2,128)(2,1)} %param.14) | copy-start | bytes 24580
  19.9 113.4 %all-to-all-start = ((bf16[64,64,2,256]{3,2,1,0:T(2,128)(2,1)}), bf16[64,64,2,256]{3,2,1,0:T(2,128)(2,1)}, u32[]{:S(2)}, u32[]{:S(2)}) async-start(bf16[64,64,2,256]{3,2,1,0:T(2,128)(2,1)} %broadcast_select_fusion), calls=%async_computation | async-start | bytes 8388608 | tf_op jit(solution)/shard_map/all_to_all | solution.py:103
where the time goes:
time: 171 us
  blocking collectives  67.2 us (39%)
  local copies, waits for them, and re-layouts  40.1 us (23%)
  waiting for transfers between devices  26.1 us (15%)
  starting transfers between devices  15.1 us (9%)
  other arithmetic  12.4 us (7%)
  matrix products  6.8 us (4%)
  between operations  2.59 us (2%)
    psum x1, blocking collectives, body(): logits = lax.psum(partial_value, 'tp')  67.2 us
    all_to_all x1, waiting for transfers between devices, body(): lax.all_to_all(outgoing, 'req', split_axis=0, concat_axis=0, tiled=True)  26.1 us
    slice x9, local copies, waits for them, and re-layouts, one_block(): value_rows = kv_block[:, 1].reshape(block_rows, head_count, head_dim)  16.7 us
    all_to_all x1, starting transfers between devices, body(): lax.all_to_all(outgoing, 'req', split_axis=0, concat_axis=0, tiled=True)  15.1 us
    while x24, local copies, waits for them, and re-layouts  10.9 us
    gather x1, local copies, waits for them, and re-layouts, body(): outgoing = jnp.take(window_kv, group_ids, axis=0)  10.6 us
    select_n x2, other arithmetic, body(): outgoing = jnp.take(window_kv, group_ids, axis=0)  8.6 us
    dot_general x10, matrix products, one_tile(): jnp.einsum('qhpk,khd->qhpd', exponentials.astype(jnp.bfloat16), value_row...  3.44 us
  transfers between devices with their start and end apart: 1, of which 1 were waited for; matrix products, arithmetic and copies ran while one was open for 1% of the time, Pallas kernels for 0%

commit v1 on v0

v1 whole, which is shorter than its diff:
```python
import functools
import math

import jax
import jax.numpy as jnp
from jax import lax
from jax.experimental import pallas as pl
from jax.experimental.pallas import tpu as pltpu
from jax.sharding import PartitionSpec as P

HEAD_DIM = 128
PICKS = 2
CHUNK = 512


def attention_kernel(
    group_ref, q_ref, wk_ref, wv_ref, xk_ref, xv_ref, gate_ref, out_ref, score_ref, *, extra_sinks
):
    rows = q_ref.shape[0]
    window_rows = wk_ref.shape[0]
    extra_rows = xk_ref.shape[0]
    scale = 1.0 / math.sqrt(HEAD_DIM)
    q = q_ref[...]
    q_stack = jnp.concatenate([q[:, :HEAD_DIM], q[:, HEAD_DIM:]], axis=0)
    stacked = q_stack.shape[0]
    query_pos = lax.broadcasted_iota(jnp.int32, (stacked, CHUNK), 0) % rows
    nt = (((1,), (1,)), ((), ()))

    def scores_of(keys):
        return lax.dot_general(q_stack, keys, nt, preferred_element_type=jnp.float32) * scale

    extra = scores_of(xk_ref[...])
    extra_pos = lax.broadcasted_iota(jnp.int32, (stacked, extra_rows), 0) % rows
    extra_key = lax.broadcasted_iota(jnp.int32, (stacked, extra_rows), 1)
    extra_visible = (extra_key <= extra_pos) | (
        (extra_key >= rows) & (extra_key < rows + extra_sinks)
    )
    extra = jnp.where(extra_visible, extra, -jnp.inf)
    top = jnp.max(extra, axis=1, keepdims=True)

    chunk_count = window_rows // CHUNK
    for c in range(chunk_count):
        s = scores_of(wk_ref[pl.ds(c * CHUNK, CHUNK), :])
        if c == 0:
            key_pos = lax.broadcasted_iota(jnp.int32, (stacked, CHUNK), 1)
            s = jnp.where(key_pos > query_pos, s, -jnp.inf)
        score_ref[:, pl.ds(c * CHUNK, CHUNK)] = s
        top = jnp.maximum(top, jnp.max(s, axis=1, keepdims=True))

    e = jnp.exp(extra - top)
    total = jnp.sum(e, axis=1, keepdims=True)
    acc = jnp.dot(e.astype(jnp.bfloat16), xv_ref[...], preferred_element_type=jnp.float32)
    for c in range(chunk_count):
        e = jnp.exp(score_ref[:, pl.ds(c * CHUNK, CHUNK)] - top)
        total = total + jnp.sum(e, axis=1, keepdims=True)
        acc = acc + jnp.dot(
            e.astype(jnp.bfloat16),
            wv_ref[pl.ds(c * CHUNK, CHUNK), :],
            preferred_element_type=jnp.float32,
        )
    attended = acc / total
    gate = gate_ref[...]
    out_ref[:, :HEAD_DIM] = (attended[:rows] * gate[:, 0:1]).astype(out_ref.dtype)
    out_ref[:, HEAD_DIM:] = (attended[rows:] * gate[:, 1:2]).astype(out_ref.dtype)


def attend(group, queries, window, extra, gate_live, head_count, extra_sinks):
    rows = queries.shape[0]
    window_rows = window.shape[0]
    extra_rows = extra.shape[0]
    kernel = functools.partial(attention_kernel, extra_sinks=extra_sinks)
    grid_spec = pltpu.PrefetchScalarGridSpec(
        num_scalar_prefetch=1,
        grid=(head_count,),
        in_specs=[
            pl.BlockSpec((rows, PICKS * HEAD_DIM), lambda h, g: (0, h)),
            pl.BlockSpec((window_rows, HEAD_DIM), lambda h, g: (0, g[0] * 2 * head_count + h)),
            pl.BlockSpec(
                (window_rows, HEAD_DIM), lambda h, g: (0, g[0] * 2 * head_count + head_count + h)
            ),
            pl.BlockSpec((extra_rows, HEAD_DIM), lambda h, g: (0, h)),
            pl.BlockSpec((extra_rows, HEAD_DIM), lambda h, g: (0, head_count + h)),
            pl.BlockSpec((rows, PICKS), lambda h, g: (0, 0)),
        ],
        out_specs=pl.BlockSpec((rows, PICKS * HEAD_DIM), lambda h, g: (0, h)),
        scratch_shapes=[pltpu.VMEM((PICKS * rows, window_rows), jnp.float32)],
    )
    return pl.pallas_call(
        kernel,
        grid_spec=grid_spec,
        out_shape=jax.ShapeDtypeStruct((rows, head_count * PICKS * HEAD_DIM), jnp.bfloat16),
    )(group, queries, window, window, extra, extra, gate_live)


def body(queries, suffix_kv, window_kv, sink_kv, lengths, group_ids, hidden_in, router, picks):
    row_count = queries.shape[0]
    head_count = suffix_kv.shape[2] // HEAD_DIM
    partial_value = jnp.dot(hidden_in, router, preferred_element_type=jnp.float32)
    logits = lax.psum(partial_value, "tp")
    experts = jnp.arange(logits.shape[1], dtype=jnp.int32)
    chosen = jnp.sum(
        jnp.where(picks[:, :, None] == experts[None, None, :], logits[:, None, :], 0.0), axis=2
    )
    gate_values = jax.nn.sigmoid(chosen - chosen[:, ::-1])
    my_group = group_ids[lax.axis_index("req")]
    length = lengths[0]
    is_live = jnp.arange(row_count, dtype=jnp.int32) < length
    gate_live = jnp.where(is_live[:, None], gate_values, 0.0)

    groups = window_kv.shape[0]
    local = jnp.transpose(window_kv, (1, 0, 2, 3))
    local = local.reshape(local.shape[0], groups * 2 * head_count * HEAD_DIM)
    window = lax.all_gather(local, "req", axis=0, tiled=True)

    sink_rows = lax.dynamic_index_in_dim(sink_kv, my_group, 0, keepdims=False)
    sink_count = sink_rows.shape[0]
    extra_rows = 2 * row_count
    width = 2 * head_count * HEAD_DIM
    extra = jnp.concatenate(
        [
            suffix_kv.reshape(row_count, width),
            sink_rows.reshape(sink_count, width),
            jnp.zeros((extra_rows - row_count - sink_count, width), suffix_kv.dtype),
        ],
        axis=0,
    )
    group = my_group.reshape(1).astype(jnp.int32)
    return attend(group, queries, window, extra, gate_live, head_count, sink_count)


def solution(mesh):
    return jax.shard_map(
        body,
        mesh=mesh,
        in_specs=(
            P("req", "tp"),
            P("req", None, "tp"),
            P(None, "req", None, "tp"),
            P(None, None, None, "tp"),
            P("req"),
            P(),
            P("req", "tp"),
            P("tp", None),
            P("req", None),
        ),
        out_specs=P("req", "tp"),
        check_vma=False,
    )
```

time: 171 us -> 344 us (2.01)
  the two profiles are of different devices: /device:TPU:40 before, /device:TPU:16 now
where the time goes in v1:
time: 344 us
  waiting for transfers between devices  296 us (86%)
  between operations  16 us (5%)
  blocking collectives  15.6 us (5%)
  Pallas kernels  7.79 us (2%)
  local copies, waits for them, and re-layouts  4.92 us (1%)
    all_gather x1, waiting for transfers between devices, body(): window = lax.all_gather(local, 'req', axis=0, tiled=True)  296 us
    psum x1, blocking collectives, body(): logits = lax.psum(partial_value, 'tp')  15.6 us
    pallas_call x1, Pallas kernels, attend(): pl.pallas_call(kernel, grid_spec=grid_spec, out_shape=jax.ShapeDtypeStruc...  7.79 us
  transfers between devices with their start and end apart: 1, of which 1 were waited for; matrix products, arithmetic and copies ran while one was open for 2% of the time, Pallas kernels for 0%

profile of v1, /device:TPU:16, one launch (start us, length us, event | category | flops | bytes accessed | tf_op | source)
XLA Modules:
  0.0 343.7 jit_solution(15258539168783821743)
XLA Ops:
  6.5 0.0 copy-start
  6.5 0.0 all-gather.2.cloned.1.call-start
  6.5 1.0 copy.13
  7.6 0.7 reshape.16
  8.3 0.0 all-gather.2.cloned.1.call-update
  8.3 1.3 dynamic_slice.7.group_ref
  11.5 0.7 dynamic-slice_bitcast_fusion
  12.2 0.9 copy.16
  13.1 0.0 copy-done
  13.1 0.8 fusion
  13.9 15.6 %psum.7 = f32[128,8]{0,1:T(8,128)S(1)} all-reduce(f32[128,8]{0,1:T(8,128)S(1)} %fusion), channel_id=1, replica_groups=mesh['req'=64,'tp'=8] {'tp'}, use_global_device_ids=true, to_apply=%region_0.0 | all-reduce | flops 1024 | bytes 8192 | tf_op jit(solution)/shard_map/psum | solution.py:99
  29.5 0.7 select_reduce_fusion
  30.2 0.1 copy.15
  30.3 0.1 rev.3
  31.1 0.1 pad.2.clone
  31.2 0.7 divide_select_fusion.gate_ref
  31.9 0.8 maximum_maximum_fusion.xk_ref.xv_ref
  32.7 296.4 %all-gather.2.cloned.1.call-done.wk_ref.wv_ref = bf16[4096,1024]{1,0:T(8,128)(2,1)} async-done(((bf16[64,1024]{1,0:T(8,128)(2,1)}), bf16[4096,1024]{1,0:T(8,128)(2,1)}) %all-gather.2.cloned.1.call-update) | async-done | bytes 8388624 | tf_op jit(solution)/shard_map/all_gather | solution.py:113
  329.0 7.8 %shard_map.91 = bf16[128,512]{1,0:T(8,128)(2,1)} custom-call(s32[1]{0:T(128)} %dynamic_slice.7.group_ref, bf16[128,512]{1,0:T(8,128)(2,1)} %q_ref.1, bf16[4096,1024]{1,0:T(8,128)(2,1)} %all-gather.2.cloned.1.call-done.wk_ref.wv_ref, bf16[4096,1024]{1,0:T(8,128)(2,1)} %all-gather.2.cloned.1.call-done.wk_ref.wv_ref, ...), custom_call_target="tpu_custom_call" | custom-call | tf_op jit(solution)/shard_map/pallas_call | solution.py:88
  (3 shorter events, 0.0 us)
Async XLA Ops:
  6.5 6.6 %copy-start = (bf16[128,256]{1,0:T(8,128)(2,1)S(1)}, bf16[128,256]{1,0:T(8,128)(2,1)}, u32[]{:S(2)}) copy-start(bf16[128,256]{1,0:T(8,128)(2,1)} %param.15) | copy-start | bytes 196612
  6.5 322.5 %all-gather.2.cloned.1.call-start = ((), (), s32[]{:S(2)}) async-start(), calls=%async_computation | async-start | bytes 8519680 | tf_op jit(solution)/shard_map/all_gather | solution.py:113
Sparse Core Ops, SparseCore 0:
  9.4 319.5 all-gather.1

commit v2 on v1

--- a/solution.py
+++ b/solution.py
@@ -74,10 +74,8 @@
         grid=(head_count,),
         in_specs=[
             pl.BlockSpec((rows, PICKS * HEAD_DIM), lambda h, g: (0, h)),
-            pl.BlockSpec((window_rows, HEAD_DIM), lambda h, g: (0, g[0] * 2 * head_count + h)),
-            pl.BlockSpec(
-                (window_rows, HEAD_DIM), lambda h, g: (0, g[0] * 2 * head_count + head_count + h)
-            ),
+            pl.BlockSpec((window_rows, HEAD_DIM), lambda h, g: (0, h)),
+            pl.BlockSpec((window_rows, HEAD_DIM), lambda h, g: (0, head_count + h)),
             pl.BlockSpec((extra_rows, HEAD_DIM), lambda h, g: (0, h)),
             pl.BlockSpec((extra_rows, HEAD_DIM), lambda h, g: (0, head_count + h)),
             pl.BlockSpec((rows, PICKS), lambda h, g: (0, 0)),
@@ -107,15 +105,18 @@
     is_live = jnp.arange(row_count, dtype=jnp.int32) < length
     gate_live = jnp.where(is_live[:, None], gate_values, 0.0)
 
-    groups = window_kv.shape[0]
-    local = jnp.transpose(window_kv, (1, 0, 2, 3))
-    local = local.reshape(local.shape[0], groups * 2 * head_count * HEAD_DIM)
-    window = lax.all_gather(local, "req", axis=0, tiled=True)
+    req_count = group_ids.shape[0]
+    width = 2 * head_count * HEAD_DIM
+    local = window_kv.reshape(window_kv.shape[0], window_kv.shape[1], width)
+    outgoing = jnp.where(
+        (group_ids == 0)[:, None, None], local[0][None], local[1][None]
+    )
+    received = lax.all_to_all(outgoing, "req", split_axis=0, concat_axis=0, tiled=True)
+    window = received.reshape(req_count * local.shape[1], width)
 
     sink_rows = lax.dynamic_index_in_dim(sink_kv, my_group, 0, keepdims=False)
     sink_count = sink_rows.shape[0]
     extra_rows = 2 * row_count
-    width = 2 * head_count * HEAD_DIM
     extra = jnp.concatenate(
         [
             suffix_kv.reshape(row_count, width),

time: 344 us -> 125 us (0.36)
  the two profiles are of different devices: /device:TPU:16 before, /device:TPU:56 now
where the time goes in v2:
time: 125 us
  blocking collectives  65.3 us (52%)
  waiting for transfers between devices  27.7 us (22%)
  starting transfers between devices  15.1 us (12%)
  Pallas kernels  7.76 us (6%)
  other arithmetic  4.56 us (4%)
  between operations  2.69 us (2%)
  local copies, waits for them, and re-layouts  1.92 us (2%)
    psum x1, blocking collectives, body(): logits = lax.psum(partial_value, 'tp')  65.3 us
    all_to_all x1, waiting for transfers between devices, body(): lax.all_to_all(outgoing, 'req', split_axis=0, concat_axis=0, tiled=True)  27.7 us
    all_to_all x1, starting transfers between devices, body(): lax.all_to_all(outgoing, 'req', split_axis=0, concat_axis=0, tiled=True)  15.1 us
    pallas_call x1, Pallas kernels, attend(): pl.pallas_call(kernel, grid_spec=grid_spec, out_shape=jax.ShapeDtypeStruc...  7.76 us
  transfers between devices with their start and end apart: 1, of which 1 were waited for; matrix products, arithmetic and copies ran while one was open for 2% of the time, Pallas kernels for 0%

profile of v2, /device:TPU:56, one launch (start us, length us, event | category | flops | bytes accessed | tf_op | source)
XLA Modules:
  0.0 125.2 jit_solution(12870282611399773667)
XLA Ops:
  0.0 0.0 copy-start
  0.0 0.7 broadcast_compare_fusion
  0.7 1.0 fusion
  1.7 2.3 %broadcast_select_fusion = bf16[64,64,512]{2,1,0:T(8,128)(2,1)} fusion(pred[64]{0:T(512)(128)(4,1)S(1)} %broadcast_compare_fusion, bf16[64,512]{1,0:T(8,128)(2,1)S(1)} %bitcast.19, bf16[64,512]{1,0:T(8,128)(2,1)S(1)} %bitcast.20), kind=kLoop, calls=%fused_computation | loop fusion | flops 2097152 | bytes 4325440 | tf_op jit(solution)/shard_map/jit(_where)/select_n | solution.py:111
  4.0 0.0 copy-start.5
  4.0 0.0 copy-start.3
  4.0 0.0 copy-start.1
  4.0 0.0 copy-start.2
  4.0 0.0 copy-start.4
  4.0 15.1 %all-to-all-start = ((bf16[64,64,512]{2,1,0:T(8,128)(2,1)}), bf16[64,64,512]{2,1,0:T(8,128)(2,1)}, u32[]{:S(2)}, u32[]{:S(2)}) async-start(bf16[64,64,512]{2,1,0:T(8,128)(2,1)} %broadcast_select_fusion), calls=%async_computation | async-start | bytes 8388608 | tf_op jit(solution)/shard_map/all_to_all | solution.py:114
  19.2 0.0 copy-done.5
  19.2 0.6 dynamic_slice.7.group_ref
  21.7 0.0 copy-done.3
  21.7 0.0 copy-done.1
  21.8 0.0 copy-done
  21.8 0.0 copy-done.2
  21.8 0.1 fusion.1
  21.9 65.3 %psum.7 = f32[128,8]{0,1:T(8,128)S(1)} all-reduce(f32[128,8]{0,1:T(8,128)S(1)} %fusion.1), channel_id=1, replica_groups=mesh['req'=64,'tp'=8] {'tp'}, use_global_device_ids=true, to_apply=%region_0.0 | all-reduce | flops 1024 | bytes 8192 | tf_op jit(solution)/shard_map/psum | solution.py:97
  87.3 0.0 copy-done.4
  87.3 0.1 copy.13
  87.4 0.1 rev.3
  88.1 0.1 pad.2.clone
  88.2 0.7 divide_select_fusion.gate_ref
  88.9 0.8 maximum_maximum_fusion.xk_ref.xv_ref
  89.8 27.7 %all-to-all-done = bf16[64,64,512]{2,1,0:T(8,128)(2,1)} async-done(((bf16[64,64,512]{2,1,0:T(8,128)(2,1)}), bf16[64,64,512]{2,1,0:T(8,128)(2,1)}, u32[]{:S(2)}, u32[]{:S(2)}) %all-to-all-start) | async-done | bytes 4194336 | tf_op jit(solution)/shard_map/all_to_all | solution.py:114
  117.4 7.8 %shard_map.91 = bf16[128,512]{1,0:T(8,128)(2,1)} custom-call(s32[1]{0:T(128)} %dynamic_slice.7.group_ref, bf16[128,512]{1,0:T(8,128)(2,1)} %q_ref.1, bf16[4096,512]{1,0:T(8,128)(2,1)} %bitcast.wk_ref.wv_ref, bf16[4096,512]{1,0:T(8,128)(2,1)} %bitcast.wk_ref.wv_ref, bf16[256,512]{1,0:T(8,128)(2,1)} %maximum_maximum_fusion.xk_ref.xv_ref, ...), custom_call_target="tpu_custom_call" | custom-call | tf_op jit(solution)/shard_map/pallas_call | solution.py:86
  (8 shorter events, 0.1 us)
Async XLA Ops:
  0.0 21.8 %copy-start = (bf16[128,256]{1,0:T(8,128)(2,1)S(1)}, bf16[128,256]{1,0:T(8,128)(2,1)}, u32[]{:S(2)}) copy-start(bf16[128,256]{1,0:T(8,128)(2,1)} %param.15) | copy-start | bytes 196612
  4.0 15.2 %copy-start.5 = (s32[64]{0:T(128)S(1)}, s32[64]{0:T(128)}, u32[]{:S(2)}) copy-start(s32[64]{0:T(128)} %param.14) | copy-start | bytes 772
  4.0 17.7 %copy-start.3 = (bf16[2,4,2,256]{3,2,1,0:T(2,128)(2,1)S(1)}, bf16[2,4,2,256]{3,2,1,0:T(2,128)(2,1)}, u32[]{:S(2)}) copy-start(bf16[2,4,2,256]{3,2,1,0:T(2,128)(2,1)} %param.12) | copy-start | bytes 24580
  4.0 17.7 %copy-start.1 = (bf16[128,2,256]{2,1,0:T(2,128)(2,1)S(1)}, bf16[128,2,256]{2,1,0:T(2,128)(2,1)}, u32[]{:S(2)}) copy-start(bf16[128,2,256]{2,1,0:T(2,128)(2,1)} %param.10) | copy-start | bytes 393220
  4.0 17.8 %copy-start.2 = (bf16[256,8]{0,1:T(8,128)(2,1)S(1)}, bf16[256,8]{0,1:T(8,128)(2,1)}, u32[]{:S(2)}) copy-start(bf16[256,8]{0,1:T(8,128)(2,1)} %param.16) | copy-start | bytes 12292
  4.0 83.2 %copy-start.4 = (s32[128,2]{0,1:T(2,128)S(1)}, s32[128,2]{0,1:T(2,128)}, u32[]{:S(2)}) copy-start(s32[128,2]{0,1:T(2,128)} %param.17) | copy-start | bytes 3076
  4.0 113.4 %all-to-all-start = ((bf16[64,64,512]{2,1,0:T(8,128)(2,1)}), bf16[64,64,512]{2,1,0:T(8,128)(2,1)}, u32[]{:S(2)}, u32[]{:S(2)}) async-start(bf16[64,64,512]{2,1,0:T(8,128)(2,1)} %broadcast_select_fusion), calls=%async_computation | async-start | bytes 8388608 | tf_op jit(solution)/shard_map/all_to_all | solution.py:114

commit v3 on v2

--- a/solution.py
+++ b/solution.py
@@ -14,7 +14,19 @@
 
 
 def attention_kernel(
-    group_ref, q_ref, wk_ref, wv_ref, xk_ref, xv_ref, gate_ref, out_ref, score_ref, *, extra_sinks
+    group_ref,
+    q_ref,
+    wk_ref,
+    wv_ref,
+    xk_ref,
+    xv_ref,
+    gate_ref,
+    out_ref,
+    score_ref,
+    *,
+    extra_sinks,
+    per_device,
+    plane_count,
 ):
     rows = q_ref.shape[0]
     window_rows = wk_ref.shape[0]
@@ -41,8 +53,11 @@
     chunk_count = window_rows // CHUNK
     for c in range(chunk_count):
         s = scores_of(wk_ref[pl.ds(c * CHUNK, CHUNK), :])
-        if c == 0:
-            key_pos = lax.broadcasted_iota(jnp.int32, (stacked, CHUNK), 1)
+        if c * per_device < rows:
+            key_row = lax.broadcasted_iota(jnp.int32, (stacked, CHUNK), 1)
+            key_pos = (
+                (key_row // per_device) * plane_count + c
+            ) * per_device + key_row % per_device
             s = jnp.where(key_pos > query_pos, s, -jnp.inf)
         score_ref[:, pl.ds(c * CHUNK, CHUNK)] = s
         top = jnp.maximum(top, jnp.max(s, axis=1, keepdims=True))
@@ -64,11 +79,16 @@
     out_ref[:, HEAD_DIM:] = (attended[rows:] * gate[:, 1:2]).astype(out_ref.dtype)
 
 
-def attend(group, queries, window, extra, gate_live, head_count, extra_sinks):
+def attend(group, queries, window, extra, gate_live, head_count, extra_sinks, per_device, plane_count):
     rows = queries.shape[0]
     window_rows = window.shape[0]
     extra_rows = extra.shape[0]
-    kernel = functools.partial(attention_kernel, extra_sinks=extra_sinks)
+    kernel = functools.partial(
+        attention_kernel,
+        extra_sinks=extra_sinks,
+        per_device=per_device,
+        plane_count=plane_count,
+    )
     grid_spec = pltpu.PrefetchScalarGridSpec(
         num_scalar_prefetch=1,
         grid=(head_count,),
@@ -100,19 +120,30 @@
         jnp.where(picks[:, :, None] == experts[None, None, :], logits[:, None, :], 0.0), axis=2
     )
     gate_values = jax.nn.sigmoid(chosen - chosen[:, ::-1])
-    my_group = group_ids[lax.axis_index("req")]
+    z_count = lax.axis_size("z")
+    plane_count = lax.axis_size("ylo") * lax.axis_size("x")
+    z_me = lax.axis_index("z")
+    plane_me = lax.axis_index("ylo") * lax.axis_size("x") + lax.axis_index("x")
+    my_group = group_ids[z_me * plane_count + plane_me]
     length = lengths[0]
     is_live = jnp.arange(row_count, dtype=jnp.int32) < length
     gate_live = jnp.where(is_live[:, None], gate_values, 0.0)
 
-    req_count = group_ids.shape[0]
     width = 2 * head_count * HEAD_DIM
-    local = window_kv.reshape(window_kv.shape[0], window_kv.shape[1], width)
+    per_device = window_kv.shape[1]
+    local = window_kv.reshape(window_kv.shape[0], per_device, width)
+    arrived = [local]
+    for shift in range(1, z_count):
+        pairs = [(j, (j + shift) % z_count) for j in range(z_count)]
+        arrived.append(lax.ppermute(local, "z", pairs))
+    by_shift = jnp.stack(arrived)
+    by_z = jnp.take(by_shift, (z_me - jnp.arange(z_count)) % z_count, axis=0)
+    peer_groups = lax.dynamic_slice_in_dim(group_ids, z_me * plane_count, plane_count)
     outgoing = jnp.where(
-        (group_ids == 0)[:, None, None], local[0][None], local[1][None]
+        (peer_groups == 0)[:, None, None, None], by_z[None, :, 0], by_z[None, :, 1]
     )
-    received = lax.all_to_all(outgoing, "req", split_axis=0, concat_axis=0, tiled=True)
-    window = received.reshape(req_count * local.shape[1], width)
+    received = lax.all_to_all(outgoing, ("ylo", "x"), split_axis=0, concat_axis=0, tiled=True)
+    window = received.reshape(plane_count * z_count * per_device, width)
 
     sink_rows = lax.dynamic_index_in_dim(sink_kv, my_group, 0, keepdims=False)
     sink_count = sink_rows.shape[0]
@@ -126,24 +157,31 @@
         axis=0,
     )
     group = my_group.reshape(1).astype(jnp.int32)
-    return attend(group, queries, window, extra, gate_live, head_count, sink_count)
+    return attend(
+        group, queries, window, extra, gate_live, head_count, sink_count, per_device, plane_count
+    )
 
 
 def solution(mesh):
+    plane_ylo, plane_x = 2, 4
+    z_count = mesh.shape["req"] // (plane_ylo * plane_x)
+    devices = mesh.devices.reshape(z_count, plane_ylo, plane_x, mesh.shape["tp"])
+    inner = jax.sharding.Mesh(devices, ("z", "ylo", "x", "tp"))
+    req = ("z", "ylo", "x")
     return jax.shard_map(
         body,
-        mesh=mesh,
+        mesh=inner,
         in_specs=(
-            P("req", "tp"),
-            P("req", None, "tp"),
-            P(None, "req", None, "tp"),
+            P(req, "tp"),
+            P(req, None, "tp"),
+            P(None, req, None, "tp"),
             P(None, None, None, "tp"),
-            P("req"),
+            P(req),
             P(),
-            P("req", "tp"),
+            P(req, "tp"),
             P("tp", None),
-            P("req", None),
+            P(req, None),
         ),
-        out_specs=P("req", "tp"),
+        out_specs=P(req, "tp"),
         check_vma=False,
     )

time: 125 us -> 124 us (level)
  the two profiles are of different devices: /device:TPU:56 before, /device:TPU:78 now
where the time goes in v3:
time: 124 us; the launch traced here: 123 us
  blocking collectives  55.3 us (45%)
  starting transfers between devices  38.5 us (31%)
  waiting for transfers between devices  10.6 us (9%)
  Pallas kernels  7.64 us (6%)
  other arithmetic  5.04 us (4%)
  local copies, waits for them, and re-layouts  3.67 us (3%)
  between operations  2.58 us (2%)
    psum x1, blocking collectives, body(): logits = lax.psum(partial_value, 'tp')  55.3 us
    ppermute x7, starting transfers between devices, body(): arrived.append(lax.ppermute(local, 'z', pairs))  32.7 us
    ppermute x7, waiting for transfers between devices, body(): arrived.append(lax.ppermute(local, 'z', pairs))  10.6 us
    pallas_call x1, Pallas kernels, attend(): pl.pallas_call(kernel, grid_spec=grid_spec, out_shape=jax.ShapeDtypeStruc...  7.64 us
    all_to_all x1, starting transfers between devices, body(): lax.all_to_all(outgoing, ('ylo', 'x'), split_axis=0, concat_axis=0, tiled...  5.82 us
    select_n x1, other arithmetic, body(): jnp.where((peer_groups == 0)[:, None, None, None], by_z[None, :, 0], by_z...  2.52 us
  transfers between devices with their start and end apart: 8, of which 3 were waited for; matrix products, arithmetic and copies ran while one was open for 4% of the time, Pallas kernels for 0%

profile of v3, /device:TPU:78, one launch (start us, length us, event | category | flops | bytes accessed | tf_op | source)
XLA Modules:
  0.0 123.5 jit_solution(7404426567619989045)
XLA Ops:
  0.0 0.0 copy-start
  0.0 1.0 reshape.76
  1.0 4.3 %collective-permute-start = (bf16[2,64,512]{2,1,0:T(8,128)(2,1)S(1)}, bf16[2,64,512]{2,1,0:T(8,128)(2,1)S(1)}, u32[]{:S(2)}, u32[]{:S(2)}) collective-permute-start(bf16[2,64,512]{2,1,0:T(8,128)(2,1)S(1)} %reshape.76), channel_id=1, source_target_pairs={{0,64},{64,128},{128,192},{192,256},{256,320},{320,384},{384,448},... | collective-permute-start | bytes 393224 | tf_op jit(solution)/shard_map/ppermute | solution.py:138
  5.3 7.3 %collective-permute-start.1 = (bf16[2,64,512]{2,1,0:T(8,128)(2,1)S(1)}, bf16[2,64,512]{2,1,0:T(8,128)(2,1)S(1)}, u32[]{:S(2)}, u32[]{:S(2)}) collective-permute-start(bf16[2,64,512]{2,1,0:T(8,128)(2,1)S(1)} %reshape.76), channel_id=1, source_target_pairs={{0,128},{64,192},{128,256},{192,320},{256,384},{320,448},{384,0},{... | collective-permute-start | bytes 393224 | tf_op jit(solution)/shard_map/ppermute | solution.py:138
  12.6 5.2 %collective-permute-start.2 = (bf16[2,64,512]{2,1,0:T(8,128)(2,1)S(1)}, bf16[2,64,512]{2,1,0:T(8,128)(2,1)S(1)}, u32[]{:S(2)}, u32[]{:S(2)}) collective-permute-start(bf16[2,64,512]{2,1,0:T(8,128)(2,1)S(1)} %reshape.76), channel_id=1, source_target_pairs={{0,192},{64,256},{128,320},{192,384},{256,448},{320,0},{384,64},{4... | collective-permute-start | bytes 393224 | tf_op jit(solution)/shard_map/ppermute | solution.py:138
  17.8 1.9 %collective-permute-start.3 = (bf16[2,64,512]{2,1,0:T(8,128)(2,1)S(1)}, bf16[2,64,512]{2,1,0:T(8,128)(2,1)S(1)}, u32[]{:S(2)}, u32[]{:S(2)}) collective-permute-start(bf16[2,64,512]{2,1,0:T(8,128)(2,1)S(1)} %reshape.76), channel_id=1, source_target_pairs={{0,256},{64,320},{128,384},{192,448},{256,0},{320,64},{384,128},{4... | collective-permute-start | bytes 393224 | tf_op jit(solution)/shard_map/ppermute | solution.py:138
  19.8 6.4 %collective-permute-start.4 = (bf16[2,64,512]{2,1,0:T(8,128)(2,1)S(1)}, bf16[2,64,512]{2,1,0:T(8,128)(2,1)S(1)}, u32[]{:S(2)}, u32[]{:S(2)}) collective-permute-start(bf16[2,64,512]{2,1,0:T(8,128)(2,1)S(1)} %reshape.76), channel_id=1, source_target_pairs={{0,320},{64,384},{128,448},{192,0},{256,64},{320,128},{384,192},{4... | collective-permute-start | bytes 393224 | tf_op jit(solution)/shard_map/ppermute | solution.py:138
  26.2 0.7 dynamic-slice_compare_fusion
  26.9 1.0 stack_reshape.3
  28.0 0.0 collective-permute-done
  28.0 3.9 %collective-permute-start.5 = (bf16[2,64,512]{2,1,0:T(8,128)(2,1)S(1)}, bf16[2,64,512]{2,1,0:T(8,128)(2,1)S(1)}, u32[]{:S(2)}, u32[]{:S(2)}) collective-permute-start(bf16[2,64,512]{2,1,0:T(8,128)(2,1)S(1)} %reshape.76), channel_id=1, source_target_pairs={{0,384},{64,448},{128,0},{192,64},{256,128},{320,192},{384,256},{4... | collective-permute-start | bytes 393224 | tf_op jit(solution)/shard_map/ppermute | solution.py:138
  31.9 0.0 collective-permute-done.1
  31.9 3.7 %collective-permute-start.6 = (bf16[2,64,512]{2,1,0:T(8,128)(2,1)S(1)}, bf16[2,64,512]{2,1,0:T(8,128)(2,1)S(1)}, u32[]{:S(2)}, u32[]{:S(2)}) collective-permute-start(bf16[2,64,512]{2,1,0:T(8,128)(2,1)S(1)} %reshape.76), channel_id=1, source_target_pairs={{0,448},{64,0},{128,64},{192,128},{256,192},{320,256},{384,320},{4... | collective-permute-start | bytes 393224 | tf_op jit(solution)/shard_map/ppermute | solution.py:138
  35.6 0.0 collective-permute-done.2
  35.6 0.0 collective-permute-done.3
  35.7 3.1 %collective-permute-done.4 = bf16[2,64,512]{2,1,0:T(8,128)(2,1)S(1)} collective-permute-done((bf16[2,64,512]{2,1,0:T(8,128)(2,1)S(1)}, bf16[2,64,512]{2,1,0:T(8,128)(2,1)S(1)}, u32[]{:S(2)}, u32[]{:S(2)}) %collective-permute-start.4) | collective-permute-done | bytes 131104 | tf_op jit(solution)/shard_map/ppermute | solution.py:138
  38.8 5.1 %collective-permute-done.5 = bf16[2,64,512]{2,1,0:T(8,128)(2,1)S(1)} collective-permute-done((bf16[2,64,512]{2,1,0:T(8,128)(2,1)S(1)}, bf16[2,64,512]{2,1,0:T(8,128)(2,1)S(1)}, u32[]{:S(2)}, u32[]{:S(2)}) %collective-permute-start.5) | collective-permute-done | bytes 131104 | tf_op jit(solution)/shard_map/ppermute | solution.py:138
  43.9 2.4 %collective-permute-done.6 = bf16[2,64,512]{2,1,0:T(8,128)(2,1)S(1)} collective-permute-done((bf16[2,64,512]{2,1,0:T(8,128)(2,1)S(1)}, bf16[2,64,512]{2,1,0:T(8,128)(2,1)S(1)}, u32[]{:S(2)}, u32[]{:S(2)}) %collective-permute-start.6) | collective-permute-done | bytes 131104 | tf_op jit(solution)/shard_map/ppermute | solution.py:138
  46.3 0.6 gather_fusion
  47.0 0.2 broadcast_select_fusion.1
  47.1 0.1 slice_bitcast_fusion.1
  47.2 2.5 %broadcast_select_fusion = bf16[8,8,64,512]{3,2,1,0:T(8,128)(2,1)} fusion(pred[8]{0:T(512)(128)(4,1)S(1)} %dynamic-slice_compare_fusion, bf16[8,64,512]{2,1,0:T(8,128)(2,1)S(1)} %get-tuple-element.6, bf16[8,64,512]{2,1,0:T(8,128)(2,1)S(1)} %get-tuple-element.5), kind=kLoop, calls=%fused_computation.1 | loop fusion | flops 2097152 | bytes 5242888 | tf_op jit(solution)/shard_map/jit(_where)/select_n | solution.py:142
  49.7 0.0 copy-start.5
  49.7 0.0 copy-start.3
  49.7 0.0 copy-start.1
  49.7 0.0 copy-start.2
  49.7 0.0 copy-start.4
  49.8 5.8 %all-to-all-start = ((bf16[8,8,64,512]{3,2,1,0:T(8,128)(2,1)}), bf16[8,8,64,512]{3,2,1,0:T(8,128)(2,1)}, u32[]{:S(2)}, u32[]{:S(2)}) async-start(bf16[8,8,64,512]{3,2,1,0:T(8,128)(2,1)} %broadcast_select_fusion), calls=%async_computation | async-start | bytes 8388608 | tf_op jit(solution)/shard_map/all_to_all | solution.py:145
  55.6 0.0 copy-done.5
  55.6 0.6 dynamic_slice.10.group_ref
  57.8 0.0 copy-done.3
  57.8 0.0 copy-done.1
  57.9 0.0 copy-done
  57.9 0.0 copy-done.2
  57.9 0.1 fusion.3
  58.0 55.3 %psum.7 = f32[128,8]{0,1:T(8,128)S(1)} all-reduce(f32[128,8]{0,1:T(8,128)S(1)} %fusion.3), channel_id=1, replica_groups=mesh['z'=8,'ylo'=2,'x'=4,'tp'=8] {'tp'}, use_global_device_ids=true, to_apply=%region_0.0 | all-reduce | flops 1024 | bytes 8192 | tf_op jit(solution)/shard_map/psum | solution.py:117
  113.3 0.0 copy-done.4
  113.3 0.1 copy.13
  113.4 0.1 rev.3
  114.2 0.1 pad.2.clone
  114.3 0.7 divide_select_fusion.gate_ref
  115.0 0.9 maximum_maximum_fusion.xk_ref.xv_ref
  115.8 0.0 all-to-all-done
  115.8 7.6 %shard_map.91 = bf16[128,512]{1,0:T(8,128)(2,1)} custom-call(s32[1]{0:T(128)} %dynamic_slice.10.group_ref, bf16[128,512]{1,0:T(8,128)(2,1)} %q_ref.1, bf16[4096,512]{1,0:T(8,128)(2,1)} %bitcast.10.wk_ref.wv_ref, bf16[4096,512]{1,0:T(8,128)(2,1)} %bitcast.10.wk_ref.wv_ref, bf16[256,512]{1,0:T(8,128)(2,1)} %maximum_maximum_fusion.xk_ref.xv_ref, ...), custom_call_target="tpu_custom_call" | custom-call | tf_op jit(solution)/shard_map/pallas_call | solution.py:106
  (17 shorter events, 0.2 us)
Async XLA Ops:
  0.0 57.9 %copy-start = (bf16[128,256]{1,0:T(8,128)(2,1)S(1)}, bf16[128,256]{1,0:T(8,128)(2,1)}, u32[]{:S(2)}) copy-start(bf16[128,256]{1,0:T(8,128)(2,1)} %param.15) | copy-start | bytes 196612
  1.0 26.9 %collective-permute-start = (bf16[2,64,512]{2,1,0:T(8,128)(2,1)S(1)}, bf16[2,64,512]{2,1,0:T(8,128)(2,1)S(1)}, u32[]{:S(2)}, u32[]{:S(2)}) collective-permute-start(bf16[2,64,512]{2,1,0:T(8,128)(2,1)S(1)} %reshape.76), channel_id=1, source_target_pairs={{0,64},{64,128},{128,192},{192,256},{256,320},{320,384},{384,448},... | collective-permute-start | bytes 393224 | tf_op jit(solution)/shard_map/ppermute | solution.py:138
  5.3 26.6 %collective-permute-start.1 = (bf16[2,64,512]{2,1,0:T(8,128)(2,1)S(1)}, bf16[2,64,512]{2,1,0:T(8,128)(2,1)S(1)}, u32[]{:S(2)}, u32[]{:S(2)}) collective-permute-start(bf16[2,64,512]{2,1,0:T(8,128)(2,1)S(1)} %reshape.76), channel_id=1, source_target_pairs={{0,128},{64,192},{128,256},{192,320},{256,384},{320,448},{384,0},{... | collective-permute-start | bytes 393224 | tf_op jit(solution)/shard_map/ppermute | solution.py:138
  12.6 23.0 %collective-permute-start.2 = (bf16[2,64,512]{2,1,0:T(8,128)(2,1)S(1)}, bf16[2,64,512]{2,1,0:T(8,128)(2,1)S(1)}, u32[]{:S(2)}, u32[]{:S(2)}) collective-permute-start(bf16[2,64,512]{2,1,0:T(8,128)(2,1)S(1)} %reshape.76), channel_id=1, source_target_pairs={{0,192},{64,256},{128,320},{192,384},{256,448},{320,0},{384,64},{4... | collective-permute-start | bytes 393224 | tf_op jit(solution)/shard_map/ppermute | solution.py:138
  17.8 17.8 %collective-permute-start.3 = (bf16[2,64,512]{2,1,0:T(8,128)(2,1)S(1)}, bf16[2,64,512]{2,1,0:T(8,128)(2,1)S(1)}, u32[]{:S(2)}, u32[]{:S(2)}) collective-permute-start(bf16[2,64,512]{2,1,0:T(8,128)(2,1)S(1)} %reshape.76), channel_id=1, source_target_pairs={{0,256},{64,320},{128,384},{192,448},{256,0},{320,64},{384,128},{4... | collective-permute-start | bytes 393224 | tf_op jit(solution)/shard_map/ppermute | solution.py:138
  19.8 19.0 %collective-permute-start.4 = (bf16[2,64,512]{2,1,0:T(8,128)(2,1)S(1)}, bf16[2,64,512]{2,1,0:T(8,128)(2,1)S(1)}, u32[]{:S(2)}, u32[]{:S(2)}) collective-permute-start(bf16[2,64,512]{2,1,0:T(8,128)(2,1)S(1)} %reshape.76), channel_id=1, source_target_pairs={{0,320},{64,384},{128,448},{192,0},{256,64},{320,128},{384,192},{4... | collective-permute-start | bytes 393224 | tf_op jit(solution)/shard_map/ppermute | solution.py:138
  28.0 15.9 %collective-permute-start.5 = (bf16[2,64,512]{2,1,0:T(8,128)(2,1)S(1)}, bf16[2,64,512]{2,1,0:T(8,128)(2,1)S(1)}, u32[]{:S(2)}, u32[]{:S(2)}) collective-permute-start(bf16[2,64,512]{2,1,0:T(8,128)(2,1)S(1)} %reshape.76), channel_id=1, source_target_pairs={{0,384},{64,448},{128,0},{192,64},{256,128},{320,192},{384,256},{4... | collective-permute-start | bytes 393224 | tf_op jit(solution)/shard_map/ppermute | solution.py:138
  31.9 14.4 %collective-permute-start.6 = (bf16[2,64,512]{2,1,0:T(8,128)(2,1)S(1)}, bf16[2,64,512]{2,1,0:T(8,128)(2,1)S(1)}, u32[]{:S(2)}, u32[]{:S(2)}) collective-permute-start(bf16[2,64,512]{2,1,0:T(8,128)(2,1)S(1)} %reshape.76), channel_id=1, source_target_pairs={{0,448},{64,0},{128,64},{192,128},{256,192},{320,256},{384,320},{4... | collective-permute-start | bytes 393224 | tf_op jit(solution)/shard_map/ppermute | solution.py:138
  49.7 5.8 %copy-start.5 = (s32[64]{0:T(128)S(1)}, s32[64]{0:T(128)}, u32[]{:S(2)}) copy-start(s32[64]{0:T(128)} %param.14) | copy-start | bytes 772
  49.7 8.0 %copy-start.3 = (bf16[2,4,2,256]{3,2,1,0:T(2,128)(2,1)S(1)}, bf16[2,4,2,256]{3,2,1,0:T(2,128)(2,1)}, u32[]{:S(2)}) copy-start(bf16[2,4,2,256]{3,2,1,0:T(2,128)(2,1)} %param.12) | copy-start | bytes 24580
  49.7 8.1 %copy-start.1 = (bf16[128,2,256]{2,1,0:T(2,128)(2,1)S(1)}, bf16[128,2,256]{2,1,0:T(2,128)(2,1)}, u32[]{:S(2)}) copy-start(bf16[128,2,256]{2,1,0:T(2,128)(2,1)} %param.10) | copy-start | bytes 393220
  49.7 8.1 %copy-start.2 = (bf16[256,8]{0,1:T(8,128)(2,1)S(1)}, bf16[256,8]{0,1:T(8,128)(2,1)}, u32[]{:S(2)}) copy-start(bf16[256,8]{0,1:T(8,128)(2,1)} %param.16) | copy-start | bytes 12292
  49.7 63.5 %copy-start.4 = (s32[128,2]{0,1:T(2,128)S(1)}, s32[128,2]{0,1:T(2,128)}, u32[]{:S(2)}) copy-start(s32[128,2]{0,1:T(2,128)} %param.17) | copy-start | bytes 3076
  49.8 66.1 %all-to-all-start = ((bf16[8,8,64,512]{3,2,1,0:T(8,128)(2,1)}), bf16[8,8,64,512]{3,2,1,0:T(8,128)(2,1)}, u32[]{:S(2)}, u32[]{:S(2)}) async-start(bf16[8,8,64,512]{3,2,1,0:T(8,128)(2,1)} %broadcast_select_fusion), calls=%async_computation | async-start | bytes 8388608 | tf_op jit(solution)/shard_map/all_to_all | solution.py:145

commit v4 on v3

v4 whole, which is shorter than its diff:
```python
import functools
import math

import jax
import jax.numpy as jnp
from jax import lax
from jax.experimental import pallas as pl
from jax.experimental.pallas import tpu as pltpu
from jax.sharding import PartitionSpec as P

HEAD_DIM = 128
PICKS = 2
CHUNK = 512


def attention_kernel(q_ref, pos_ref, *refs, extra_sinks, per_device, part_slots):
    part_count = len(part_slots)
    window_refs = refs[: 2 * part_count]
    xk_ref, xv_ref, gate_ref, out_ref, score_ref = refs[2 * part_count :]
    rows = q_ref.shape[0]
    scale = 1.0 / math.sqrt(HEAD_DIM)
    q = q_ref[...]
    q_stack = jnp.concatenate([q[:, :HEAD_DIM], q[:, HEAD_DIM:]], axis=0)
    stacked = q_stack.shape[0]
    query_pos = lax.broadcasted_iota(jnp.int32, (stacked, 1), 0) % rows
    nt = (((1,), (1,)), ((), ()))

    def scores_of(keys):
        return lax.dot_general(q_stack, keys, nt, preferred_element_type=jnp.float32) * scale

    extra_rows = xk_ref.shape[0]
    extra = scores_of(xk_ref[...])
    extra_pos = lax.broadcasted_iota(jnp.int32, (stacked, extra_rows), 0) % rows
    extra_key = lax.broadcasted_iota(jnp.int32, (stacked, extra_rows), 1)
    extra_visible = (extra_key <= extra_pos) | (
        (extra_key >= rows) & (extra_key < rows + extra_sinks)
    )
    extra = jnp.where(extra_visible, extra, -jnp.inf)
    top = jnp.max(extra, axis=1, keepdims=True)

    chunks = []
    offset = 0
    for part, slots in enumerate(part_slots):
        for c in range(window_refs[2 * part].shape[0] // CHUNK):
            chunks.append((part, c, offset))
            s = scores_of(window_refs[2 * part][pl.ds(c * CHUNK, CHUNK), :])
            if (c * CHUNK) // (slots * per_device) * per_device < rows:
                key_pos = pos_ref[:, pl.ds(offset, CHUNK)]
                s = jnp.where(key_pos > query_pos, s, -jnp.inf)
            score_ref[:, pl.ds(offset, CHUNK)] = s
            top = jnp.maximum(top, jnp.max(s, axis=1, keepdims=True))
            offset += CHUNK

    e = jnp.exp(extra - top)
    total = jnp.sum(e, axis=1, keepdims=True)
    acc = jnp.dot(e.astype(jnp.bfloat16), xv_ref[...], preferred_element_type=jnp.float32)
    for part, c, offset in chunks:
        e = jnp.exp(score_ref[:, pl.ds(offset, CHUNK)] - top)
        total = total + jnp.sum(e, axis=1, keepdims=True)
        acc = acc + jnp.dot(
            e.astype(jnp.bfloat16),
            window_refs[2 * part + 1][pl.ds(c * CHUNK, CHUNK), :],
            preferred_element_type=jnp.float32,
        )
    attended = acc / total
    gate = gate_ref[...]
    out_ref[:, :HEAD_DIM] = (attended[:rows] * gate[:, 0:1]).astype(out_ref.dtype)
    out_ref[:, HEAD_DIM:] = (attended[rows:] * gate[:, 1:2]).astype(out_ref.dtype)


def attend(queries, key_pos, parts, part_slots, extra, gate_live, head_count, extra_sinks, per_device):
    rows = queries.shape[0]
    extra_rows = extra.shape[0]
    window_rows = key_pos.shape[1]
    kernel = functools.partial(
        attention_kernel,
        extra_sinks=extra_sinks,
        per_device=per_device,
        part_slots=part_slots,
    )
    window_specs = []
    window_args = []
    for part in parts:
        window_specs.append(pl.BlockSpec((part.shape[0], HEAD_DIM), lambda h: (0, h)))
        window_specs.append(pl.BlockSpec((part.shape[0], HEAD_DIM), lambda h: (0, head_count + h)))
        window_args += [part, part]
    return pl.pallas_call(
        kernel,
        grid=(head_count,),
        in_specs=[
            pl.BlockSpec((rows, PICKS * HEAD_DIM), lambda h: (0, h)),
            pl.BlockSpec((1, window_rows), lambda h: (0, 0)),
        ]
        + window_specs
        + [
            pl.BlockSpec((extra_rows, HEAD_DIM), lambda h: (0, h)),
            pl.BlockSpec((extra_rows, HEAD_DIM), lambda h: (0, head_count + h)),
            pl.BlockSpec((rows, PICKS), lambda h: (0, 0)),
        ],
        out_specs=pl.BlockSpec((rows, PICKS * HEAD_DIM), lambda h: (0, h)),
        scratch_shapes=[pltpu.VMEM((PICKS * rows, window_rows), jnp.float32)],
        out_shape=jax.ShapeDtypeStruct((rows, head_count * PICKS * HEAD_DIM), jnp.bfloat16),
    )(queries, key_pos, *window_args, extra, extra, gate_live)


def body(queries, suffix_kv, window_kv, sink_kv, lengths, group_ids, hidden_in, router, picks):
    row_count = queries.shape[0]
    head_count = suffix_kv.shape[2] // HEAD_DIM
    partial_value = jnp.dot(hidden_in, router, preferred_element_type=jnp.float32)
    logits = lax.psum(partial_value, "tp")
    experts = jnp.arange(logits.shape[1], dtype=jnp.int32)
    chosen = jnp.sum(
        jnp.where(picks[:, :, None] == experts[None, None, :], logits[:, None, :], 0.0), axis=2
    )
    gate_values = jax.nn.sigmoid(chosen - chosen[:, ::-1])
    z_count = lax.axis_size("z")
    plane_count = lax.axis_size("ylo") * lax.axis_size("x")
    z_me = lax.axis_index("z")
    plane_me = lax.axis_index("ylo") * lax.axis_size("x") + lax.axis_index("x")
    my_group = group_ids[z_me * plane_count + plane_me]
    length = lengths[0]
    is_live = jnp.arange(row_count, dtype=jnp.int32) < length
    gate_live = jnp.where(is_live[:, None], gate_values, 0.0)

    width = 2 * head_count * HEAD_DIM
    per_device = window_kv.shape[1]
    local = window_kv.reshape(window_kv.shape[0], per_device, width)
    near = [0] + [k for k in range(1, z_count) if min(k, z_count - k) == 1]
    far = sorted(
        (k for k in range(1, z_count) if k not in near), key=lambda k: min(k, z_count - k)
    )
    part_shifts = (tuple(near), tuple(far))
    peer_groups = lax.dynamic_slice_in_dim(group_ids, z_me * plane_count, plane_count)
    parts = []
    positions = []
    for shifts in part_shifts:
        arrived = []
        for shift in shifts:
            if shift == 0:
                arrived.append(local)
            else:
                pairs = [(j, (j + shift) % z_count) for j in range(z_count)]
                arrived.append(lax.ppermute(local, "z", pairs))
        by_slot = jnp.stack(arrived)
        outgoing = jnp.where(
            (peer_groups == 0)[:, None, None, None], by_slot[None, :, 0], by_slot[None, :, 1]
        )
        received = lax.all_to_all(
            outgoing, ("ylo", "x"), split_axis=0, concat_axis=0, tiled=True
        )
        parts.append(received.reshape(plane_count * len(shifts) * per_device, width))
        z_of_slot = (z_me - jnp.array(shifts, jnp.int32)) % z_count
        plane_ids = jnp.arange(plane_count, dtype=jnp.int32)
        row_ids = jnp.arange(per_device, dtype=jnp.int32)
        part_pos = (
            (z_of_slot[None, :, None] * plane_count + plane_ids[:, None, None]) * per_device
            + row_ids[None, None, :]
        )
        positions.append(part_pos.reshape(-1))

    sink_rows = lax.dynamic_index_in_dim(sink_kv, my_group, 0, keepdims=False)
    sink_count = sink_rows.shape[0]
    extra_rows = 2 * row_count
    extra = jnp.concatenate(
        [
            suffix_kv.reshape(row_count, width),
            sink_rows.reshape(sink_count, width),
            jnp.zeros((extra_rows - row_count - sink_count, width), suffix_kv.dtype),
        ],
        axis=0,
    )
    key_pos = jnp.concatenate(positions).reshape(1, -1)
    part_slots = tuple(len(shifts) for shifts in part_shifts)
    return attend(
        queries, key_pos, parts, part_slots, extra, gate_live, head_count, sink_count, per_device
    )


def solution(mesh):
    plane_ylo, plane_x = 2, 4
    z_count = mesh.shape["req"] // (plane_ylo * plane_x)
    devices = mesh.devices.reshape(z_count, plane_ylo, plane_x, mesh.shape["tp"])
    inner = jax.sharding.Mesh(devices, ("z", "ylo", "x", "tp"))
    req = ("z", "ylo", "x")
    return jax.shard_map(
        body,
        mesh=inner,
        in_specs=(
            P(req, "tp"),
            P(req, None, "tp"),
            P(None, req, None, "tp"),
            P(None, None, None, "tp"),
            P(req),
            P(),
            P(req, "tp"),
            P("tp", None),
            P(req, None),
        ),
        out_specs=P(req, "tp"),
        check_vma=False,
    )
```

time: 124 us -> 114 us (0.919)
  blocking collectives: 55.3 us -> 35 us
  starting transfers between devices: 38.5 us -> 42.9 us
  waiting for transfers between devices: 10.6 us -> 13.1 us
  local copies, waits for them, and re-layouts: 3.67 us -> 5.89 us
  other arithmetic: 5.04 us -> 6.31 us
    psum x1, blocking collectives: 55.3 us -> 35 us  [body(): logits = lax.psum(partial_value, 'tp')]
    all_to_all x1 -> x2, starting transfers between devices: 5.82 us -> 11.4 us  [body(): lax.all_to_all(outgoing, ('ylo', 'x'), split_axis=0, concat_axis=0, tiled...]
    unnamed x22 -> x27, local copies, waits for them, and re-layouts: 0.13 us -> 2.77 us
    ppermute x7, waiting for transfers between devices: 10.6 us -> 13.1 us  [body(): arrived.append(lax.ppermute(local, 'z', pairs))]
    select_n x3 -> x2, other arithmetic: 2.7 us -> 3.21 us  [body(): jnp.where((peer_groups == 0)[:, None, None, None], by_slot[None, :, 0], b...]
  transfers between devices with their start and end apart: 8 -> 9, of which waited for: 3 -> 3; matrix products, arithmetic and copies ran while one was open for 4% -> 6% of each run, Pallas kernels for 0% -> 0%
where the time goes in v4:
time: 114 us; the launch traced here: 113 us
  starting transfers between devices  42.9 us (38%)
  blocking collectives  35 us (31%)
  waiting for transfers between devices  13.1 us (11%)
  Pallas kernels  7.09 us (6%)
  other arithmetic  6.31 us (6%)
  local copies, waits for them, and re-layouts  5.89 us (5%)
  between operations  2.89 us (3%)
    psum x1, blocking collectives, body(): logits = lax.psum(partial_value, 'tp')  35 us
    ppermute x7, starting transfers between devices, body(): arrived.append(lax.ppermute(local, 'z', pairs))  31.5 us
    ppermute x7, waiting for transfers between devices, body(): arrived.append(lax.ppermute(local, 'z', pairs))  13.1 us
    all_to_all x2, starting transfers between devices, body(): lax.all_to_all(outgoing, ('ylo', 'x'), split_axis=0, concat_axis=0, tiled...  11.4 us
    pallas_call x1, Pallas kernels, attend(): pl.pallas_call(kernel, grid=(head_count,), in_specs=[pl.BlockSpec((rows,...  7.09 us
    select_n x2, other arithmetic, body(): jnp.where((peer_groups == 0)[:, None, None, None], by_slot[None, :, 0], b...  3.21 us
    unnamed x27, local copies, waits for them, and re-layouts  2.77 us
  transfers between devices with their start and end apart: 9, of which 3 were waited for; matrix products, arithmetic and copies ran while one was open for 6% of the time, Pallas kernels for 0%

profile of v4, /device:TPU:78, one launch (start us, length us, event | category | flops | bytes accessed | tf_op | source)
XLA Modules:
  0.0 113.3 jit_solution(10796264250431378538)
XLA Ops:
  0.0 0.0 copy-start
  0.0 1.0 reshape.89
  1.0 4.3 %collective-permute-start = (bf16[2,64,512]{2,1,0:T(8,128)(2,1)S(1)}, bf16[2,64,512]{2,1,0:T(8,128)(2,1)S(1)}, u32[]{:S(2)}, u32[]{:S(2)}) collective-permute-start(bf16[2,64,512]{2,1,0:T(8,128)(2,1)S(1)} %reshape.89), channel_id=1, source_target_pairs={{0,64},{64,128},{128,192},{192,256},{256,320},{320,384},{384,448},... | collective-permute-start | bytes 393224 | tf_op jit(solution)/shard_map/ppermute | solution.py:143
  5.3 1.9 %collective-permute-start.1 = (bf16[2,64,512]{2,1,0:T(8,128)(2,1)S(1)}, bf16[2,64,512]{2,1,0:T(8,128)(2,1)S(1)}, u32[]{:S(2)}, u32[]{:S(2)}) collective-permute-start(bf16[2,64,512]{2,1,0:T(8,128)(2,1)S(1)} %reshape.89), channel_id=1, source_target_pairs={{0,448},{64,0},{128,64},{192,128},{256,192},{320,256},{384,320},{4... | collective-permute-start | bytes 393224 | tf_op jit(solution)/shard_map/ppermute | solution.py:143
  7.3 1.0 stack_reshape.3
  8.3 0.7 dynamic-slice_compare_fusion
  9.0 0.0 collective-permute-done
  9.0 3.8 %collective-permute-done.1 = bf16[2,64,512]{2,1,0:T(8,128)(2,1)S(1)} collective-permute-done((bf16[2,64,512]{2,1,0:T(8,128)(2,1)S(1)}, bf16[2,64,512]{2,1,0:T(8,128)(2,1)S(1)}, u32[]{:S(2)}, u32[]{:S(2)}) %collective-permute-start.1) | collective-permute-done | bytes 131104 | tf_op jit(solution)/shard_map/ppermute | solution.py:143
  12.9 1.4 %broadcast_select_fusion.1 = bf16[8,3,64,512]{3,2,1,0:T(8,128)(2,1)} fusion(pred[8]{0:T(512)(128)(4,1)S(1)} %dynamic-slice_compare_fusion, bf16[3,64,512]{2,1,0:T(8,128)(2,1)S(1)} %get-tuple-element.8, bf16[3,64,512]{2,1,0:T(8,128)(2,1)S(1)} %get-tuple-element.7), kind=kLoop, calls=%fused_computation.1 | loop fusion | flops 786432 | bytes 1966088 | tf_op jit(solution)/shard_map/jit(_where)/select_n | solution.py:145
  14.3 5.7 %all-to-all-start = ((bf16[8,3,64,512]{3,2,1,0:T(8,128)(2,1)}), bf16[8,3,64,512]{3,2,1,0:T(8,128)(2,1)S(1)}, u32[]{:S(2)}, u32[]{:S(2)}) async-start(bf16[8,3,64,512]{3,2,1,0:T(8,128)(2,1)} %broadcast_select_fusion.1), calls=%async_computation | async-start | bytes 3145728 | tf_op jit(solution)/shard_map/all_to_all | solution.py:148
  19.9 7.9 %collective-permute-start.2 = (bf16[2,64,512]{2,1,0:T(8,128)(2,1)S(1)}, bf16[2,64,512]{2,1,0:T(8,128)(2,1)S(1)}, u32[]{:S(2)}, u32[]{:S(2)}) collective-permute-start(bf16[2,64,512]{2,1,0:T(8,128)(2,1)S(1)} %reshape.89), channel_id=1, source_target_pairs={{0,128},{64,192},{128,256},{192,320},{256,384},{320,448},{384,0},{... | collective-permute-start | bytes 393224 | tf_op jit(solution)/shard_map/ppermute | solution.py:143
  27.8 2.6 %collective-permute-start.3 = (bf16[2,64,512]{2,1,0:T(8,128)(2,1)S(1)}, bf16[2,64,512]{2,1,0:T(8,128)(2,1)S(1)}, u32[]{:S(2)}, u32[]{:S(2)}) collective-permute-start(bf16[2,64,512]{2,1,0:T(8,128)(2,1)S(1)} %reshape.89), channel_id=1, source_target_pairs={{0,384},{64,448},{128,0},{192,64},{256,128},{320,192},{384,256},{4... | collective-permute-start | bytes 393224 | tf_op jit(solution)/shard_map/ppermute | solution.py:143
  30.4 5.1 %collective-permute-start.4 = (bf16[2,64,512]{2,1,0:T(8,128)(2,1)S(1)}, bf16[2,64,512]{2,1,0:T(8,128)(2,1)S(1)}, u32[]{:S(2)}, u32[]{:S(2)}) collective-permute-start(bf16[2,64,512]{2,1,0:T(8,128)(2,1)S(1)} %reshape.89), channel_id=1, source_target_pairs={{0,192},{64,256},{128,320},{192,384},{256,448},{320,0},{384,64},{4... | collective-permute-start | bytes 393224 | tf_op jit(solution)/shard_map/ppermute | solution.py:143
  35.5 3.8 %collective-permute-start.5 = (bf16[2,64,512]{2,1,0:T(8,128)(2,1)S(1)}, bf16[2,64,512]{2,1,0:T(8,128)(2,1)S(1)}, u32[]{:S(2)}, u32[]{:S(2)}) collective-permute-start(bf16[2,64,512]{2,1,0:T(8,128)(2,1)S(1)} %reshape.89), channel_id=1, source_target_pairs={{0,320},{64,384},{128,448},{192,0},{256,64},{320,128},{384,192},{4... | collective-permute-start | bytes 393224 | tf_op jit(solution)/shard_map/ppermute | solution.py:143
  39.3 6.0 %collective-permute-start.6 = (bf16[2,64,512]{2,1,0:T(8,128)(2,1)S(1)}, bf16[2,64,512]{2,1,0:T(8,128)(2,1)S(1)}, u32[]{:S(2)}, u32[]{:S(2)}) collective-permute-start(bf16[2,64,512]{2,1,0:T(8,128)(2,1)S(1)} %reshape.89), channel_id=1, source_target_pairs={{0,256},{64,320},{128,384},{192,448},{256,0},{320,64},{384,128},{4... | collective-permute-start | bytes 393224 | tf_op jit(solution)/shard_map/ppermute | solution.py:143
  45.3 0.0 collective-permute-done.2
  45.3 0.0 collective-permute-done.3
  45.3 0.0 collective-permute-done.4
  45.3 4.8 %collective-permute-done.5 = bf16[2,64,512]{2,1,0:T(8,128)(2,1)S(1)} collective-permute-done((bf16[2,64,512]{2,1,0:T(8,128)(2,1)S(1)}, bf16[2,64,512]{2,1,0:T(8,128)(2,1)S(1)}, u32[]{:S(2)}, u32[]{:S(2)}) %collective-permute-start.5) | collective-permute-done | bytes 131104 | tf_op jit(solution)/shard_map/ppermute | solution.py:143
  50.2 4.4 %collective-permute-done.6 = bf16[2,64,512]{2,1,0:T(8,128)(2,1)S(1)} collective-permute-done((bf16[2,64,512]{2,1,0:T(8,128)(2,1)S(1)}, bf16[2,64,512]{2,1,0:T(8,128)(2,1)S(1)}, u32[]{:S(2)}, u32[]{:S(2)}) %collective-permute-start.6) | collective-permute-done | bytes 131104 | tf_op jit(solution)/shard_map/ppermute | solution.py:143
  54.7 1.8 %broadcast_select_fusion = bf16[8,5,64,512]{3,2,1,0:T(8,128)(2,1)} fusion(pred[8]{0:T(512)(128)(4,1)S(1)} %dynamic-slice_compare_fusion, bf16[5,64,512]{2,1,0:T(8,128)(2,1)S(1)} %get-tuple-element.6, bf16[5,64,512]{2,1,0:T(8,128)(2,1)S(1)} %get-tuple-element.5), kind=kLoop, calls=%fused_computation | loop fusion | flops 1310720 | bytes 3276808 | tf_op jit(solution)/shard_map/jit(_where)/select_n | solution.py:145
  56.5 0.0 copy-start.7
  56.5 0.0 copy-start.5
  56.5 0.0 copy-start.3
  56.6 0.0 copy-start.9
  56.6 0.0 copy-start.8
  56.6 0.0 copy-start.4
  56.6 0.0 copy-start.6
  56.6 0.0 all-to-all-done
  56.6 0.0 copy-start.2
  56.6 1.2 %copy-done.2 = bf16[8,3,64,512]{3,2,1,0:T(8,128)(2,1)} copy-done((bf16[8,3,64,512]{3,2,1,0:T(8,128)(2,1)}, bf16[8,3,64,512]{3,2,1,0:T(8,128)(2,1)S(1)}, u32[]{:S(2)}) %copy-start.2) | copy-done | bytes 1572888
  57.8 5.7 %all-to-all-start.1 = ((bf16[8,5,64,512]{3,2,1,0:T(8,128)(2,1)}), bf16[8,5,64,512]{3,2,1,0:T(8,128)(2,1)S(1)}, u32[]{:S(2)}, u32[]{:S(2)}) async-start(bf16[8,5,64,512]{3,2,1,0:T(8,128)(2,1)} %broadcast_select_fusion), calls=%async_computation.1 | async-start | bytes 5242880 | tf_op jit(solution)/shard_map/all_to_all | solution.py:148
  63.5 0.0 copy-done.7
  63.5 0.6 dynamic_slice.11
  66.0 0.0 copy-done.5
  66.0 0.0 copy-done.3
  66.1 0.0 copy-done.9
  66.1 0.1 iota_add_fusion
  66.2 0.1 add.118
  66.3 0.0 copy-done.8
  66.3 0.1 iota_add_fusion.1
  66.4 0.1 add.110
  66.5 0.0 copy-done
  66.5 0.0 copy-done.4
  66.5 0.1 fusion.4
  66.6 35.0 %psum.7 = f32[128,8]{0,1:T(8,128)S(1)} all-reduce(f32[128,8]{0,1:T(8,128)S(1)} %fusion.4), channel_id=1, replica_groups=mesh['z'=8,'ylo'=2,'x'=4,'tp'=8] {'tp'}, use_global_device_ids=true, to_apply=%region_0.0 | all-reduce | flops 1024 | bytes 8192 | tf_op jit(solution)/shard_map/psum | solution.py:110
  101.6 0.0 copy-done.6
  101.6 0.1 copy.17
  101.7 0.1 rev.3
  102.5 0.1 pad.2.clone
  102.6 0.6 pad_add_fusion
  103.2 0.7 divide_select_fusion.refs_6_
  103.9 0.8 maximum_maximum_fusion.refs_4_.refs_5_
  104.7 0.0 all-to-all-done.1
  104.7 0.0 copy-start.1
  104.7 1.5 %copy-done.1 = bf16[8,5,64,512]{3,2,1,0:T(8,128)(2,1)} copy-done((bf16[8,5,64,512]{3,2,1,0:T(8,128)(2,1)}, bf16[8,5,64,512]{3,2,1,0:T(8,128)(2,1)S(1)}, u32[]{:S(2)}) %copy-start.1) | copy-done | bytes 2621464
  106.2 7.1 %shard_map.109 = bf16[128,512]{1,0:T(8,128)(2,1)} custom-call(bf16[128,512]{1,0:T(8,128)(2,1)} %q_ref.1, s32[1,4096]{1,0:T(1,128)} %bitcast.42, bf16[1536,512]{1,0:T(8,128)(2,1)} %bitcast.36, bf16[1536,512]{1,0:T(8,128)(2,1)} %bitcast.37, bf16[2560,512]{1,0:T(8,128)(2,1)} %bitcast.34, bf16[2560,512]{1,0:T(8,128)(2,1)} %bitcast.35, ...), custom_call_target="tpu_custom_call" | custom-call | tf_op jit(solution)/shard_map/pallas_call | solution.py:87
  (18 shorter events, 0.3 us)
Async XLA Ops:
  0.0 66.5 %copy-start = (bf16[128,256]{1,0:T(8,128)(2,1)S(1)}, bf16[128,256]{1,0:T(8,128)(2,1)}, u32[]{:S(2)}) copy-start(bf16[128,256]{1,0:T(8,128)(2,1)} %param.17) | copy-start | bytes 196612
  1.0 8.0 %collective-permute-start = (bf16[2,64,512]{2,1,0:T(8,128)(2,1)S(1)}, bf16[2,64,512]{2,1,0:T(8,128)(2,1)S(1)}, u32[]{:S(2)}, u32[]{:S(2)}) collective-permute-start(bf16[2,64,512]{2,1,0:T(8,128)(2,1)S(1)} %reshape.89), channel_id=1, source_target_pairs={{0,64},{64,128},{128,192},{192,256},{256,320},{320,384},{384,448},... | collective-permute-start | bytes 393224 | tf_op jit(solution)/shard_map/ppermute | solution.py:143
  5.3 7.5 %collective-permute-start.1 = (bf16[2,64,512]{2,1,0:T(8,128)(2,1)S(1)}, bf16[2,64,512]{2,1,0:T(8,128)(2,1)S(1)}, u32[]{:S(2)}, u32[]{:S(2)}) collective-permute-start(bf16[2,64,512]{2,1,0:T(8,128)(2,1)S(1)} %reshape.89), channel_id=1, source_target_pairs={{0,448},{64,0},{128,64},{192,128},{256,192},{320,256},{384,320},{4... | collective-permute-start | bytes 393224 | tf_op jit(solution)/shard_map/ppermute | solution.py:143
  14.3 42.3 %all-to-all-start = ((bf16[8,3,64,512]{3,2,1,0:T(8,128)(2,1)}), bf16[8,3,64,512]{3,2,1,0:T(8,128)(2,1)S(1)}, u32[]{:S(2)}, u32[]{:S(2)}) async-start(bf16[8,3,64,512]{3,2,1,0:T(8,128)(2,1)} %broadcast_select_fusion.1), calls=%async_computation | async-start | bytes 3145728 | tf_op jit(solution)/shard_map/all_to_all | solution.py:148
  19.9 25.3 %collective-permute-start.2 = (bf16[2,64,512]{2,1,0:T(8,128)(2,1)S(1)}, bf16[2,64,512]{2,1,0:T(8,128)(2,1)S(1)}, u32[]{:S(2)}, u32[]{:S(2)}) collective-permute-start(bf16[2,64,512]{2,1,0:T(8,128)(2,1)S(1)} %reshape.89), channel_id=1, source_target_pairs={{0,128},{64,192},{128,256},{192,320},{256,384},{320,448},{384,0},{... | collective-permute-start | bytes 393224 | tf_op jit(solution)/shard_map/ppermute | solution.py:143
  27.8 17.5 %collective-permute-start.3 = (bf16[2,64,512]{2,1,0:T(8,128)(2,1)S(1)}, bf16[2,64,512]{2,1,0:T(8,128)(2,1)S(1)}, u32[]{:S(2)}, u32[]{:S(2)}) collective-permute-start(bf16[2,64,512]{2,1,0:T(8,128)(2,1)S(1)} %reshape.89), channel_id=1, source_target_pairs={{0,384},{64,448},{128,0},{192,64},{256,128},{320,192},{384,256},{4... | collective-permute-start | bytes 393224 | tf_op jit(solution)/shard_map/ppermute | solution.py:143
  30.4 14.9 %collective-permute-start.4 = (bf16[2,64,512]{2,1,0:T(8,128)(2,1)S(1)}, bf16[2,64,512]{2,1,0:T(8,128)(2,1)S(1)}, u32[]{:S(2)}, u32[]{:S(2)}) collective-permute-start(bf16[2,64,512]{2,1,0:T(8,128)(2,1)S(1)} %reshape.89), channel_id=1, source_target_pairs={{0,192},{64,256},{128,320},{192,384},{256,448},{320,0},{384,64},{4... | collective-permute-start | bytes 393224 | tf_op jit(solution)/shard_map/ppermute | solution.py:143
  35.5 14.7 %collective-permute-start.5 = (bf16[2,64,512]{2,1,0:T(8,128)(2,1)S(1)}, bf16[2,64,512]{2,1,0:T(8,128)(2,1)S(1)}, u32[]{:S(2)}, u32[]{:S(2)}) collective-permute-start(bf16[2,64,512]{2,1,0:T(8,128)(2,1)S(1)} %reshape.89), channel_id=1, source_target_pairs={{0,320},{64,384},{128,448},{192,0},{256,64},{320,128},{384,192},{4... | collective-permute-start | bytes 393224 | tf_op jit(solution)/shard_map/ppermute | solution.py:143
  39.3 15.4 %collective-permute-start.6 = (bf16[2,64,512]{2,1,0:T(8,128)(2,1)S(1)}, bf16[2,64,512]{2,1,0:T(8,128)(2,1)S(1)}, u32[]{:S(2)}, u32[]{:S(2)}) collective-permute-start(bf16[2,64,512]{2,1,0:T(8,128)(2,1)S(1)} %reshape.89), channel_id=1, source_target_pairs={{0,256},{64,320},{128,384},{192,448},{256,0},{320,64},{384,128},{4... | collective-permute-start | bytes 393224 | tf_op jit(solution)/shard_map/ppermute | solution.py:143
  56.5 6.9 %copy-start.7 = (s32[64]{0:T(128)S(1)}, s32[64]{0:T(128)}, u32[]{:S(2)}) copy-start(s32[64]{0:T(128)} %param.16) | copy-start | bytes 772
  56.5 9.5 %copy-start.5 = (bf16[2,4,2,256]{3,2,1,0:T(2,128)(2,1)S(1)}, bf16[2,4,2,256]{3,2,1,0:T(2,128)(2,1)}, u32[]{:S(2)}) copy-start(bf16[2,4,2,256]{3,2,1,0:T(2,128)(2,1)} %param.14) | copy-start | bytes 24580
  56.5 9.5 %copy-start.3 = (bf16[128,2,256]{2,1,0:T(2,128)(2,1)S(1)}, bf16[128,2,256]{2,1,0:T(2,128)(2,1)}, u32[]{:S(2)}) copy-start(bf16[128,2,256]{2,1,0:T(2,128)(2,1)} %param.12) | copy-start | bytes 393220
  56.6 9.5 %copy-start.9 = (s32[5]{0:T(128)S(1)}, s32[5]{0:T(128)}, u32[]{:S(2)}) copy-start(s32[5]{0:T(128)} %constant.68) | copy-start | bytes 64
  56.6 9.7 %copy-start.8 = (s32[3]{0:T(128)S(1)}, s32[3]{0:T(128)}, u32[]{:S(2)}) copy-start(s32[3]{0:T(128)} %constant.67) | copy-start | bytes 40
  56.6 9.9 %copy-start.4 = (bf16[256,8]{0,1:T(8,128)(2,1)S(1)}, bf16[256,8]{0,1:T(8,128)(2,1)}, u32[]{:S(2)}) copy-start(bf16[256,8]{0,1:T(8,128)(2,1)} %param.18) | copy-start | bytes 12292
  56.6 45.0 %copy-start.6 = (s32[128,2]{0,1:T(2,128)S(1)}, s32[128,2]{0,1:T(2,128)}, u32[]{:S(2)}) copy-start(s32[128,2]{0,1:T(2,128)} %param.19) | copy-start | bytes 3076
  56.6 1.2 %copy-start.2 = (bf16[8,3,64,512]{3,2,1,0:T(8,128)(2,1)}, bf16[8,3,64,512]{3,2,1,0:T(8,128)(2,1)S(1)}, u32[]{:S(2)}) copy-start(bf16[8,3,64,512]{3,2,1,0:T(8,128)(2,1)S(1)} %all-to-all-done) | copy-start | bytes 4718596
  57.8 46.9 %all-to-all-start.1 = ((bf16[8,5,64,512]{3,2,1,0:T(8,128)(2,1)}), bf16[8,5,64,512]{3,2,1,0:T(8,128)(2,1)S(1)}, u32[]{:S(2)}, u32[]{:S(2)}) async-start(bf16[8,5,64,512]{3,2,1,0:T(8,128)(2,1)} %broadcast_select_fusion), calls=%async_computation.1 | async-start | bytes 5242880 | tf_op jit(solution)/shard_map/all_to_all | solution.py:148
  104.7 1.5 %copy-start.1 = (bf16[8,5,64,512]{3,2,1,0:T(8,128)(2,1)}, bf16[8,5,64,512]{3,2,1,0:T(8,128)(2,1)S(1)}, u32[]{:S(2)}) copy-start(bf16[8,5,64,512]{3,2,1,0:T(8,128)(2,1)S(1)} %all-to-all-done.1) | copy-start | bytes 7864324

commit v5 on v4

--- a/solution.py
+++ b/solution.py
@@ -125,22 +125,23 @@
     width = 2 * head_count * HEAD_DIM
     per_device = window_kv.shape[1]
     local = window_kv.reshape(window_kv.shape[0], per_device, width)
-    near = [0] + [k for k in range(1, z_count) if min(k, z_count - k) == 1]
-    far = sorted(
-        (k for k in range(1, z_count) if k not in near), key=lambda k: min(k, z_count - k)
-    )
-    part_shifts = (tuple(near), tuple(far))
+    def shifted(value, shift):
+        pairs = [(j, (j + shift) % z_count) for j in range(z_count)]
+        return lax.ppermute(value, "z", pairs)
+
+    up = shifted(local, 1)
+    down = shifted(local, z_count - 1)
+    near_shifts = (0, 1, z_count - 1)
+    near_slots = [local, up, down]
+    far_up = shifted(jnp.stack([down, local, up]), 3)
+    far_down = shifted(jnp.stack([local, up]), z_count - 3)
+    far_shifts = (2, 3, 4, z_count - 3, z_count - 2)
+    far_slots = [far_up[0], far_up[1], far_up[2], far_down[0], far_down[1]]
+    part_shifts = (near_shifts, far_shifts)
     peer_groups = lax.dynamic_slice_in_dim(group_ids, z_me * plane_count, plane_count)
     parts = []
     positions = []
-    for shifts in part_shifts:
-        arrived = []
-        for shift in shifts:
-            if shift == 0:
-                arrived.append(local)
-            else:
-                pairs = [(j, (j + shift) % z_count) for j in range(z_count)]
-                arrived.append(lax.ppermute(local, "z", pairs))
+    for shifts, arrived in zip(part_shifts, (near_slots, far_slots)):
         by_slot = jnp.stack(arrived)
         outgoing = jnp.where(
             (peer_groups == 0)[:, None, None, None], by_slot[None, :, 0], by_slot[None, :, 1]

time: 114 us -> 112 us (0.982)
  the two profiles are of different devices: /device:TPU:78 before, /device:TPU:142 now
where the time goes in v5:
time: 112 us; the launch traced here: 111 us
  blocking collectives  36.2 us (32%)
  waiting for transfers between devices  26.5 us (24%)
  starting transfers between devices  26.4 us (24%)
  Pallas kernels  7.09 us (6%)
  other arithmetic  6.35 us (6%)
  local copies, waits for them, and re-layouts  5.87 us (5%)
  between operations  2.84 us (3%)
    psum x1, blocking collectives, body(): logits = lax.psum(partial_value, 'tp')  36.2 us
    ppermute x4, waiting for transfers between devices, shifted(): return lax.ppermute(value, 'z', pairs)  26.5 us
    ppermute x4, starting transfers between devices, shifted(): return lax.ppermute(value, 'z', pairs)  15 us
    all_to_all x2, starting transfers between devices, body(): lax.all_to_all(outgoing, ('ylo', 'x'), split_axis=0, concat_axis=0, tiled...  11.4 us
    pallas_call x1, Pallas kernels, attend(): pl.pallas_call(kernel, grid=(head_count,), in_specs=[pl.BlockSpec((rows,...  7.09 us
    select_n x2, other arithmetic, body(): jnp.where((peer_groups == 0)[:, None, None, None], by_slot[None, :, 0], b...  3.2 us
    unnamed x24, local copies, waits for them, and re-layouts  2.75 us
  transfers between devices with their start and end apart: 6, of which 2 were waited for; matrix products, arithmetic and copies ran while one was open for 6% of the time, Pallas kernels for 0%

profile of v5, /device:TPU:142, one launch (start us, length us, event | category | flops | bytes accessed | tf_op | source)
XLA Modules:
  0.0 111.4 jit_solution(5722139577816481375)
XLA Ops:
  0.0 0.0 copy-start
  0.0 1.0 reshape.89
  1.0 4.3 %collective-permute-start = (bf16[2,64,512]{2,1,0:T(8,128)(2,1)S(1)}, bf16[2,64,512]{2,1,0:T(8,128)(2,1)S(1)}, u32[]{:S(2)}, u32[]{:S(2)}) collective-permute-start(bf16[2,64,512]{2,1,0:T(8,128)(2,1)S(1)} %reshape.89), channel_id=1, source_target_pairs={{0,64},{64,128},{128,192},{192,256},{256,320},{320,384},{384,448},... | collective-permute-start | bytes 393224 | tf_op jit(solution)/shard_map/ppermute | solution.py:130
  5.3 1.9 %collective-permute-start.1 = (bf16[2,64,512]{2,1,0:T(8,128)(2,1)S(1)}, bf16[2,64,512]{2,1,0:T(8,128)(2,1)S(1)}, u32[]{:S(2)}, u32[]{:S(2)}) collective-permute-start(bf16[2,64,512]{2,1,0:T(8,128)(2,1)S(1)} %reshape.89), channel_id=1, source_target_pairs={{0,448},{64,0},{128,64},{192,128},{256,192},{320,256},{384,320},{4... | collective-permute-start | bytes 393224 | tf_op jit(solution)/shard_map/ppermute | solution.py:130
  7.3 1.0 stack_reshape.2
  8.3 0.7 dynamic-slice_compare_fusion
  9.0 0.0 collective-permute-done
  9.0 5.0 %collective-permute-done.1 = bf16[2,64,512]{2,1,0:T(8,128)(2,1)S(1)} collective-permute-done((bf16[2,64,512]{2,1,0:T(8,128)(2,1)S(1)}, bf16[2,64,512]{2,1,0:T(8,128)(2,1)S(1)}, u32[]{:S(2)}, u32[]{:S(2)}) %collective-permute-start.1) | collective-permute-done | bytes 131104 | tf_op jit(solution)/shard_map/ppermute | solution.py:130
  14.0 0.1 pad_maximum_fusion.1
  14.1 1.4 %broadcast_select_fusion.1 = bf16[8,3,64,512]{3,2,1,0:T(8,128)(2,1)} fusion(pred[8]{0:T(512)(128)(4,1)S(1)} %dynamic-slice_compare_fusion, bf16[3,64,512]{2,1,0:T(8,128)(2,1)S(1)} %get-tuple-element.10, bf16[3,64,512]{2,1,0:T(8,128)(2,1)S(1)} %get-tuple-element.9), kind=kLoop, calls=%fused_computation.1 | loop fusion | flops 786432 | bytes 1966088 | tf_op jit(solution)/shard_map/jit(_where)/select_n | solution.py:146
  15.5 5.7 %all-to-all-start = ((bf16[8,3,64,512]{3,2,1,0:T(8,128)(2,1)}), bf16[8,3,64,512]{3,2,1,0:T(8,128)(2,1)S(1)}, u32[]{:S(2)}, u32[]{:S(2)}) async-start(bf16[8,3,64,512]{3,2,1,0:T(8,128)(2,1)} %broadcast_select_fusion.1), calls=%async_computation | async-start | bytes 3145728 | tf_op jit(solution)/shard_map/all_to_all | solution.py:149
  21.2 5.5 %collective-permute-start.2 = (bf16[3,2,64,512]{3,2,1,0:T(8,128)(2,1)S(1)}, bf16[3,2,64,512]{3,2,1,0:T(8,128)(2,1)S(1)}, u32[]{:S(2)}, u32[]{:S(2)}) collective-permute-start(bf16[3,2,64,512]{3,2,1,0:T(8,128)(2,1)S(1)} %get-tuple-element.7), channel_id=1, source_target_pairs={{0,192},{64,256},{128,320},{192,384},{256,448},{320,0},{384,64},{4... | collective-permute-start | bytes 1179656 | tf_op jit(solution)/shard_map/ppermute | solution.py:130
  26.7 3.4 %collective-permute-start.3 = (bf16[2,2,64,512]{3,2,1,0:T(8,128)(2,1)S(1)}, bf16[2,2,64,512]{3,2,1,0:T(8,128)(2,1)S(1)}, u32[]{:S(2)}, u32[]{:S(2)}) collective-permute-start(bf16[2,2,64,512]{3,2,1,0:T(8,128)(2,1)S(1)} %pad_maximum_fusion.2), channel_id=1, source_target_pairs={{0,320},{64,384},{128,448},{192,0},{256,64},{320,128},{384,192},{4... | collective-permute-start | bytes 786440 | tf_op jit(solution)/shard_map/ppermute | solution.py:130
  30.1 21.5 %collective-permute-done.2 = bf16[3,2,64,512]{3,2,1,0:T(8,128)(2,1)S(1)} collective-permute-done((bf16[3,2,64,512]{3,2,1,0:T(8,128)(2,1)S(1)}, bf16[3,2,64,512]{3,2,1,0:T(8,128)(2,1)S(1)}, u32[]{:S(2)}, u32[]{:S(2)}) %collective-permute-start.2) | collective-permute-done | bytes 393248 | tf_op jit(solution)/shard_map/ppermute | solution.py:130
  51.6 0.0 collective-permute-done.3
  51.7 1.8 %broadcast_select_fusion = bf16[8,5,64,512]{3,2,1,0:T(8,128)(2,1)} fusion(pred[8]{0:T(512)(128)(4,1)S(1)} %dynamic-slice_compare_fusion, bf16[5,64,512]{2,1,0:T(8,128)(2,1)S(1)} %get-tuple-element.6, bf16[5,64,512]{2,1,0:T(8,128)(2,1)S(1)} %get-tuple-element.5), kind=kLoop, calls=%fused_computation | loop fusion | flops 1310720 | bytes 3276808 | tf_op jit(solution)/shard_map/jit(_where)/select_n | solution.py:146
  53.5 0.0 copy-start.7
  53.5 0.0 copy-start.5
  53.5 0.0 copy-start.3
  53.5 0.0 copy-start.9
  53.5 0.0 copy-start.8
  53.5 0.0 copy-start.4
  53.5 0.0 copy-start.6
  53.6 0.0 all-to-all-done
  53.6 0.0 copy-start.2
  53.6 1.2 %copy-done.2 = bf16[8,3,64,512]{3,2,1,0:T(8,128)(2,1)} copy-done((bf16[8,3,64,512]{3,2,1,0:T(8,128)(2,1)}, bf16[8,3,64,512]{3,2,1,0:T(8,128)(2,1)S(1)}, u32[]{:S(2)}) %copy-start.2) | copy-done | bytes 1572888
  54.7 5.7 %all-to-all-start.1 = ((bf16[8,5,64,512]{3,2,1,0:T(8,128)(2,1)}), bf16[8,5,64,512]{3,2,1,0:T(8,128)(2,1)S(1)}, u32[]{:S(2)}, u32[]{:S(2)}) async-start(bf16[8,5,64,512]{3,2,1,0:T(8,128)(2,1)} %broadcast_select_fusion), calls=%async_computation.1 | async-start | bytes 5242880 | tf_op jit(solution)/shard_map/all_to_all | solution.py:149
  60.4 0.0 copy-done.7
  60.4 0.6 dynamic_slice.11
  63.0 0.0 copy-done.5
  63.0 0.0 copy-done.3
  63.0 0.0 copy-done.9
  63.1 0.1 iota_add_fusion
  63.2 0.1 add.118
  63.2 0.0 copy-done.8
  63.3 0.1 iota_add_fusion.1
  63.3 0.1 add.110
  63.4 0.0 copy-done
  63.4 0.0 copy-done.4
  63.4 0.1 fusion.4
  63.5 36.2 %psum.7 = f32[128,8]{0,1:T(8,128)S(1)} all-reduce(f32[128,8]{0,1:T(8,128)S(1)} %fusion.4), channel_id=1, replica_groups=mesh['z'=8,'ylo'=2,'x'=4,'tp'=8] {'tp'}, use_global_device_ids=true, to_apply=%region_0.0 | all-reduce | flops 1024 | bytes 8192 | tf_op jit(solution)/shard_map/psum | solution.py:110
  99.7 0.0 copy-done.6
  99.8 0.1 copy.17
  99.9 0.1 rev.3
  100.6 0.1 pad.2.clone
  100.7 0.6 pad_add_fusion
  101.3 0.7 divide_select_fusion.refs_6_
  102.0 0.8 maximum_maximum_fusion.refs_4_.refs_5_
  102.8 0.0 all-to-all-done.1
  102.8 0.0 copy-start.1
  102.8 1.5 %copy-done.1 = bf16[8,5,64,512]{3,2,1,0:T(8,128)(2,1)} copy-done((bf16[8,5,64,512]{3,2,1,0:T(8,128)(2,1)}, bf16[8,5,64,512]{3,2,1,0:T(8,128)(2,1)S(1)}, u32[]{:S(2)}) %copy-start.1) | copy-done | bytes 2621464
  104.3 7.1 %shard_map.109 = bf16[128,512]{1,0:T(8,128)(2,1)} custom-call(bf16[128,512]{1,0:T(8,128)(2,1)} %q_ref.1, s32[1,4096]{1,0:T(1,128)} %bitcast.33, bf16[1536,512]{1,0:T(8,128)(2,1)} %bitcast.26, bf16[1536,512]{1,0:T(8,128)(2,1)} %bitcast.27, bf16[2560,512]{1,0:T(8,128)(2,1)} %bitcast.24, bf16[2560,512]{1,0:T(8,128)(2,1)} %bitcast.25, ...), custom_call_target="tpu_custom_call" | custom-call | tf_op jit(solution)/shard_map/pallas_call | solution.py:87
  (15 shorter events, 0.2 us)
Async XLA Ops:
  0.0 63.4 %copy-start = (bf16[128,256]{1,0:T(8,128)(2,1)S(1)}, bf16[128,256]{1,0:T(8,128)(2,1)}, u32[]{:S(2)}) copy-start(bf16[128,256]{1,0:T(8,128)(2,1)} %param.17) | copy-start | bytes 196612
  1.0 8.0 %collective-permute-start = (bf16[2,64,512]{2,1,0:T(8,128)(2,1)S(1)}, bf16[2,64,512]{2,1,0:T(8,128)(2,1)S(1)}, u32[]{:S(2)}, u32[]{:S(2)}) collective-permute-start(bf16[2,64,512]{2,1,0:T(8,128)(2,1)S(1)} %reshape.89), channel_id=1, source_target_pairs={{0,64},{64,128},{128,192},{192,256},{256,320},{320,384},{384,448},... | collective-permute-start | bytes 393224 | tf_op jit(solution)/shard_map/ppermute | solution.py:130
  5.3 8.7 %collective-permute-start.1 = (bf16[2,64,512]{2,1,0:T(8,128)(2,1)S(1)}, bf16[2,64,512]{2,1,0:T(8,128)(2,1)S(1)}, u32[]{:S(2)}, u32[]{:S(2)}) collective-permute-start(bf16[2,64,512]{2,1,0:T(8,128)(2,1)S(1)} %reshape.89), channel_id=1, source_target_pairs={{0,448},{64,0},{128,64},{192,128},{256,192},{320,256},{384,320},{4... | collective-permute-start | bytes 393224 | tf_op jit(solution)/shard_map/ppermute | solution.py:130
  15.5 38.1 %all-to-all-start = ((bf16[8,3,64,512]{3,2,1,0:T(8,128)(2,1)}), bf16[8,3,64,512]{3,2,1,0:T(8,128)(2,1)S(1)}, u32[]{:S(2)}, u32[]{:S(2)}) async-start(bf16[8,3,64,512]{3,2,1,0:T(8,128)(2,1)} %broadcast_select_fusion.1), calls=%async_computation | async-start | bytes 3145728 | tf_op jit(solution)/shard_map/all_to_all | solution.py:149
  21.2 30.4 %collective-permute-start.2 = (bf16[3,2,64,512]{3,2,1,0:T(8,128)(2,1)S(1)}, bf16[3,2,64,512]{3,2,1,0:T(8,128)(2,1)S(1)}, u32[]{:S(2)}, u32[]{:S(2)}) collective-permute-start(bf16[3,2,64,512]{3,2,1,0:T(8,128)(2,1)S(1)} %get-tuple-element.7), channel_id=1, source_target_pairs={{0,192},{64,256},{128,320},{192,384},{256,448},{320,0},{384,64},{4... | collective-permute-start | bytes 1179656 | tf_op jit(solution)/shard_map/ppermute | solution.py:130
  26.7 24.9 %collective-permute-start.3 = (bf16[2,2,64,512]{3,2,1,0:T(8,128)(2,1)S(1)}, bf16[2,2,64,512]{3,2,1,0:T(8,128)(2,1)S(1)}, u32[]{:S(2)}, u32[]{:S(2)}) collective-permute-start(bf16[2,2,64,512]{3,2,1,0:T(8,128)(2,1)S(1)} %pad_maximum_fusion.2), channel_id=1, source_target_pairs={{0,320},{64,384},{128,448},{192,0},{256,64},{320,128},{384,192},{4... | collective-permute-start | bytes 786440 | tf_op jit(solution)/shard_map/ppermute | solution.py:130
  53.5 6.9 %copy-start.7 = (s32[64]{0:T(128)S(1)}, s32[64]{0:T(128)}, u32[]{:S(2)}) copy-start(s32[64]{0:T(128)} %param.16) | copy-start | bytes 772
  53.5 9.5 %copy-start.5 = (bf16[2,4,2,256]{3,2,1,0:T(2,128)(2,1)S(1)}, bf16[2,4,2,256]{3,2,1,0:T(2,128)(2,1)}, u32[]{:S(2)}) copy-start(bf16[2,4,2,256]{3,2,1,0:T(2,128)(2,1)} %param.14) | copy-start | bytes 24580
  53.5 9.5 %copy-start.3 = (bf16[128,2,256]{2,1,0:T(2,128)(2,1)S(1)}, bf16[128,2,256]{2,1,0:T(2,128)(2,1)}, u32[]{:S(2)}) copy-start(bf16[128,2,256]{2,1,0:T(2,128)(2,1)} %param.12) | copy-start | bytes 393220
  53.5 9.5 %copy-start.9 = (s32[5]{0:T(128)S(1)}, s32[5]{0:T(128)}, u32[]{:S(2)}) copy-start(s32[5]{0:T(128)} %constant.68) | copy-start | bytes 64
  53.5 9.7 %copy-start.8 = (s32[3]{0:T(128)S(1)}, s32[3]{0:T(128)}, u32[]{:S(2)}) copy-start(s32[3]{0:T(128)} %constant.67) | copy-start | bytes 40
  53.5 9.9 %copy-start.4 = (bf16[256,8]{0,1:T(8,128)(2,1)S(1)}, bf16[256,8]{0,1:T(8,128)(2,1)}, u32[]{:S(2)}) copy-start(bf16[256,8]{0,1:T(8,128)(2,1)} %param.18) | copy-start | bytes 12292
  53.5 46.2 %copy-start.6 = (s32[128,2]{0,1:T(2,128)S(1)}, s32[128,2]{0,1:T(2,128)}, u32[]{:S(2)}) copy-start(s32[128,2]{0,1:T(2,128)} %param.19) | copy-start | bytes 3076
  53.6 1.2 %copy-start.2 = (bf16[8,3,64,512]{3,2,1,0:T(8,128)(2,1)}, bf16[8,3,64,512]{3,2,1,0:T(8,128)(2,1)S(1)}, u32[]{:S(2)}) copy-start(bf16[8,3,64,512]{3,2,1,0:T(8,128)(2,1)S(1)} %all-to-all-done) | copy-start | bytes 4718596
  54.7 48.1 %all-to-all-start.1 = ((bf16[8,5,64,512]{3,2,1,0:T(8,128)(2,1)}), bf16[8,5,64,512]{3,2,1,0:T(8,128)(2,1)S(1)}, u32[]{:S(2)}, u32[]{:S(2)}) async-start(bf16[8,5,64,512]{3,2,1,0:T(8,128)(2,1)} %broadcast_select_fusion), calls=%async_computation.1 | async-start | bytes 5242880 | tf_op jit(solution)/shard_map/all_to_all | solution.py:149
  102.8 1.5 %copy-start.1 = (bf16[8,5,64,512]{3,2,1,0:T(8,128)(2,1)}, bf16[8,5,64,512]{3,2,1,0:T(8,128)(2,1)S(1)}, u32[]{:S(2)}) copy-start(bf16[8,5,64,512]{3,2,1,0:T(8,128)(2,1)S(1)} %all-to-all-done.1) | copy-start | bytes 7864324

commit v6 on v5

--- a/solution.py
+++ b/solution.py
@@ -13,8 +13,8 @@
 CHUNK = 512
 
 
-def attention_kernel(q_ref, pos_ref, *refs, extra_sinks, per_device, part_slots):
-    part_count = len(part_slots)
+def attention_kernel(q_ref, pos_ref, *refs, extra_sinks, per_device, plane_rows):
+    part_count = len(plane_rows)
     window_refs = refs[: 2 * part_count]
     xk_ref, xv_ref, gate_ref, out_ref, score_ref = refs[2 * part_count :]
     rows = q_ref.shape[0]
@@ -40,11 +40,11 @@
 
     chunks = []
     offset = 0
-    for part, slots in enumerate(part_slots):
+    for part, stride in enumerate(plane_rows):
         for c in range(window_refs[2 * part].shape[0] // CHUNK):
             chunks.append((part, c, offset))
             s = scores_of(window_refs[2 * part][pl.ds(c * CHUNK, CHUNK), :])
-            if (c * CHUNK) // (slots * per_device) * per_device < rows:
+            if (c * CHUNK) // stride * per_device < rows:
                 key_pos = pos_ref[:, pl.ds(offset, CHUNK)]
                 s = jnp.where(key_pos > query_pos, s, -jnp.inf)
             score_ref[:, pl.ds(offset, CHUNK)] = s
@@ -68,7 +68,7 @@
     out_ref[:, HEAD_DIM:] = (attended[rows:] * gate[:, 1:2]).astype(out_ref.dtype)
 
 
-def attend(queries, key_pos, parts, part_slots, extra, gate_live, head_count, extra_sinks, per_device):
+def attend(queries, key_pos, parts, plane_rows, extra, gate_live, head_count, extra_sinks, per_device):
     rows = queries.shape[0]
     extra_rows = extra.shape[0]
     window_rows = key_pos.shape[1]
@@ -76,7 +76,7 @@
         attention_kernel,
         extra_sinks=extra_sinks,
         per_device=per_device,
-        part_slots=part_slots,
+        plane_rows=plane_rows,
     )
     window_specs = []
     window_args = []
@@ -129,35 +129,40 @@
         pairs = [(j, (j + shift) % z_count) for j in range(z_count)]
         return lax.ppermute(value, "z", pairs)
 
+    half = per_device // 2
     up = shifted(local, 1)
     down = shifted(local, z_count - 1)
-    near_shifts = (0, 1, z_count - 1)
-    near_slots = [local, up, down]
-    far_up = shifted(jnp.stack([down, local, up]), 3)
-    far_down = shifted(jnp.stack([local, up]), z_count - 3)
-    far_shifts = (2, 3, 4, z_count - 3, z_count - 2)
-    far_slots = [far_up[0], far_up[1], far_up[2], far_down[0], far_down[1]]
-    part_shifts = (near_shifts, far_shifts)
+    far_up = shifted(jnp.concatenate([down, local, up[:, :half]], axis=1), 3)
+    far_down = shifted(jnp.concatenate([local, up, down[:, half:]], axis=1), z_count - 3)
+    near_pieces = ((0, 0, per_device), (1, 0, per_device), (z_count - 1, 0, per_device))
+    far_pieces = (
+        (2, 0, per_device),
+        (3, 0, per_device),
+        (4, 0, half),
+        (z_count - 3, 0, per_device),
+        (z_count - 2, 0, per_device),
+        (4, half, per_device - half),
+    )
+    part_pieces = (near_pieces, far_pieces)
+    part_data = (jnp.concatenate([local, up, down], axis=1), jnp.concatenate([far_up, far_down], axis=1))
     peer_groups = lax.dynamic_slice_in_dim(group_ids, z_me * plane_count, plane_count)
+    plane_ids = jnp.arange(plane_count, dtype=jnp.int32)
     parts = []
     positions = []
-    for shifts, arrived in zip(part_shifts, (near_slots, far_slots)):
-        by_slot = jnp.stack(arrived)
-        outgoing = jnp.where(
-            (peer_groups == 0)[:, None, None, None], by_slot[None, :, 0], by_slot[None, :, 1]
-        )
+    for pieces, data in zip(part_pieces, part_data):
+        outgoing = jnp.where((peer_groups == 0)[:, None, None], data[None, 0], data[None, 1])
         received = lax.all_to_all(
             outgoing, ("ylo", "x"), split_axis=0, concat_axis=0, tiled=True
         )
-        parts.append(received.reshape(plane_count * len(shifts) * per_device, width))
-        z_of_slot = (z_me - jnp.array(shifts, jnp.int32)) % z_count
-        plane_ids = jnp.arange(plane_count, dtype=jnp.int32)
-        row_ids = jnp.arange(per_device, dtype=jnp.int32)
-        part_pos = (
-            (z_of_slot[None, :, None] * plane_count + plane_ids[:, None, None]) * per_device
-            + row_ids[None, None, :]
-        )
-        positions.append(part_pos.reshape(-1))
+        parts.append(received.reshape(plane_count * data.shape[1], width))
+        piece_pos = []
+        for shift, first, count in pieces:
+            z_of = (z_me - shift) % z_count
+            rows_of = first + jnp.arange(count, dtype=jnp.int32)
+            piece_pos.append(
+                (z_of * plane_count + plane_ids[:, None]) * per_device + rows_of[None, :]
+            )
+        positions.append(jnp.concatenate(piece_pos, axis=1).reshape(-1))
 
     sink_rows = lax.dynamic_index_in_dim(sink_kv, my_group, 0, keepdims=False)
     sink_count = sink_rows.shape[0]
@@ -171,9 +176,9 @@
         axis=0,
     )
     key_pos = jnp.concatenate(positions).reshape(1, -1)
-    part_slots = tuple(len(shifts) for shifts in part_shifts)
+    plane_rows = tuple(data.shape[1] for data in part_data)
     return attend(
-        queries, key_pos, parts, part_slots, extra, gate_live, head_count, sink_count, per_device
+        queries, key_pos, parts, plane_rows, extra, gate_live, head_count, sink_count, per_device
     )
 
 

time: 112 us -> 112 us (level)
  the two profiles are of different devices: /device:TPU:142 before, /device:TPU:14 now
where the time goes in v6:
time: 112 us; the launch traced here: 111 us
  blocking collectives  33.6 us (30%)
  starting transfers between devices  33.1 us (30%)
  waiting for transfers between devices  22.8 us (20%)
  Pallas kernels  7.09 us (6%)
  other arithmetic  6.64 us (6%)
  local copies, waits for them, and re-layouts  4.99 us (4%)
  between operations  2.85 us (3%)
    psum x1, blocking collectives, body(): logits = lax.psum(partial_value, 'tp')  33.6 us
    ppermute x4, waiting for transfers between devices, shifted(): return lax.ppermute(value, 'z', pairs)  22.8 us
    ppermute x4, starting transfers between devices, shifted(): return lax.ppermute(value, 'z', pairs)  21.7 us
    all_to_all x2, starting transfers between devices, body(): lax.all_to_all(outgoing, ('ylo', 'x'), split_axis=0, concat_axis=0, tiled...  11.4 us
    pallas_call x1, Pallas kernels, attend(): pl.pallas_call(kernel, grid=(head_count,), in_specs=[pl.BlockSpec((rows,...  7.09 us
    select_n x2, other arithmetic, body(): jnp.where((peer_groups == 0)[:, None, None], data[None, 0], data[None, 1])  3.22 us
    unnamed x22, local copies, waits for them, and re-layouts  2.76 us
  transfers between devices with their start and end apart: 6, of which 4 were waited for; matrix products, arithmetic and copies ran while one was open for 6% of the time, Pallas kernels for 0%

profile of v6, /device:TPU:14, one launch (start us, length us, event | category | flops | bytes accessed | tf_op | source)
XLA Modules:
  0.0 111.2 jit_solution(13781490737846004954)
XLA Ops:
  0.0 0.0 copy-start
  0.0 1.0 reshape.95
  1.0 4.3 %collective-permute-start = (bf16[2,64,512]{2,1,0:T(8,128)(2,1)S(1)}, bf16[2,64,512]{2,1,0:T(8,128)(2,1)S(1)}, u32[]{:S(2)}, u32[]{:S(2)}) collective-permute-start(bf16[2,64,512]{2,1,0:T(8,128)(2,1)S(1)} %reshape.95), channel_id=1, source_target_pairs={{0,64},{64,128},{128,192},{192,256},{256,320},{320,384},{384,448},... | collective-permute-start | bytes 393224 | tf_op jit(solution)/shard_map/ppermute | solution.py:130
  5.3 8.6 %collective-permute-start.1 = (bf16[2,64,512]{2,1,0:T(8,128)(2,1)S(1)}, bf16[2,64,512]{2,1,0:T(8,128)(2,1)S(1)}, u32[]{:S(2)}, u32[]{:S(2)}) collective-permute-start(bf16[2,64,512]{2,1,0:T(8,128)(2,1)S(1)} %reshape.95), channel_id=1, source_target_pairs={{0,448},{64,0},{128,64},{192,128},{256,192},{320,256},{384,320},{4... | collective-permute-start | bytes 393224 | tf_op jit(solution)/shard_map/ppermute | solution.py:130
  13.9 0.7 dynamic-slice_compare_fusion
  14.7 0.8 collective-permute-done
  15.5 1.2 %collective-permute-done.1 = bf16[2,64,512]{2,1,0:T(8,128)(2,1)S(1)} collective-permute-done((bf16[2,64,512]{2,1,0:T(8,128)(2,1)S(1)}, bf16[2,64,512]{2,1,0:T(8,128)(2,1)S(1)}, u32[]{:S(2)}, u32[]{:S(2)}) %collective-permute-start.1) | collective-permute-done | bytes 131104 | tf_op jit(solution)/shard_map/ppermute | solution.py:130
  16.7 1.4 %broadcast_select_fusion.1 = bf16[8,192,512]{2,1,0:T(8,128)(2,1)} fusion(pred[8]{0:T(512)(128)(4,1)S(1)} %dynamic-slice_compare_fusion, bf16[192,512]{1,0:T(8,128)(2,1)S(1)} %get-tuple-element.8, bf16[192,512]{1,0:T(8,128)(2,1)S(1)} %get-tuple-element.7), kind=kLoop, calls=%fused_computation.1 | loop fusion | flops 786432 | bytes 1966088 | tf_op jit(solution)/shard_map/jit(_where)/select_n | solution.py:153
  18.1 5.7 %all-to-all-start = ((bf16[8,192,512]{2,1,0:T(8,128)(2,1)}), bf16[8,192,512]{2,1,0:T(8,128)(2,1)S(1)}, u32[]{:S(2)}, u32[]{:S(2)}) async-start(bf16[8,192,512]{2,1,0:T(8,128)(2,1)} %broadcast_select_fusion.1), calls=%async_computation | async-start | bytes 3145728 | tf_op jit(solution)/shard_map/all_to_all | solution.py:154
  23.8 0.1 pad_maximum_fusion.1
  23.8 5.9 %collective-permute-start.2 = (bf16[2,160,512]{2,1,0:T(8,128)(2,1)S(1)}, bf16[2,160,512]{2,1,0:T(8,128)(2,1)S(1)}, u32[]{:S(2)}, u32[]{:S(2)}) collective-permute-start(bf16[2,160,512]{2,1,0:T(8,128)(2,1)S(1)} %get-tuple-element.10), channel_id=1, source_target_pairs={{0,192},{64,256},{128,320},{192,384},{256,448},{320,0},{384,64},{4... | collective-permute-start | bytes 983048 | tf_op jit(solution)/shard_map/ppermute | solution.py:130
  29.7 3.0 %collective-permute-start.3 = (bf16[2,160,512]{2,1,0:T(8,128)(2,1)S(1)}, bf16[2,160,512]{2,1,0:T(8,128)(2,1)S(1)}, u32[]{:S(2)}, u32[]{:S(2)}) collective-permute-start(bf16[2,160,512]{2,1,0:T(8,128)(2,1)S(1)} %get-tuple-element.9), channel_id=1, source_target_pairs={{0,320},{64,384},{128,448},{192,0},{256,64},{320,128},{384,192},{4... | collective-permute-start | bytes 983048 | tf_op jit(solution)/shard_map/ppermute | solution.py:130
  32.7 16.3 %collective-permute-done.2 = bf16[2,160,512]{2,1,0:T(8,128)(2,1)S(1)} collective-permute-done((bf16[2,160,512]{2,1,0:T(8,128)(2,1)S(1)}, bf16[2,160,512]{2,1,0:T(8,128)(2,1)S(1)}, u32[]{:S(2)}, u32[]{:S(2)}) %collective-permute-start.2) | collective-permute-done | bytes 327712 | tf_op jit(solution)/shard_map/ppermute | solution.py:130
  49.0 4.5 %collective-permute-done.3 = bf16[2,160,512]{2,1,0:T(8,128)(2,1)S(1)} collective-permute-done((bf16[2,160,512]{2,1,0:T(8,128)(2,1)S(1)}, bf16[2,160,512]{2,1,0:T(8,128)(2,1)S(1)}, u32[]{:S(2)}, u32[]{:S(2)}) %collective-permute-start.3) | collective-permute-done | bytes 327712 | tf_op jit(solution)/shard_map/ppermute | solution.py:130
  53.6 1.9 %broadcast_select_fusion = bf16[8,320,512]{2,1,0:T(8,128)(2,1)} fusion(pred[8]{0:T(512)(128)(4,1)S(1)} %dynamic-slice_compare_fusion, bf16[320,512]{1,0:T(8,128)(2,1)S(1)} %get-tuple-element.6, bf16[320,512]{1,0:T(8,128)(2,1)S(1)} %get-tuple-element.5), kind=kLoop, calls=%fused_computation | loop fusion | flops 1310720 | bytes 3276808 | tf_op jit(solution)/shard_map/jit(_where)/select_n | solution.py:153
  55.5 0.0 copy-start.7
  55.5 0.0 copy-start.5
  55.5 0.0 copy-start.3
  55.5 0.0 copy-start.4
  55.5 0.0 copy-start.6
  55.5 0.0 all-to-all-done
  55.5 0.0 copy-start.2
  55.5 1.2 %copy-done.2 = bf16[8,192,512]{2,1,0:T(8,128)(2,1)} copy-done((bf16[8,192,512]{2,1,0:T(8,128)(2,1)}, bf16[8,192,512]{2,1,0:T(8,128)(2,1)S(1)}, u32[]{:S(2)}) %copy-start.2) | copy-done | bytes 1572888
  56.7 5.7 %all-to-all-start.1 = ((bf16[8,320,512]{2,1,0:T(8,128)(2,1)}), bf16[8,320,512]{2,1,0:T(8,128)(2,1)S(1)}, u32[]{:S(2)}, u32[]{:S(2)}) async-start(bf16[8,320,512]{2,1,0:T(8,128)(2,1)} %broadcast_select_fusion), calls=%async_computation.1 | async-start | bytes 5242880 | tf_op jit(solution)/shard_map/all_to_all | solution.py:154
  62.4 0.1 iota_add_fusion.7
  62.5 0.1 iota_add_fusion.5
  62.6 0.1 pad_add_fusion.1
  62.6 0.1 reshape.92
  62.8 0.1 iota_add_fusion
  62.8 0.1 broadcast_add_fusion
  62.9 0.1 iota_add_fusion.3
  63.0 0.1 concatenate.25
  63.1 0.1 reshape.93
  63.1 0.0 copy-done.7
  63.1 0.6 dynamic_slice.11
  65.7 0.0 copy-done.5
  65.7 0.0 copy-done.3
  65.8 0.0 copy-done
  65.8 0.0 copy-done.4
  65.8 0.1 fusion
  65.9 33.6 %psum.7 = f32[128,8]{0,1:T(8,128)S(1)} all-reduce(f32[128,8]{0,1:T(8,128)S(1)} %fusion), channel_id=1, replica_groups=mesh['z'=8,'ylo'=2,'x'=4,'tp'=8] {'tp'}, use_global_device_ids=true, to_apply=%region_0.0 | all-reduce | flops 1024 | bytes 8192 | tf_op jit(solution)/shard_map/psum | solution.py:110
  99.5 0.0 copy-done.6
  99.5 0.1 copy.13
  99.6 0.1 rev.3
  100.4 0.1 pad.2.clone
  100.4 0.6 pad_add_fusion
  101.1 0.7 divide_select_fusion.refs_6_
  101.8 0.8 maximum_maximum_fusion.refs_4_.refs_5_
  102.6 0.0 all-to-all-done.1
  102.6 0.0 copy-start.1
  102.6 1.5 %copy-done.1 = bf16[8,320,512]{2,1,0:T(8,128)(2,1)} copy-done((bf16[8,320,512]{2,1,0:T(8,128)(2,1)}, bf16[8,320,512]{2,1,0:T(8,128)(2,1)S(1)}, u32[]{:S(2)}) %copy-start.1) | copy-done | bytes 2621464
  104.1 7.1 %shard_map.91 = bf16[128,512]{1,0:T(8,128)(2,1)} custom-call(bf16[128,512]{1,0:T(8,128)(2,1)} %q_ref.1, s32[1,4096]{1,0:T(1,128)} %bitcast.28, bf16[1536,512]{1,0:T(8,128)(2,1)} %bitcast.24, bf16[1536,512]{1,0:T(8,128)(2,1)} %bitcast.25, bf16[2560,512]{1,0:T(8,128)(2,1)} %bitcast.22, bf16[2560,512]{1,0:T(8,128)(2,1)} %bitcast.23, ...), custom_call_target="tpu_custom_call" | custom-call | tf_op jit(solution)/shard_map/pallas_call | solution.py:87
  (24 shorter events, 0.3 us)
Async XLA Ops:
  0.0 65.8 %copy-start = (bf16[128,256]{1,0:T(8,128)(2,1)S(1)}, bf16[128,256]{1,0:T(8,128)(2,1)}, u32[]{:S(2)}) copy-start(bf16[128,256]{1,0:T(8,128)(2,1)} %param.15) | copy-start | bytes 196612
  1.0 14.4 %collective-permute-start = (bf16[2,64,512]{2,1,0:T(8,128)(2,1)S(1)}, bf16[2,64,512]{2,1,0:T(8,128)(2,1)S(1)}, u32[]{:S(2)}, u32[]{:S(2)}) collective-permute-start(bf16[2,64,512]{2,1,0:T(8,128)(2,1)S(1)} %reshape.95), channel_id=1, source_target_pairs={{0,64},{64,128},{128,192},{192,256},{256,320},{320,384},{384,448},... | collective-permute-start | bytes 393224 | tf_op jit(solution)/shard_map/ppermute | solution.py:130
  5.3 11.3 %collective-permute-start.1 = (bf16[2,64,512]{2,1,0:T(8,128)(2,1)S(1)}, bf16[2,64,512]{2,1,0:T(8,128)(2,1)S(1)}, u32[]{:S(2)}, u32[]{:S(2)}) collective-permute-start(bf16[2,64,512]{2,1,0:T(8,128)(2,1)S(1)} %reshape.95), channel_id=1, source_target_pairs={{0,448},{64,0},{128,64},{192,128},{256,192},{320,256},{384,320},{4... | collective-permute-start | bytes 393224 | tf_op jit(solution)/shard_map/ppermute | solution.py:130
  18.1 37.4 %all-to-all-start = ((bf16[8,192,512]{2,1,0:T(8,128)(2,1)}), bf16[8,192,512]{2,1,0:T(8,128)(2,1)S(1)}, u32[]{:S(2)}, u32[]{:S(2)}) async-start(bf16[8,192,512]{2,1,0:T(8,128)(2,1)} %broadcast_select_fusion.1), calls=%async_computation | async-start | bytes 3145728 | tf_op jit(solution)/shard_map/all_to_all | solution.py:154
  23.8 25.2 %collective-permute-start.2 = (bf16[2,160,512]{2,1,0:T(8,128)(2,1)S(1)}, bf16[2,160,512]{2,1,0:T(8,128)(2,1)S(1)}, u32[]{:S(2)}, u32[]{:S(2)}) collective-permute-start(bf16[2,160,512]{2,1,0:T(8,128)(2,1)S(1)} %get-tuple-element.10), channel_id=1, source_target_pairs={{0,192},{64,256},{128,320},{192,384},{256,448},{320,0},{384,64},{4... | collective-permute-start | bytes 983048 | tf_op jit(solution)/shard_map/ppermute | solution.py:130
  29.7 23.9 %collective-permute-start.3 = (bf16[2,160,512]{2,1,0:T(8,128)(2,1)S(1)}, bf16[2,160,512]{2,1,0:T(8,128)(2,1)S(1)}, u32[]{:S(2)}, u32[]{:S(2)}) collective-permute-start(bf16[2,160,512]{2,1,0:T(8,128)(2,1)S(1)} %get-tuple-element.9), channel_id=1, source_target_pairs={{0,320},{64,384},{128,448},{192,0},{256,64},{320,128},{384,192},{4... | collective-permute-start | bytes 983048 | tf_op jit(solution)/shard_map/ppermute | solution.py:130
  55.5 7.7 %copy-start.7 = (s32[64]{0:T(128)S(1)}, s32[64]{0:T(128)}, u32[]{:S(2)}) copy-start(s32[64]{0:T(128)} %param.14) | copy-start | bytes 772
  55.5 10.2 %copy-start.5 = (bf16[2,4,2,256]{3,2,1,0:T(2,128)(2,1)S(1)}, bf16[2,4,2,256]{3,2,1,0:T(2,128)(2,1)}, u32[]{:S(2)}) copy-start(bf16[2,4,2,256]{3,2,1,0:T(2,128)(2,1)} %param.12) | copy-start | bytes 24580
  55.5 10.2 %copy-start.3 = (bf16[128,2,256]{2,1,0:T(2,128)(2,1)S(1)}, bf16[128,2,256]{2,1,0:T(2,128)(2,1)}, u32[]{:S(2)}) copy-start(bf16[128,2,256]{2,1,0:T(2,128)(2,1)} %param.10) | copy-start | bytes 393220
  55.5 10.3 %copy-start.4 = (bf16[256,8]{0,1:T(8,128)(2,1)S(1)}, bf16[256,8]{0,1:T(8,128)(2,1)}, u32[]{:S(2)}) copy-start(bf16[256,8]{0,1:T(8,128)(2,1)} %param.16) | copy-start | bytes 12292
  55.5 44.0 %copy-start.6 = (s32[128,2]{0,1:T(2,128)S(1)}, s32[128,2]{0,1:T(2,128)}, u32[]{:S(2)}) copy-start(s32[128,2]{0,1:T(2,128)} %param.17) | copy-start | bytes 3076
  55.5 1.2 %copy-start.2 = (bf16[8,192,512]{2,1,0:T(8,128)(2,1)}, bf16[8,192,512]{2,1,0:T(8,128)(2,1)S(1)}, u32[]{:S(2)}) copy-start(bf16[8,192,512]{2,1,0:T(8,128)(2,1)S(1)} %all-to-all-done) | copy-start | bytes 4718596
  56.7 45.9 %all-to-all-start.1 = ((bf16[8,320,512]{2,1,0:T(8,128)(2,1)}), bf16[8,320,512]{2,1,0:T(8,128)(2,1)S(1)}, u32[]{:S(2)}, u32[]{:S(2)}) async-start(bf16[8,320,512]{2,1,0:T(8,128)(2,1)} %broadcast_select_fusion), calls=%async_computation.1 | async-start | bytes 5242880 | tf_op jit(solution)/shard_map/all_to_all | solution.py:154
  102.6 1.5 %copy-start.1 = (bf16[8,320,512]{2,1,0:T(8,128)(2,1)}, bf16[8,320,512]{2,1,0:T(8,128)(2,1)S(1)}, u32[]{:S(2)}) copy-start(bf16[8,320,512]{2,1,0:T(8,128)(2,1)S(1)} %all-to-all-done.1) | copy-start | bytes 7864324

commit v7 on v6

--- a/solution.py
+++ b/solution.py
@@ -125,6 +125,7 @@
     width = 2 * head_count * HEAD_DIM
     per_device = window_kv.shape[1]
     local = window_kv.reshape(window_kv.shape[0], per_device, width)
+    local, logits = lax.optimization_barrier((local, logits))
     def shifted(value, shift):
         pairs = [(j, (j + shift) % z_count) for j in range(z_count)]
         return lax.ppermute(value, "z", pairs)

time: 112 us -> 116 us (1.036)
  the two profiles are of different devices: /device:TPU:14 before, /device:TPU:16 now
where the time goes in v7:
time: 116 us
  waiting for transfers between devices  46.4 us (40%)
  starting transfers between devices  30.5 us (26%)
  blocking collectives  15.6 us (13%)
  Pallas kernels  7.09 us (6%)
  other arithmetic  6.65 us (6%)
  local copies, waits for them, and re-layouts  5.79 us (5%)
  between operations  2.84 us (2%)
    ppermute x4, waiting for transfers between devices, shifted(): return lax.ppermute(value, 'z', pairs)  24.2 us
    all_to_all x2, waiting for transfers between devices, body(): lax.all_to_all(outgoing, ('ylo', 'x'), split_axis=0, concat_axis=0, tiled...  22.2 us
    ppermute x4, starting transfers between devices, shifted(): return lax.ppermute(value, 'z', pairs)  20 us
    psum x1, blocking collectives, body(): logits = lax.psum(partial_value, 'tp')  15.6 us
    all_to_all x2, starting transfers between devices, body(): lax.all_to_all(outgoing, ('ylo', 'x'), split_axis=0, concat_axis=0, tiled...  10.5 us
    pallas_call x1, Pallas kernels, attend(): pl.pallas_call(kernel, grid=(head_count,), in_specs=[pl.BlockSpec((rows,...  7.09 us
    unnamed x20, local copies, waits for them, and re-layouts  3.59 us
    select_n x2, other arithmetic, body(): jnp.where((peer_groups == 0)[:, None, None], data[None, 0], data[None, 1])  3.22 us
  transfers between devices with their start and end apart: 6, of which 5 were waited for; matrix products, arithmetic and copies ran while one was open for 6% of the time, Pallas kernels for 0%

profile of v7, /device:TPU:16, one launch (start us, length us, event | category | flops | bytes accessed | tf_op | source)
XLA Modules:
  0.0 115.7 jit_solution(1748077336981109645)
XLA Ops:
  0.0 0.0 copy-start
  0.0 0.8 copy-done
  0.8 0.8 fusion
  1.7 15.6 %psum.7 = f32[128,8]{0,1:T(8,128)S(1)} all-reduce(f32[128,8]{0,1:T(8,128)S(1)} %fusion), channel_id=1, replica_groups=mesh['z'=8,'ylo'=2,'x'=4,'tp'=8] {'tp'}, use_global_device_ids=true, to_apply=%region_0.0 | all-reduce | flops 1024 | bytes 8192 | tf_op jit(solution)/shard_map/psum | solution.py:110
  17.2 1.0 reshape.95
  18.2 2.6 %collective-permute-start = (bf16[2,64,512]{2,1,0:T(8,128)(2,1)S(1)}, bf16[2,64,512]{2,1,0:T(8,128)(2,1)S(1)}, u32[]{:S(2)}, u32[]{:S(2)}) collective-permute-start(bf16[2,64,512]{2,1,0:T(8,128)(2,1)S(1)} %reshape.95), channel_id=1, source_target_pairs={{0,64},{64,128},{128,192},{192,256},{256,320},{320,384},{384,448},... | collective-permute-start | bytes 393224 | tf_op jit(solution)/shard_map/ppermute | solution.py:131
  20.8 8.6 %collective-permute-start.1 = (bf16[2,64,512]{2,1,0:T(8,128)(2,1)S(1)}, bf16[2,64,512]{2,1,0:T(8,128)(2,1)S(1)}, u32[]{:S(2)}, u32[]{:S(2)}) collective-permute-start(bf16[2,64,512]{2,1,0:T(8,128)(2,1)S(1)} %reshape.95), channel_id=1, source_target_pairs={{0,448},{64,0},{128,64},{192,128},{256,192},{320,256},{384,320},{4... | collective-permute-start | bytes 393224 | tf_op jit(solution)/shard_map/ppermute | solution.py:131
  29.4 0.7 dynamic-slice_compare_fusion
  30.2 0.8 collective-permute-done
  31.0 1.2 %collective-permute-done.1 = bf16[2,64,512]{2,1,0:T(8,128)(2,1)S(1)} collective-permute-done((bf16[2,64,512]{2,1,0:T(8,128)(2,1)S(1)}, bf16[2,64,512]{2,1,0:T(8,128)(2,1)S(1)}, u32[]{:S(2)}, u32[]{:S(2)}) %collective-permute-start.1) | collective-permute-done | bytes 131104 | tf_op jit(solution)/shard_map/ppermute | solution.py:131
  32.2 1.4 %broadcast_select_fusion.1 = bf16[8,192,512]{2,1,0:T(8,128)(2,1)} fusion(pred[8]{0:T(512)(128)(4,1)S(1)} %dynamic-slice_compare_fusion, bf16[192,512]{1,0:T(8,128)(2,1)S(1)} %get-tuple-element.10, bf16[192,512]{1,0:T(8,128)(2,1)S(1)} %get-tuple-element.9), kind=kLoop, calls=%fused_computation.1 | loop fusion | flops 786432 | bytes 1966088 | tf_op jit(solution)/shard_map/jit(_where)/select_n | solution.py:154
  33.6 5.1 %all-to-all-start = ((bf16[8,192,512]{2,1,0:T(8,128)(2,1)}), bf16[8,192,512]{2,1,0:T(8,128)(2,1)S(1)}, u32[]{:S(2)}, u32[]{:S(2)}) async-start(bf16[8,192,512]{2,1,0:T(8,128)(2,1)} %broadcast_select_fusion.1), calls=%async_computation | async-start | bytes 3145728 | tf_op jit(solution)/shard_map/all_to_all | solution.py:155
  38.7 0.1 pad_maximum_fusion.1
  38.8 5.8 %collective-permute-start.2 = (bf16[2,160,512]{2,1,0:T(8,128)(2,1)S(1)}, bf16[2,160,512]{2,1,0:T(8,128)(2,1)S(1)}, u32[]{:S(2)}, u32[]{:S(2)}) collective-permute-start(bf16[2,160,512]{2,1,0:T(8,128)(2,1)S(1)} %get-tuple-element.12), channel_id=1, source_target_pairs={{0,192},{64,256},{128,320},{192,384},{256,448},{320,0},{384,64},{4... | collective-permute-start | bytes 983048 | tf_op jit(solution)/shard_map/ppermute | solution.py:131
  44.6 3.0 %collective-permute-start.3 = (bf16[2,160,512]{2,1,0:T(8,128)(2,1)S(1)}, bf16[2,160,512]{2,1,0:T(8,128)(2,1)S(1)}, u32[]{:S(2)}, u32[]{:S(2)}) collective-permute-start(bf16[2,160,512]{2,1,0:T(8,128)(2,1)S(1)} %get-tuple-element.11), channel_id=1, source_target_pairs={{0,320},{64,384},{128,448},{192,0},{256,64},{320,128},{384,192},{4... | collective-permute-start | bytes 983048 | tf_op jit(solution)/shard_map/ppermute | solution.py:131
  47.6 15.4 %collective-permute-done.2 = bf16[2,160,512]{2,1,0:T(8,128)(2,1)S(1)} collective-permute-done((bf16[2,160,512]{2,1,0:T(8,128)(2,1)S(1)}, bf16[2,160,512]{2,1,0:T(8,128)(2,1)S(1)}, u32[]{:S(2)}, u32[]{:S(2)}) %collective-permute-start.2) | collective-permute-done | bytes 327712 | tf_op jit(solution)/shard_map/ppermute | solution.py:131
  63.1 6.8 %collective-permute-done.3 = bf16[2,160,512]{2,1,0:T(8,128)(2,1)S(1)} collective-permute-done((bf16[2,160,512]{2,1,0:T(8,128)(2,1)S(1)}, bf16[2,160,512]{2,1,0:T(8,128)(2,1)S(1)}, u32[]{:S(2)}, u32[]{:S(2)}) %collective-permute-start.3) | collective-permute-done | bytes 327712 | tf_op jit(solution)/shard_map/ppermute | solution.py:131
  70.0 1.8 %broadcast_select_fusion = bf16[8,320,512]{2,1,0:T(8,128)(2,1)} fusion(pred[8]{0:T(512)(128)(4,1)S(1)} %dynamic-slice_compare_fusion, bf16[320,512]{1,0:T(8,128)(2,1)S(1)} %get-tuple-element.8, bf16[320,512]{1,0:T(8,128)(2,1)S(1)} %get-tuple-element.7), kind=kLoop, calls=%fused_computation | loop fusion | flops 1310720 | bytes 3276808 | tf_op jit(solution)/shard_map/jit(_where)/select_n | solution.py:154
  71.8 0.0 copy-start.6
  71.8 0.0 copy-start.4
  71.8 0.0 copy-start.3
  71.8 0.0 copy-start.5
  71.8 0.0 all-to-all-done
  71.8 0.0 copy-start.2
  71.8 1.2 %copy-done.2 = bf16[8,192,512]{2,1,0:T(8,128)(2,1)} copy-done((bf16[8,192,512]{2,1,0:T(8,128)(2,1)}, bf16[8,192,512]{2,1,0:T(8,128)(2,1)S(1)}, u32[]{:S(2)}) %copy-start.2) | copy-done | bytes 1572888
  73.0 5.4 %all-to-all-start.1 = ((bf16[8,320,512]{2,1,0:T(8,128)(2,1)}), bf16[8,320,512]{2,1,0:T(8,128)(2,1)S(1)}, u32[]{:S(2)}, u32[]{:S(2)}) async-start(bf16[8,320,512]{2,1,0:T(8,128)(2,1)} %broadcast_select_fusion), calls=%async_computation.1 | async-start | bytes 5242880 | tf_op jit(solution)/shard_map/all_to_all | solution.py:155
  78.5 0.1 iota_add_fusion.7
  78.5 0.1 iota_add_fusion.5
  78.6 0.1 pad_add_fusion.1
  78.7 0.1 reshape.92
  78.8 0.1 iota_add_fusion
  78.9 0.1 broadcast_add_fusion
  79.0 0.1 iota_add_fusion.3
  79.0 0.1 concatenate.25
  79.1 0.1 reshape.93
  79.2 0.0 copy-done.6
  79.2 0.6 dynamic_slice.11
  81.7 0.0 copy-done.4
  81.8 0.0 copy-done.3
  81.8 0.0 copy-done.5
  81.8 0.1 copy.13
  82.0 0.1 rev.3
  82.7 0.1 pad.2.clone
  82.8 0.6 pad_add_fusion
  83.4 0.7 divide_select_fusion.refs_6_
  84.1 0.8 maximum_maximum_fusion.refs_4_.refs_5_
  84.9 22.2 %all-to-all-done.1 = bf16[8,320,512]{2,1,0:T(8,128)(2,1)S(1)} async-done(((bf16[8,320,512]{2,1,0:T(8,128)(2,1)}), bf16[8,320,512]{2,1,0:T(8,128)(2,1)S(1)}, u32[]{:S(2)}, u32[]{:S(2)}) %all-to-all-start.1) | async-done | bytes 2621472 | tf_op jit(solution)/shard_map/all_to_all | solution.py:155
  107.1 0.0 copy-start.1
  107.1 1.5 %copy-done.1 = bf16[8,320,512]{2,1,0:T(8,128)(2,1)} copy-done((bf16[8,320,512]{2,1,0:T(8,128)(2,1)}, bf16[8,320,512]{2,1,0:T(8,128)(2,1)S(1)}, u32[]{:S(2)}) %copy-start.1) | copy-done | bytes 2621464
  108.6 7.1 %shard_map.91 = bf16[128,512]{1,0:T(8,128)(2,1)} custom-call(bf16[128,512]{1,0:T(8,128)(2,1)} %q_ref.1, s32[1,4096]{1,0:T(1,128)} %bitcast.28, bf16[1536,512]{1,0:T(8,128)(2,1)} %bitcast.24, bf16[1536,512]{1,0:T(8,128)(2,1)} %bitcast.25, bf16[2560,512]{1,0:T(8,128)(2,1)} %bitcast.22, bf16[2560,512]{1,0:T(8,128)(2,1)} %bitcast.23, ...), custom_call_target="tpu_custom_call" | custom-call | tf_op jit(solution)/shard_map/pallas_call | solution.py:87
  (24 shorter events, 0.3 us)
Async XLA Ops:
  0.0 0.8 copy-start
  18.2 12.8 %collective-permute-start = (bf16[2,64,512]{2,1,0:T(8,128)(2,1)S(1)}, bf16[2,64,512]{2,1,0:T(8,128)(2,1)S(1)}, u32[]{:S(2)}, u32[]{:S(2)}) collective-permute-start(bf16[2,64,512]{2,1,0:T(8,128)(2,1)S(1)} %reshape.95), channel_id=1, source_target_pairs={{0,64},{64,128},{128,192},{192,256},{256,320},{320,384},{384,448},... | collective-permute-start | bytes 393224 | tf_op jit(solution)/shard_map/ppermute | solution.py:131
  20.8 11.4 %collective-permute-start.1 = (bf16[2,64,512]{2,1,0:T(8,128)(2,1)S(1)}, bf16[2,64,512]{2,1,0:T(8,128)(2,1)S(1)}, u32[]{:S(2)}, u32[]{:S(2)}) collective-permute-start(bf16[2,64,512]{2,1,0:T(8,128)(2,1)S(1)} %reshape.95), channel_id=1, source_target_pairs={{0,448},{64,0},{128,64},{192,128},{256,192},{320,256},{384,320},{4... | collective-permute-start | bytes 393224 | tf_op jit(solution)/shard_map/ppermute | solution.py:131
  33.6 38.2 %all-to-all-start = ((bf16[8,192,512]{2,1,0:T(8,128)(2,1)}), bf16[8,192,512]{2,1,0:T(8,128)(2,1)S(1)}, u32[]{:S(2)}, u32[]{:S(2)}) async-start(bf16[8,192,512]{2,1,0:T(8,128)(2,1)} %broadcast_select_fusion.1), calls=%async_computation | async-start | bytes 3145728 | tf_op jit(solution)/shard_map/all_to_all | solution.py:155
  38.8 24.3 %collective-permute-start.2 = (bf16[2,160,512]{2,1,0:T(8,128)(2,1)S(1)}, bf16[2,160,512]{2,1,0:T(8,128)(2,1)S(1)}, u32[]{:S(2)}, u32[]{:S(2)}) collective-permute-start(bf16[2,160,512]{2,1,0:T(8,128)(2,1)S(1)} %get-tuple-element.12), channel_id=1, source_target_pairs={{0,192},{64,256},{128,320},{192,384},{256,448},{320,0},{384,64},{4... | collective-permute-start | bytes 983048 | tf_op jit(solution)/shard_map/ppermute | solution.py:131
  44.6 25.3 %collective-permute-start.3 = (bf16[2,160,512]{2,1,0:T(8,128)(2,1)S(1)}, bf16[2,160,512]{2,1,0:T(8,128)(2,1)S(1)}, u32[]{:S(2)}, u32[]{:S(2)}) collective-permute-start(bf16[2,160,512]{2,1,0:T(8,128)(2,1)S(1)} %get-tuple-element.11), channel_id=1, source_target_pairs={{0,320},{64,384},{128,448},{192,0},{256,64},{320,128},{384,192},{4... | collective-permute-start | bytes 983048 | tf_op jit(solution)/shard_map/ppermute | solution.py:131
  71.8 7.4 %copy-start.6 = (s32[64]{0:T(128)S(1)}, s32[64]{0:T(128)}, u32[]{:S(2)}) copy-start(s32[64]{0:T(128)} %param.14) | copy-start | bytes 772
  71.8 9.9 %copy-start.4 = (bf16[2,4,2,256]{3,2,1,0:T(2,128)(2,1)S(1)}, bf16[2,4,2,256]{3,2,1,0:T(2,128)(2,1)}, u32[]{:S(2)}) copy-start(bf16[2,4,2,256]{3,2,1,0:T(2,128)(2,1)} %param.12) | copy-start | bytes 24580
  71.8 10.0 %copy-start.3 = (bf16[128,2,256]{2,1,0:T(2,128)(2,1)S(1)}, bf16[128,2,256]{2,1,0:T(2,128)(2,1)}, u32[]{:S(2)}) copy-start(bf16[128,2,256]{2,1,0:T(2,128)(2,1)} %param.10) | copy-start | bytes 393220
  71.8 10.0 %copy-start.5 = (s32[128,2]{0,1:T(2,128)S(1)}, s32[128,2]{0,1:T(2,128)}, u32[]{:S(2)}) copy-start(s32[128,2]{0,1:T(2,128)} %param.17) | copy-start | bytes 3076
  71.8 1.2 %copy-start.2 = (bf16[8,192,512]{2,1,0:T(8,128)(2,1)}, bf16[8,192,512]{2,1,0:T(8,128)(2,1)S(1)}, u32[]{:S(2)}) copy-start(bf16[8,192,512]{2,1,0:T(8,128)(2,1)S(1)} %all-to-all-done) | copy-start | bytes 4718596
  73.0 34.1 %all-to-all-start.1 = ((bf16[8,320,512]{2,1,0:T(8,128)(2,1)}), bf16[8,320,512]{2,1,0:T(8,128)(2,1)S(1)}, u32[]{:S(2)}, u32[]{:S(2)}) async-start(bf16[8,320,512]{2,1,0:T(8,128)(2,1)} %broadcast_select_fusion), calls=%async_computation.1 | async-start | bytes 5242880 | tf_op jit(solution)/shard_map/all_to_all | solution.py:155
  107.1 1.5 %copy-start.1 = (bf16[8,320,512]{2,1,0:T(8,128)(2,1)}, bf16[8,320,512]{2,1,0:T(8,128)(2,1)S(1)}, u32[]{:S(2)}) copy-start(bf16[8,320,512]{2,1,0:T(8,128)(2,1)S(1)} %all-to-all-done.1) | copy-start | bytes 7864324

commit v8 on v6

--- a/solution.py
+++ b/solution.py
@@ -13,55 +13,110 @@
 CHUNK = 512
 
 
-def attention_kernel(q_ref, pos_ref, *refs, extra_sinks, per_device, plane_rows):
-    part_count = len(plane_rows)
-    window_refs = refs[: 2 * part_count]
-    xk_ref, xv_ref, gate_ref, out_ref, score_ref = refs[2 * part_count :]
-    rows = q_ref.shape[0]
-    scale = 1.0 / math.sqrt(HEAD_DIM)
+def stacked_queries(q_ref):
     q = q_ref[...]
-    q_stack = jnp.concatenate([q[:, :HEAD_DIM], q[:, HEAD_DIM:]], axis=0)
+    return jnp.concatenate([q[:, :HEAD_DIM], q[:, HEAD_DIM:]], axis=0)
+
+
+def window_scores(q_stack, pos_ref, wk_ref, score_ref, rows, per_device, stride, scale):
     stacked = q_stack.shape[0]
     query_pos = lax.broadcasted_iota(jnp.int32, (stacked, 1), 0) % rows
     nt = (((1,), (1,)), ((), ()))
-
-    def scores_of(keys):
-        return lax.dot_general(q_stack, keys, nt, preferred_element_type=jnp.float32) * scale
-
+    top = jnp.full((stacked, 1), -jnp.inf, jnp.float32)
+    for c in range(wk_ref.shape[0] // CHUNK):
+        keys = wk_ref[pl.ds(c * CHUNK, CHUNK), :]
+        s = lax.dot_general(q_stack, keys, nt, preferred_element_type=jnp.float32) * scale
+        if (c * CHUNK) // stride * per_device < rows:
+            key_pos = pos_ref[:, pl.ds(c * CHUNK, CHUNK)]
+            s = jnp.where(key_pos > query_pos, s, -jnp.inf)
+        score_ref[:, pl.ds(c * CHUNK, CHUNK)] = s
+        top = jnp.maximum(top, jnp.max(s, axis=1, keepdims=True))
+    return top
+
+
+def window_sums(wv_ref, score_ref, top, total, acc):
+    for c in range(wv_ref.shape[0] // CHUNK):
+        e = jnp.exp(score_ref[:, pl.ds(c * CHUNK, CHUNK)] - top)
+        total = total + jnp.sum(e, axis=1, keepdims=True)
+        acc = acc + jnp.dot(
+            e.astype(jnp.bfloat16),
+            wv_ref[pl.ds(c * CHUNK, CHUNK), :],
+            preferred_element_type=jnp.float32,
+        )
+    return total, acc
+
+
+def first_kernel(
+    q_ref,
+    pos_ref,
+    wk_ref,
+    wv_ref,
+    xk_ref,
+    xv_ref,
+    acc_ref,
+    top_ref,
+    total_ref,
+    score_ref,
+    *,
+    extra_sinks,
+    per_device,
+    stride,
+):
+    rows = q_ref.shape[0]
+    scale = 1.0 / math.sqrt(HEAD_DIM)
+    q_stack = stacked_queries(q_ref)
+    stacked = q_stack.shape[0]
+    nt = (((1,), (1,)), ((), ()))
     extra_rows = xk_ref.shape[0]
-    extra = scores_of(xk_ref[...])
+    extra = (
+        lax.dot_general(q_stack, xk_ref[...], nt, preferred_element_type=jnp.float32) * scale
+    )
     extra_pos = lax.broadcasted_iota(jnp.int32, (stacked, extra_rows), 0) % rows
     extra_key = lax.broadcasted_iota(jnp.int32, (stacked, extra_rows), 1)
     extra_visible = (extra_key <= extra_pos) | (
         (extra_key >= rows) & (extra_key < rows + extra_sinks)
     )
     extra = jnp.where(extra_visible, extra, -jnp.inf)
-    top = jnp.max(extra, axis=1, keepdims=True)
-
-    chunks = []
-    offset = 0
-    for part, stride in enumerate(plane_rows):
-        for c in range(window_refs[2 * part].shape[0] // CHUNK):
-            chunks.append((part, c, offset))
-            s = scores_of(window_refs[2 * part][pl.ds(c * CHUNK, CHUNK), :])
-            if (c * CHUNK) // stride * per_device < rows:
-                key_pos = pos_ref[:, pl.ds(offset, CHUNK)]
-                s = jnp.where(key_pos > query_pos, s, -jnp.inf)
-            score_ref[:, pl.ds(offset, CHUNK)] = s
-            top = jnp.maximum(top, jnp.max(s, axis=1, keepdims=True))
-            offset += CHUNK
-
+    top = jnp.maximum(
+        jnp.max(extra, axis=1, keepdims=True),
+        window_scores(q_stack, pos_ref, wk_ref, score_ref, rows, per_device, stride, scale),
+    )
     e = jnp.exp(extra - top)
     total = jnp.sum(e, axis=1, keepdims=True)
     acc = jnp.dot(e.astype(jnp.bfloat16), xv_ref[...], preferred_element_type=jnp.float32)
-    for part, c, offset in chunks:
-        e = jnp.exp(score_ref[:, pl.ds(offset, CHUNK)] - top)
-        total = total + jnp.sum(e, axis=1, keepdims=True)
-        acc = acc + jnp.dot(
-            e.astype(jnp.bfloat16),
-            window_refs[2 * part + 1][pl.ds(c * CHUNK, CHUNK), :],
-            preferred_element_type=jnp.float32,
-        )
+    total, acc = window_sums(wv_ref, score_ref, top, total, acc)
+    acc_ref[...] = acc
+    top_ref[...] = jnp.broadcast_to(top, top_ref.shape)
+    total_ref[...] = jnp.broadcast_to(total, total_ref.shape)
+
+
+def second_kernel(
+    q_ref,
+    pos_ref,
+    wk_ref,
+    wv_ref,
+    acc_ref,
+    top_ref,
+    total_ref,
+    gate_ref,
+    out_ref,
+    score_ref,
+    *,
+    per_device,
+    stride,
+):
+    rows = q_ref.shape[0]
+    scale = 1.0 / math.sqrt(HEAD_DIM)
+    q_stack = stacked_queries(q_ref)
+    first_top = top_ref[:, 0:1]
+    top = jnp.maximum(
+        first_top,
+        window_scores(q_stack, pos_ref, wk_ref, score_ref, rows, per_device, stride, scale),
+    )
+    factor = jnp.exp(first_top - top)
+    total, acc = window_sums(
+        wv_ref, score_ref, top, total_ref[:, 0:1] * factor, acc_ref[...] * factor
+    )
     attended = acc / total
     gate = gate_ref[...]
     out_ref[:, :HEAD_DIM] = (attended[:rows] * gate[:, 0:1]).astype(out_ref.dtype)
@@ -70,37 +125,57 @@
 
 def attend(queries, key_pos, parts, plane_rows, extra, gate_live, head_count, extra_sinks, per_device):
     rows = queries.shape[0]
+    stacked = PICKS * rows
     extra_rows = extra.shape[0]
-    window_rows = key_pos.shape[1]
-    kernel = functools.partial(
-        attention_kernel,
-        extra_sinks=extra_sinks,
-        per_device=per_device,
-        plane_rows=plane_rows,
-    )
-    window_specs = []
-    window_args = []
-    for part in parts:
-        window_specs.append(pl.BlockSpec((part.shape[0], HEAD_DIM), lambda h: (0, h)))
-        window_specs.append(pl.BlockSpec((part.shape[0], HEAD_DIM), lambda h: (0, head_count + h)))
-        window_args += [part, part]
-    return pl.pallas_call(
-        kernel,
+    first, second = parts
+    first_rows = first.shape[0]
+    second_rows = second.shape[0]
+    first_pos = key_pos[:, :first_rows]
+    second_pos = key_pos[:, first_rows:]
+    q_spec = pl.BlockSpec((rows, PICKS * HEAD_DIM), lambda h: (0, h))
+    state_spec = pl.BlockSpec((None, stacked, HEAD_DIM), lambda h: (h, 0, 0))
+    state_shape = jax.ShapeDtypeStruct((head_count, stacked, HEAD_DIM), jnp.float32)
+
+    def key_spec(part_rows):
+        return pl.BlockSpec((part_rows, HEAD_DIM), lambda h: (0, h))
+
+    def value_spec(part_rows):
+        return pl.BlockSpec((part_rows, HEAD_DIM), lambda h: (0, head_count + h))
+
+    acc, top, total = pl.pallas_call(
+        functools.partial(
+            first_kernel, extra_sinks=extra_sinks, per_device=per_device, stride=plane_rows[0]
+        ),
         grid=(head_count,),
         in_specs=[
-            pl.BlockSpec((rows, PICKS * HEAD_DIM), lambda h: (0, h)),
-            pl.BlockSpec((1, window_rows), lambda h: (0, 0)),
-        ]
-        + window_specs
-        + [
-            pl.BlockSpec((extra_rows, HEAD_DIM), lambda h: (0, h)),
-            pl.BlockSpec((extra_rows, HEAD_DIM), lambda h: (0, head_count + h)),
+            q_spec,
+            pl.BlockSpec((1, first_rows), lambda h: (0, 0)),
+            key_spec(first_rows),
+            value_spec(first_rows),
+            key_spec(extra_rows),
+            value_spec(extra_rows),
+        ],
+        out_specs=[state_spec, state_spec, state_spec],
+        scratch_shapes=[pltpu.VMEM((stacked, first_rows), jnp.float32)],
+        out_shape=[state_shape, state_shape, state_shape],
+    )(queries, first_pos, first, first, extra, extra)
+    return pl.pallas_call(
+        functools.partial(second_kernel, per_device=per_device, stride=plane_rows[1]),
+        grid=(head_count,),
+        in_specs=[
+            q_spec,
+            pl.BlockSpec((1, second_rows), lambda h: (0, 0)),
+            key_spec(second_rows),
+            value_spec(second_rows),
+            state_spec,
+            state_spec,
+            state_spec,
             pl.BlockSpec((rows, PICKS), lambda h: (0, 0)),
         ],
-        out_specs=pl.BlockSpec((rows, PICKS * HEAD_DIM), lambda h: (0, h)),
-        scratch_shapes=[pltpu.VMEM((PICKS * rows, window_rows), jnp.float32)],
+        out_specs=q_spec,
+        scratch_shapes=[pltpu.VMEM((stacked, second_rows), jnp.float32)],
         out_shape=jax.ShapeDtypeStruct((rows, head_count * PICKS * HEAD_DIM), jnp.bfloat16),
-    )(queries, key_pos, *window_args, extra, extra, gate_live)
+    )(queries, second_pos, second, second, acc, top, total, gate_live)
 
 
 def body(queries, suffix_kv, window_kv, sink_kv, lengths, group_ids, hidden_in, router, picks):

time: 112 us -> 116 us (1.036)
  the two profiles are of different devices: /device:TPU:14 before, /device:TPU:142 now
where the time goes in v8:
time: 116 us
  blocking collectives  36.1 us (31%)
  starting transfers between devices  29.1 us (25%)
  waiting for transfers between devices  26 us (22%)
  Pallas kernels  9.22 us (8%)
  local copies, waits for them, and re-layouts  6.19 us (5%)
  other arithmetic  6.08 us (5%)
  between operations  2.82 us (2%)
    psum x1, blocking collectives, body(): logits = lax.psum(partial_value, 'tp')  36.1 us
    ppermute x4, waiting for transfers between devices, shifted(): return lax.ppermute(value, 'z', pairs)  26 us
    ppermute x4, starting transfers between devices, shifted(): return lax.ppermute(value, 'z', pairs)  17.2 us
    all_to_all x2, starting transfers between devices, body(): lax.all_to_all(outgoing, ('ylo', 'x'), split_axis=0, concat_axis=0, tiled...  12 us
    pallas_call x1, Pallas kernels, attend(): pl.pallas_call(functools.partial(second_kernel, per_device=per_device, st...  5.21 us
    pallas_call x1, Pallas kernels, attend(): pl.pallas_call(functools.partial(first_kernel, extra_sinks=extra_sinks, p...  4 us
    select_n x2, other arithmetic, body(): jnp.where((peer_groups == 0)[:, None, None], data[None, 0], data[None, 1])  3.22 us
    unnamed x22, local copies, waits for them, and re-layouts  2.75 us
  transfers between devices with their start and end apart: 6, of which 3 were waited for; matrix products, arithmetic and copies ran while one was open for 6% of the time, Pallas kernels for 3%

profile of v8, /device:TPU:142, one launch (start us, length us, event | category | flops | bytes accessed | tf_op | source)
XLA Modules:
  0.0 115.7 jit_solution(12674699998103118862)
XLA Ops:
  0.0 0.0 copy-start
  0.0 1.0 reshape.95
  1.0 1.9 %collective-permute-start = (bf16[2,64,512]{2,1,0:T(8,128)(2,1)S(1)}, bf16[2,64,512]{2,1,0:T(8,128)(2,1)S(1)}, u32[]{:S(2)}, u32[]{:S(2)}) collective-permute-start(bf16[2,64,512]{2,1,0:T(8,128)(2,1)S(1)} %reshape.95), channel_id=1, source_target_pairs={{0,448},{64,0},{128,64},{192,128},{256,192},{320,256},{384,320},{4... | collective-permute-start | bytes 393224 | tf_op jit(solution)/shard_map/ppermute | solution.py:205
  3.0 4.3 %collective-permute-start.1 = (bf16[2,64,512]{2,1,0:T(8,128)(2,1)S(1)}, bf16[2,64,512]{2,1,0:T(8,128)(2,1)S(1)}, u32[]{:S(2)}, u32[]{:S(2)}) collective-permute-start(bf16[2,64,512]{2,1,0:T(8,128)(2,1)S(1)} %reshape.95), channel_id=1, source_target_pairs={{0,64},{64,128},{128,192},{192,256},{256,320},{320,384},{384,448},... | collective-permute-start | bytes 393224 | tf_op jit(solution)/shard_map/ppermute | solution.py:205
  7.3 0.7 dynamic-slice_compare_fusion
  8.0 2.1 %collective-permute-done.1 = bf16[2,64,512]{2,1,0:T(8,128)(2,1)S(1)} collective-permute-done((bf16[2,64,512]{2,1,0:T(8,128)(2,1)S(1)}, bf16[2,64,512]{2,1,0:T(8,128)(2,1)S(1)}, u32[]{:S(2)}, u32[]{:S(2)}) %collective-permute-start.1) | collective-permute-done | bytes 131104 | tf_op jit(solution)/shard_map/ppermute | solution.py:205
  10.1 0.0 collective-permute-done
  10.2 1.4 %broadcast_select_fusion.1 = bf16[8,192,512]{2,1,0:T(8,128)(2,1)} fusion(pred[8]{0:T(512)(128)(4,1)S(1)} %dynamic-slice_compare_fusion, bf16[192,512]{1,0:T(8,128)(2,1)S(1)} %get-tuple-element.14, bf16[192,512]{1,0:T(8,128)(2,1)S(1)} %get-tuple-element.13), kind=kLoop, calls=%fused_computation.1 | loop fusion | flops 786432 | bytes 1966088 | tf_op jit(solution)/shard_map/jit(_where)/select_n | solution.py:228
  11.5 6.3 %all-to-all-start.1 = ((bf16[8,192,512]{2,1,0:T(8,128)(2,1)}), bf16[8,192,512]{2,1,0:T(8,128)(2,1)S(1)}, u32[]{:S(2)}, u32[]{:S(2)}) async-start(bf16[8,192,512]{2,1,0:T(8,128)(2,1)} %broadcast_select_fusion.1), calls=%async_computation.1 | async-start | bytes 3145728 | tf_op jit(solution)/shard_map/all_to_all | solution.py:229
  17.8 0.1 pad_maximum_fusion.1
  17.9 7.9 %collective-permute-start.2 = (bf16[2,160,512]{2,1,0:T(8,128)(2,1)S(1)}, bf16[2,160,512]{2,1,0:T(8,128)(2,1)S(1)}, u32[]{:S(2)}, u32[]{:S(2)}) collective-permute-start(bf16[2,160,512]{2,1,0:T(8,128)(2,1)S(1)} %get-tuple-element.16), channel_id=1, source_target_pairs={{0,192},{64,256},{128,320},{192,384},{256,448},{320,0},{384,64},{4... | collective-permute-start | bytes 983048 | tf_op jit(solution)/shard_map/ppermute | solution.py:205
  25.8 3.1 %collective-permute-start.3 = (bf16[2,160,512]{2,1,0:T(8,128)(2,1)S(1)}, bf16[2,160,512]{2,1,0:T(8,128)(2,1)S(1)}, u32[]{:S(2)}, u32[]{:S(2)}) collective-permute-start(bf16[2,160,512]{2,1,0:T(8,128)(2,1)S(1)} %get-tuple-element.15), channel_id=1, source_target_pairs={{0,320},{64,384},{128,448},{192,0},{256,64},{320,128},{384,192},{4... | collective-permute-start | bytes 983048 | tf_op jit(solution)/shard_map/ppermute | solution.py:205
  28.9 14.4 %collective-permute-done.2 = bf16[2,160,512]{2,1,0:T(8,128)(2,1)S(1)} collective-permute-done((bf16[2,160,512]{2,1,0:T(8,128)(2,1)S(1)}, bf16[2,160,512]{2,1,0:T(8,128)(2,1)S(1)}, u32[]{:S(2)}, u32[]{:S(2)}) %collective-permute-start.2) | collective-permute-done | bytes 327712 | tf_op jit(solution)/shard_map/ppermute | solution.py:205
  43.3 9.5 %collective-permute-done.3 = bf16[2,160,512]{2,1,0:T(8,128)(2,1)S(1)} collective-permute-done((bf16[2,160,512]{2,1,0:T(8,128)(2,1)S(1)}, bf16[2,160,512]{2,1,0:T(8,128)(2,1)S(1)}, u32[]{:S(2)}, u32[]{:S(2)}) %collective-permute-start.3) | collective-permute-done | bytes 327712 | tf_op jit(solution)/shard_map/ppermute | solution.py:205
  52.9 1.9 %broadcast_select_fusion = bf16[8,320,512]{2,1,0:T(8,128)(2,1)} fusion(pred[8]{0:T(512)(128)(4,1)S(1)} %dynamic-slice_compare_fusion, bf16[320,512]{1,0:T(8,128)(2,1)S(1)} %get-tuple-element.12, bf16[320,512]{1,0:T(8,128)(2,1)S(1)} %get-tuple-element.11), kind=kLoop, calls=%fused_computation | loop fusion | flops 1310720 | bytes 3276808 | tf_op jit(solution)/shard_map/jit(_where)/select_n | solution.py:228
  54.8 0.0 copy-start.7
  54.8 0.0 copy-start.5
  54.8 0.0 copy-start.3
  54.8 0.0 copy-start.4
  54.8 0.0 copy-start.6
  54.8 0.0 all-to-all-done.1
  54.8 0.0 copy-start.2
  54.8 1.2 copy-done.2
  56.0 5.7 %all-to-all-start = ((bf16[8,320,512]{2,1,0:T(8,128)(2,1)}), bf16[8,320,512]{2,1,0:T(8,128)(2,1)S(1)}, u32[]{:S(2)}, u32[]{:S(2)}) async-start(bf16[8,320,512]{2,1,0:T(8,128)(2,1)} %broadcast_select_fusion), calls=%async_computation | async-start | bytes 5242880 | tf_op jit(solution)/shard_map/all_to_all | solution.py:229
  61.7 0.1 iota_add_fusion.3
  61.8 0.1 broadcast_add_fusion
  61.9 0.1 iota_add_fusion
  61.9 0.1 concatenate.25
  62.0 0.1 reshape.93
  62.1 0.1 iota_add_fusion.7
  62.2 0.1 iota_add_fusion.5
  62.3 0.1 pad_add_fusion.1
  62.3 0.1 reshape.92
  62.4 0.6 slice.32.pos_ref
  63.0 0.6 slice.37.pos_ref
  63.6 0.0 copy-done.7
  63.6 0.6 dynamic_slice.11
  66.1 0.0 copy-done.5
  66.2 0.0 copy-done.3
  66.2 0.0 copy-done
  66.2 0.0 copy-done.4
  66.2 0.1 fusion
  66.3 36.1 %psum.7 = f32[128,8]{0,1:T(8,128)S(1)} all-reduce(f32[128,8]{0,1:T(8,128)S(1)} %fusion), channel_id=1, replica_groups=mesh['z'=8,'ylo'=2,'x'=4,'tp'=8] {'tp'}, use_global_device_ids=true, to_apply=%region_0.0 | all-reduce | flops 1024 | bytes 8192 | tf_op jit(solution)/shard_map/psum | solution.py:185
  102.4 0.0 copy-done.6
  102.4 0.1 copy.13
  102.5 0.1 rev.3
  103.3 0.1 pad.2.clone
  103.4 0.7 divide_select_fusion.gate_ref
  104.1 0.8 maximum_maximum_fusion.xk_ref.xv_ref
  104.9 4.0 %shard_map.91 = (f32[2,256,128]{2,1,0:T(8,128)}, f32[2,256,128]{2,1,0:T(8,128)}, f32[2,256,128]{2,1,0:T(8,128)}) custom-call(bf16[128,512]{1,0:T(8,128)(2,1)} %q_ref.3, s32[1,1536]{1,0:T(1,128)} %slice.37.pos_ref, bf16[1536,512]{1,0:T(8,128)(2,1)} %bitcast.24, bf16[1536,512]{1,0:T(8,128)(2,1)} %bitcast.25, ...), custom_call_target="tpu_custom_call" | custom-call | tf_op jit(solution)/shard_map/pallas_call | solution.py:145
  108.9 0.0 all-to-all-done
  108.9 0.0 copy-start.1
  108.9 1.5 %copy-done.1 = bf16[8,320,512]{2,1,0:T(8,128)(2,1)} copy-done((bf16[8,320,512]{2,1,0:T(8,128)(2,1)}, bf16[8,320,512]{2,1,0:T(8,128)(2,1)S(1)}, u32[]{:S(2)}) %copy-start.1) | copy-done | bytes 2621464
  110.4 5.2 %shard_map.92 = bf16[128,512]{1,0:T(8,128)(2,1)} custom-call(bf16[128,512]{1,0:T(8,128)(2,1)} %q_ref.3, s32[1,2560]{1,0:T(1,128)} %slice.32.pos_ref, bf16[2560,512]{1,0:T(8,128)(2,1)} %bitcast.22, bf16[2560,512]{1,0:T(8,128)(2,1)} %bitcast.23, f32[2,256,128]{2,1,0:T(8,128)} %get-tuple-element.8.acc_ref, f32[2,256,128]{2,1,0:T(8,128)} %get-tuple-element.9.top_ref, ...), custom_call_target="tpu_custom_call" | custom-call | tf_op jit(solution)/shard_map/pallas_call | solution.py:162
  (25 shorter events, 0.3 us)
Async XLA Ops:
  0.0 66.2 %copy-start = (bf16[128,256]{1,0:T(8,128)(2,1)S(1)}, bf16[128,256]{1,0:T(8,128)(2,1)}, u32[]{:S(2)}) copy-start(bf16[128,256]{1,0:T(8,128)(2,1)} %param.15) | copy-start | bytes 196612
  1.0 9.1 %collective-permute-start = (bf16[2,64,512]{2,1,0:T(8,128)(2,1)S(1)}, bf16[2,64,512]{2,1,0:T(8,128)(2,1)S(1)}, u32[]{:S(2)}, u32[]{:S(2)}) collective-permute-start(bf16[2,64,512]{2,1,0:T(8,128)(2,1)S(1)} %reshape.95), channel_id=1, source_target_pairs={{0,448},{64,0},{128,64},{192,128},{256,192},{320,256},{384,320},{4... | collective-permute-start | bytes 393224 | tf_op jit(solution)/shard_map/ppermute | solution.py:205
  3.0 7.1 %collective-permute-start.1 = (bf16[2,64,512]{2,1,0:T(8,128)(2,1)S(1)}, bf16[2,64,512]{2,1,0:T(8,128)(2,1)S(1)}, u32[]{:S(2)}, u32[]{:S(2)}) collective-permute-start(bf16[2,64,512]{2,1,0:T(8,128)(2,1)S(1)} %reshape.95), channel_id=1, source_target_pairs={{0,64},{64,128},{128,192},{192,256},{256,320},{320,384},{384,448},... | collective-permute-start | bytes 393224 | tf_op jit(solution)/shard_map/ppermute | solution.py:205
  11.5 43.2 %all-to-all-start.1 = ((bf16[8,192,512]{2,1,0:T(8,128)(2,1)}), bf16[8,192,512]{2,1,0:T(8,128)(2,1)S(1)}, u32[]{:S(2)}, u32[]{:S(2)}) async-start(bf16[8,192,512]{2,1,0:T(8,128)(2,1)} %broadcast_select_fusion.1), calls=%async_computation.1 | async-start | bytes 3145728 | tf_op jit(solution)/shard_map/all_to_all | solution.py:229
  17.9 25.4 %collective-permute-start.2 = (bf16[2,160,512]{2,1,0:T(8,128)(2,1)S(1)}, bf16[2,160,512]{2,1,0:T(8,128)(2,1)S(1)}, u32[]{:S(2)}, u32[]{:S(2)}) collective-permute-start(bf16[2,160,512]{2,1,0:T(8,128)(2,1)S(1)} %get-tuple-element.16), channel_id=1, source_target_pairs={{0,192},{64,256},{128,320},{192,384},{256,448},{320,0},{384,64},{4... | collective-permute-start | bytes 983048 | tf_op jit(solution)/shard_map/ppermute | solution.py:205
  25.8 27.0 %collective-permute-start.3 = (bf16[2,160,512]{2,1,0:T(8,128)(2,1)S(1)}, bf16[2,160,512]{2,1,0:T(8,128)(2,1)S(1)}, u32[]{:S(2)}, u32[]{:S(2)}) collective-permute-start(bf16[2,160,512]{2,1,0:T(8,128)(2,1)S(1)} %get-tuple-element.15), channel_id=1, source_target_pairs={{0,320},{64,384},{128,448},{192,0},{256,64},{320,128},{384,192},{4... | collective-permute-start | bytes 983048 | tf_op jit(solution)/shard_map/ppermute | solution.py:205
  54.8 8.9 %copy-start.7 = (s32[64]{0:T(128)S(1)}, s32[64]{0:T(128)}, u32[]{:S(2)}) copy-start(s32[64]{0:T(128)} %param.14) | copy-start | bytes 772
  54.8 11.4 %copy-start.5 = (bf16[2,4,2,256]{3,2,1,0:T(2,128)(2,1)S(1)}, bf16[2,4,2,256]{3,2,1,0:T(2,128)(2,1)}, u32[]{:S(2)}) copy-start(bf16[2,4,2,256]{3,2,1,0:T(2,128)(2,1)} %param.12) | copy-start | bytes 24580
  54.8 11.4 %copy-start.3 = (bf16[128,2,256]{2,1,0:T(2,128)(2,1)S(1)}, bf16[128,2,256]{2,1,0:T(2,128)(2,1)}, u32[]{:S(2)}) copy-start(bf16[128,2,256]{2,1,0:T(2,128)(2,1)} %param.10) | copy-start | bytes 393220
  54.8 11.4 %copy-start.4 = (bf16[256,8]{0,1:T(8,128)(2,1)S(1)}, bf16[256,8]{0,1:T(8,128)(2,1)}, u32[]{:S(2)}) copy-start(bf16[256,8]{0,1:T(8,128)(2,1)} %param.16) | copy-start | bytes 12292
  54.8 47.6 %copy-start.6 = (s32[128,2]{0,1:T(2,128)S(1)}, s32[128,2]{0,1:T(2,128)}, u32[]{:S(2)}) copy-start(s32[128,2]{0,1:T(2,128)} %param.17) | copy-start | bytes 3076
  54.8 1.2 %copy-start.2 = (bf16[8,192,512]{2,1,0:T(8,128)(2,1)}, bf16[8,192,512]{2,1,0:T(8,128)(2,1)S(1)}, u32[]{:S(2)}) copy-start(bf16[8,192,512]{2,1,0:T(8,128)(2,1)S(1)} %all-to-all-done.1) | copy-start | bytes 4718596
  56.0 53.0 %all-to-all-start = ((bf16[8,320,512]{2,1,0:T(8,128)(2,1)}), bf16[8,320,512]{2,1,0:T(8,128)(2,1)S(1)}, u32[]{:S(2)}, u32[]{:S(2)}) async-start(bf16[8,320,512]{2,1,0:T(8,128)(2,1)} %broadcast_select_fusion), calls=%async_computation | async-start | bytes 5242880 | tf_op jit(solution)/shard_map/all_to_all | solution.py:229
  108.9 1.5 %copy-start.1 = (bf16[8,320,512]{2,1,0:T(8,128)(2,1)}, bf16[8,320,512]{2,1,0:T(8,128)(2,1)S(1)}, u32[]{:S(2)}) copy-start(bf16[8,320,512]{2,1,0:T(8,128)(2,1)S(1)} %all-to-all-done) | copy-start | bytes 7864324

commit v9 on v8

--- a/solution.py
+++ b/solution.py
@@ -123,7 +123,7 @@
     out_ref[:, HEAD_DIM:] = (attended[rows:] * gate[:, 1:2]).astype(out_ref.dtype)
 
 
-def attend(queries, key_pos, parts, plane_rows, extra, gate_live, head_count, extra_sinks, per_device):
+def attend_first(queries, key_pos, parts, plane_rows, extra, head_count, extra_sinks, per_device):
     rows = queries.shape[0]
     stacked = PICKS * rows
     extra_rows = extra.shape[0]
@@ -159,6 +159,26 @@
         scratch_shapes=[pltpu.VMEM((stacked, first_rows), jnp.float32)],
         out_shape=[state_shape, state_shape, state_shape],
     )(queries, first_pos, first, first, extra, extra)
+    return acc, top, total
+
+
+def attend_second(queries, key_pos, parts, plane_rows, state, gate_live, head_count, per_device):
+    rows = queries.shape[0]
+    stacked = PICKS * rows
+    first, second = parts
+    first_rows = first.shape[0]
+    second_rows = second.shape[0]
+    second_pos = key_pos[:, first_rows:]
+    acc, top, total = state
+    q_spec = pl.BlockSpec((rows, PICKS * HEAD_DIM), lambda h: (0, h))
+    state_spec = pl.BlockSpec((None, stacked, HEAD_DIM), lambda h: (h, 0, 0))
+
+    def key_spec(part_rows):
+        return pl.BlockSpec((part_rows, HEAD_DIM), lambda h: (0, h))
+
+    def value_spec(part_rows):
+        return pl.BlockSpec((part_rows, HEAD_DIM), lambda h: (0, head_count + h))
+
     return pl.pallas_call(
         functools.partial(second_kernel, per_device=per_device, stride=plane_rows[1]),
         grid=(head_count,),
@@ -182,20 +202,11 @@
     row_count = queries.shape[0]
     head_count = suffix_kv.shape[2] // HEAD_DIM
     partial_value = jnp.dot(hidden_in, router, preferred_element_type=jnp.float32)
-    logits = lax.psum(partial_value, "tp")
-    experts = jnp.arange(logits.shape[1], dtype=jnp.int32)
-    chosen = jnp.sum(
-        jnp.where(picks[:, :, None] == experts[None, None, :], logits[:, None, :], 0.0), axis=2
-    )
-    gate_values = jax.nn.sigmoid(chosen - chosen[:, ::-1])
     z_count = lax.axis_size("z")
     plane_count = lax.axis_size("ylo") * lax.axis_size("x")
     z_me = lax.axis_index("z")
     plane_me = lax.axis_index("ylo") * lax.axis_size("x") + lax.axis_index("x")
     my_group = group_ids[z_me * plane_count + plane_me]
-    length = lengths[0]
-    is_live = jnp.arange(row_count, dtype=jnp.int32) < length
-    gate_live = jnp.where(is_live[:, None], gate_values, 0.0)
 
     width = 2 * head_count * HEAD_DIM
     per_device = window_kv.shape[1]
@@ -252,8 +263,18 @@
     )
     key_pos = jnp.concatenate(positions).reshape(1, -1)
     plane_rows = tuple(data.shape[1] for data in part_data)
-    return attend(
-        queries, key_pos, parts, plane_rows, extra, gate_live, head_count, sink_count, per_device
+    state = attend_first(queries, key_pos, parts, plane_rows, extra, head_count, sink_count, per_device)
+    state, partial_value = lax.optimization_barrier((state, partial_value))
+    logits = lax.psum(partial_value, "tp")
+    experts = jnp.arange(logits.shape[1], dtype=jnp.int32)
+    chosen = jnp.sum(
+        jnp.where(picks[:, :, None] == experts[None, None, :], logits[:, None, :], 0.0), axis=2
+    )
+    gate_values = jax.nn.sigmoid(chosen - chosen[:, ::-1])
+    is_live = jnp.arange(row_count, dtype=jnp.int32) < lengths[0]
+    gate_live = jnp.where(is_live[:, None], gate_values, 0.0)
+    return attend_second(
+        queries, key_pos, parts, plane_rows, state, gate_live, head_count, per_device
     )
 
 

time: 116 us -> 110 us (0.948)
  blocking collectives: 36.1 us -> 30.4 us
    psum x1, blocking collectives: 36.1 us -> 30.4 us  [body(): logits = lax.psum(partial_value, 'tp')]
  transfers between devices with their start and end apart: 6 -> 6, of which waited for: 3 -> 3; matrix products, arithmetic and copies ran while one was open for 6% -> 7% of each run, Pallas kernels for 3% -> 4%
where the time goes in v9:
time: 110 us
  blocking collectives  30.4 us (28%)
  starting transfers between devices  29.1 us (26%)
  waiting for transfers between devices  26 us (24%)
  Pallas kernels  9.23 us (8%)
  local copies, waits for them, and re-layouts  6.2 us (6%)
  other arithmetic  6.08 us (6%)
  between operations  2.77 us (3%)
    psum x1, blocking collectives, body(): logits = lax.psum(partial_value, 'tp')  30.4 us
    ppermute x4, waiting for transfers between devices, shifted(): return lax.ppermute(value, 'z', pairs)  26 us
    ppermute x4, starting transfers between devices, shifted(): return lax.ppermute(value, 'z', pairs)  17.2 us
    all_to_all x2, starting transfers between devices, body(): lax.all_to_all(outgoing, ('ylo', 'x'), split_axis=0, concat_axis=0, tiled...  12 us
    pallas_call x1, Pallas kernels, attend_second(): pl.pallas_call(functools.partial(second_kernel, per_device=per_device, st...  5.21 us
    pallas_call x1, Pallas kernels, attend_first(): pl.pallas_call(functools.partial(first_kernel, extra_sinks=extra_sinks, p...  4.01 us
    select_n x2, other arithmetic, body(): jnp.where((peer_groups == 0)[:, None, None], data[None, 0], data[None, 1])  3.22 us
    unnamed x22, local copies, waits for them, and re-layouts  2.76 us
  transfers between devices with their start and end apart: 6, of which 3 were waited for; matrix products, arithmetic and copies ran while one was open for 7% of the time, Pallas kernels for 4%

profile of v9, /device:TPU:142, one launch (start us, length us, event | category | flops | bytes accessed | tf_op | source)
XLA Modules:
  0.0 110.0 jit_solution(14535824039550500739)
XLA Ops:
  0.0 0.0 copy-start
  0.0 1.0 reshape.95
  1.0 1.9 %collective-permute-start = (bf16[2,64,512]{2,1,0:T(8,128)(2,1)S(1)}, bf16[2,64,512]{2,1,0:T(8,128)(2,1)S(1)}, u32[]{:S(2)}, u32[]{:S(2)}) collective-permute-start(bf16[2,64,512]{2,1,0:T(8,128)(2,1)S(1)} %reshape.95), channel_id=1, source_target_pairs={{0,448},{64,0},{128,64},{192,128},{256,192},{320,256},{384,320},{4... | collective-permute-start | bytes 393224 | tf_op jit(solution)/shard_map/ppermute | solution.py:216
  3.0 4.3 %collective-permute-start.1 = (bf16[2,64,512]{2,1,0:T(8,128)(2,1)S(1)}, bf16[2,64,512]{2,1,0:T(8,128)(2,1)S(1)}, u32[]{:S(2)}, u32[]{:S(2)}) collective-permute-start(bf16[2,64,512]{2,1,0:T(8,128)(2,1)S(1)} %reshape.95), channel_id=1, source_target_pairs={{0,64},{64,128},{128,192},{192,256},{256,320},{320,384},{384,448},... | collective-permute-start | bytes 393224 | tf_op jit(solution)/shard_map/ppermute | solution.py:216
  7.3 0.7 dynamic-slice_compare_fusion
  8.0 2.1 %collective-permute-done.1 = bf16[2,64,512]{2,1,0:T(8,128)(2,1)S(1)} collective-permute-done((bf16[2,64,512]{2,1,0:T(8,128)(2,1)S(1)}, bf16[2,64,512]{2,1,0:T(8,128)(2,1)S(1)}, u32[]{:S(2)}, u32[]{:S(2)}) %collective-permute-start.1) | collective-permute-done | bytes 131104 | tf_op jit(solution)/shard_map/ppermute | solution.py:216
  10.1 0.0 collective-permute-done
  10.2 1.4 %broadcast_select_fusion.1 = bf16[8,192,512]{2,1,0:T(8,128)(2,1)} fusion(pred[8]{0:T(512)(128)(4,1)S(1)} %dynamic-slice_compare_fusion, bf16[192,512]{1,0:T(8,128)(2,1)S(1)} %get-tuple-element.22, bf16[192,512]{1,0:T(8,128)(2,1)S(1)} %get-tuple-element.21), kind=kLoop, calls=%fused_computation.1 | loop fusion | flops 786432 | bytes 1966088 | tf_op jit(solution)/shard_map/jit(_where)/select_n | solution.py:239
  11.5 6.3 %all-to-all-start.1 = ((bf16[8,192,512]{2,1,0:T(8,128)(2,1)}), bf16[8,192,512]{2,1,0:T(8,128)(2,1)S(1)}, u32[]{:S(2)}, u32[]{:S(2)}) async-start(bf16[8,192,512]{2,1,0:T(8,128)(2,1)} %broadcast_select_fusion.1), calls=%async_computation.1 | async-start | bytes 3145728 | tf_op jit(solution)/shard_map/all_to_all | solution.py:240
  17.8 0.1 pad_maximum_fusion.1
  17.9 7.9 %collective-permute-start.2 = (bf16[2,160,512]{2,1,0:T(8,128)(2,1)S(1)}, bf16[2,160,512]{2,1,0:T(8,128)(2,1)S(1)}, u32[]{:S(2)}, u32[]{:S(2)}) collective-permute-start(bf16[2,160,512]{2,1,0:T(8,128)(2,1)S(1)} %get-tuple-element.24), channel_id=1, source_target_pairs={{0,192},{64,256},{128,320},{192,384},{256,448},{320,0},{384,64},{4... | collective-permute-start | bytes 983048 | tf_op jit(solution)/shard_map/ppermute | solution.py:216
  25.8 3.1 %collective-permute-start.3 = (bf16[2,160,512]{2,1,0:T(8,128)(2,1)S(1)}, bf16[2,160,512]{2,1,0:T(8,128)(2,1)S(1)}, u32[]{:S(2)}, u32[]{:S(2)}) collective-permute-start(bf16[2,160,512]{2,1,0:T(8,128)(2,1)S(1)} %get-tuple-element.23), channel_id=1, source_target_pairs={{0,320},{64,384},{128,448},{192,0},{256,64},{320,128},{384,192},{4... | collective-permute-start | bytes 983048 | tf_op jit(solution)/shard_map/ppermute | solution.py:216
  28.9 14.4 %collective-permute-done.2 = bf16[2,160,512]{2,1,0:T(8,128)(2,1)S(1)} collective-permute-done((bf16[2,160,512]{2,1,0:T(8,128)(2,1)S(1)}, bf16[2,160,512]{2,1,0:T(8,128)(2,1)S(1)}, u32[]{:S(2)}, u32[]{:S(2)}) %collective-permute-start.2) | collective-permute-done | bytes 327712 | tf_op jit(solution)/shard_map/ppermute | solution.py:216
  43.3 9.5 %collective-permute-done.3 = bf16[2,160,512]{2,1,0:T(8,128)(2,1)S(1)} collective-permute-done((bf16[2,160,512]{2,1,0:T(8,128)(2,1)S(1)}, bf16[2,160,512]{2,1,0:T(8,128)(2,1)S(1)}, u32[]{:S(2)}, u32[]{:S(2)}) %collective-permute-start.3) | collective-permute-done | bytes 327712 | tf_op jit(solution)/shard_map/ppermute | solution.py:216
  52.9 1.9 %broadcast_select_fusion = bf16[8,320,512]{2,1,0:T(8,128)(2,1)} fusion(pred[8]{0:T(512)(128)(4,1)S(1)} %dynamic-slice_compare_fusion, bf16[320,512]{1,0:T(8,128)(2,1)S(1)} %get-tuple-element.20, bf16[320,512]{1,0:T(8,128)(2,1)S(1)} %get-tuple-element.19), kind=kLoop, calls=%fused_computation | loop fusion | flops 1310720 | bytes 3276808 | tf_op jit(solution)/shard_map/jit(_where)/select_n | solution.py:239
  54.8 0.0 copy-start.7
  54.8 0.0 copy-start.5
  54.8 0.0 copy-start.3
  54.8 0.0 copy-start.4
  54.8 0.0 all-to-all-done.1
  54.8 0.0 copy-start.2
  54.8 1.2 %copy-done.2 = bf16[8,192,512]{2,1,0:T(8,128)(2,1)} copy-done((bf16[8,192,512]{2,1,0:T(8,128)(2,1)}, bf16[8,192,512]{2,1,0:T(8,128)(2,1)S(1)}, u32[]{:S(2)}) %copy-start.2) | copy-done | bytes 1572888
  55.9 5.7 %all-to-all-start = ((bf16[8,320,512]{2,1,0:T(8,128)(2,1)}), bf16[8,320,512]{2,1,0:T(8,128)(2,1)S(1)}, u32[]{:S(2)}, u32[]{:S(2)}) async-start(bf16[8,320,512]{2,1,0:T(8,128)(2,1)} %broadcast_select_fusion), calls=%async_computation | async-start | bytes 5242880 | tf_op jit(solution)/shard_map/all_to_all | solution.py:240
  61.7 0.1 iota_add_fusion.3
  61.8 0.1 broadcast_add_fusion
  61.9 0.1 iota_add_fusion
  61.9 0.1 concatenate.25
  62.0 0.1 reshape.93
  62.1 0.1 iota_add_fusion.7
  62.2 0.1 iota_add_fusion.5
  62.3 0.1 pad_add_fusion.1
  62.3 0.1 reshape.92
  62.4 0.6 slice.32.pos_ref
  63.0 0.6 slice.37.pos_ref
  63.6 0.0 copy-done.7
  63.6 0.6 dynamic_slice.11
  66.1 0.0 copy-done.5
  66.1 0.0 copy-done.3
  66.8 0.1 pad.2.clone
  66.9 0.0 copy-done
  66.9 0.0 copy-done.4
  66.9 0.1 fusion
  67.1 0.8 maximum_maximum_fusion.xk_ref.xv_ref
  67.9 0.0 copy-start.6
  67.9 4.0 %shard_map.91 = (f32[2,256,128]{2,1,0:T(8,128)}, f32[2,256,128]{2,1,0:T(8,128)}, f32[2,256,128]{2,1,0:T(8,128)}) custom-call(bf16[128,512]{1,0:T(8,128)(2,1)} %q_ref.3, s32[1,1536]{1,0:T(1,128)} %slice.37.pos_ref, bf16[1536,512]{1,0:T(8,128)(2,1)} %bitcast.24, bf16[1536,512]{1,0:T(8,128)(2,1)} %bitcast.25, ...), custom_call_target="tpu_custom_call" | custom-call | tf_op jit(solution)/shard_map/pallas_call | solution.py:145
  71.9 30.4 %psum.7 = f32[128,8]{0,1:T(8,128)S(1)} all-reduce(f32[128,8]{0,1:T(8,128)S(1)} %fusion), channel_id=1, replica_groups=mesh['z'=8,'ylo'=2,'x'=4,'tp'=8] {'tp'}, use_global_device_ids=true, to_apply=%region_0.1 | all-reduce | flops 1024 | bytes 8192 | tf_op jit(solution)/shard_map/psum | solution.py:268
  102.4 0.0 copy-done.6
  102.4 0.1 copy.13
  102.5 0.1 rev.3
  102.6 0.7 divide_select_fusion.gate_ref
  103.3 0.0 all-to-all-done
  103.3 0.0 copy-start.1
  103.3 1.5 %copy-done.1 = bf16[8,320,512]{2,1,0:T(8,128)(2,1)} copy-done((bf16[8,320,512]{2,1,0:T(8,128)(2,1)}, bf16[8,320,512]{2,1,0:T(8,128)(2,1)S(1)}, u32[]{:S(2)}) %copy-start.1) | copy-done | bytes 2621464
  104.8 5.2 %shard_map.92 = bf16[128,512]{1,0:T(8,128)(2,1)} custom-call(bf16[128,512]{1,0:T(8,128)(2,1)} %q_ref.3, s32[1,2560]{1,0:T(1,128)} %slice.32.pos_ref, bf16[2560,512]{1,0:T(8,128)(2,1)} %bitcast.22, bf16[2560,512]{1,0:T(8,128)(2,1)} %bitcast.23, f32[2,256,128]{2,1,0:T(8,128)} %get-tuple-element.15.acc_ref, f32[2,256,128]{2,1,0:T(8,128)} %get-tuple-element.16.top_ref, ...), custom_call_target="tpu_custom_call" | custom-call | tf_op jit(solution)/shard_map/pallas_call | solution.py:182
  (25 shorter events, 0.3 us)
Async XLA Ops:
  0.0 66.9 %copy-start = (bf16[128,256]{1,0:T(8,128)(2,1)S(1)}, bf16[128,256]{1,0:T(8,128)(2,1)}, u32[]{:S(2)}) copy-start(bf16[128,256]{1,0:T(8,128)(2,1)} %param.15) | copy-start | bytes 196612
  1.0 9.1 %collective-permute-start = (bf16[2,64,512]{2,1,0:T(8,128)(2,1)S(1)}, bf16[2,64,512]{2,1,0:T(8,128)(2,1)S(1)}, u32[]{:S(2)}, u32[]{:S(2)}) collective-permute-start(bf16[2,64,512]{2,1,0:T(8,128)(2,1)S(1)} %reshape.95), channel_id=1, source_target_pairs={{0,448},{64,0},{128,64},{192,128},{256,192},{320,256},{384,320},{4... | collective-permute-start | bytes 393224 | tf_op jit(solution)/shard_map/ppermute | solution.py:216
  3.0 7.1 %collective-permute-start.1 = (bf16[2,64,512]{2,1,0:T(8,128)(2,1)S(1)}, bf16[2,64,512]{2,1,0:T(8,128)(2,1)S(1)}, u32[]{:S(2)}, u32[]{:S(2)}) collective-permute-start(bf16[2,64,512]{2,1,0:T(8,128)(2,1)S(1)} %reshape.95), channel_id=1, source_target_pairs={{0,64},{64,128},{128,192},{192,256},{256,320},{320,384},{384,448},... | collective-permute-start | bytes 393224 | tf_op jit(solution)/shard_map/ppermute | solution.py:216
  11.5 43.2 %all-to-all-start.1 = ((bf16[8,192,512]{2,1,0:T(8,128)(2,1)}), bf16[8,192,512]{2,1,0:T(8,128)(2,1)S(1)}, u32[]{:S(2)}, u32[]{:S(2)}) async-start(bf16[8,192,512]{2,1,0:T(8,128)(2,1)} %broadcast_select_fusion.1), calls=%async_computation.1 | async-start | bytes 3145728 | tf_op jit(solution)/shard_map/all_to_all | solution.py:240
  17.9 25.4 %collective-permute-start.2 = (bf16[2,160,512]{2,1,0:T(8,128)(2,1)S(1)}, bf16[2,160,512]{2,1,0:T(8,128)(2,1)S(1)}, u32[]{:S(2)}, u32[]{:S(2)}) collective-permute-start(bf16[2,160,512]{2,1,0:T(8,128)(2,1)S(1)} %get-tuple-element.24), channel_id=1, source_target_pairs={{0,192},{64,256},{128,320},{192,384},{256,448},{320,0},{384,64},{4... | collective-permute-start | bytes 983048 | tf_op jit(solution)/shard_map/ppermute | solution.py:216
  25.8 27.0 %collective-permute-start.3 = (bf16[2,160,512]{2,1,0:T(8,128)(2,1)S(1)}, bf16[2,160,512]{2,1,0:T(8,128)(2,1)S(1)}, u32[]{:S(2)}, u32[]{:S(2)}) collective-permute-start(bf16[2,160,512]{2,1,0:T(8,128)(2,1)S(1)} %get-tuple-element.23), channel_id=1, source_target_pairs={{0,320},{64,384},{128,448},{192,0},{256,64},{320,128},{384,192},{4... | collective-permute-start | bytes 983048 | tf_op jit(solution)/shard_map/ppermute | solution.py:216
  54.8 8.9 %copy-start.7 = (s32[64]{0:T(128)S(1)}, s32[64]{0:T(128)}, u32[]{:S(2)}) copy-start(s32[64]{0:T(128)} %param.14) | copy-start | bytes 772
  54.8 11.4 %copy-start.5 = (bf16[2,4,2,256]{3,2,1,0:T(2,128)(2,1)S(1)}, bf16[2,4,2,256]{3,2,1,0:T(2,128)(2,1)}, u32[]{:S(2)}) copy-start(bf16[2,4,2,256]{3,2,1,0:T(2,128)(2,1)} %param.12) | copy-start | bytes 24580
  54.8 11.4 %copy-start.3 = (bf16[128,2,256]{2,1,0:T(2,128)(2,1)S(1)}, bf16[128,2,256]{2,1,0:T(2,128)(2,1)}, u32[]{:S(2)}) copy-start(bf16[128,2,256]{2,1,0:T(2,128)(2,1)} %param.10) | copy-start | bytes 393220
  54.8 12.2 %copy-start.4 = (bf16[256,8]{0,1:T(8,128)(2,1)S(1)}, bf16[256,8]{0,1:T(8,128)(2,1)}, u32[]{:S(2)}) copy-start(bf16[256,8]{0,1:T(8,128)(2,1)} %param.16) | copy-start | bytes 12292
  54.8 1.2 %copy-start.2 = (bf16[8,192,512]{2,1,0:T(8,128)(2,1)}, bf16[8,192,512]{2,1,0:T(8,128)(2,1)S(1)}, u32[]{:S(2)}) copy-start(bf16[8,192,512]{2,1,0:T(8,128)(2,1)S(1)} %all-to-all-done.1) | copy-start | bytes 4718596
  55.9 47.3 %all-to-all-start = ((bf16[8,320,512]{2,1,0:T(8,128)(2,1)}), bf16[8,320,512]{2,1,0:T(8,128)(2,1)S(1)}, u32[]{:S(2)}, u32[]{:S(2)}) async-start(bf16[8,320,512]{2,1,0:T(8,128)(2,1)} %broadcast_select_fusion), calls=%async_computation | async-start | bytes 5242880 | tf_op jit(solution)/shard_map/all_to_all | solution.py:240
  67.9 34.5 %copy-start.6 = (s32[128,2]{0,1:T(2,128)S(1)}, s32[128,2]{0,1:T(2,128)}, u32[]{:S(2)}) copy-start(s32[128,2]{0,1:T(2,128)} %param.17) | copy-start | bytes 3076
  103.3 1.5 %copy-start.1 = (bf16[8,320,512]{2,1,0:T(8,128)(2,1)}, bf16[8,320,512]{2,1,0:T(8,128)(2,1)S(1)}, u32[]{:S(2)}) copy-start(bf16[8,320,512]{2,1,0:T(8,128)(2,1)S(1)} %all-to-all-done) | copy-start | bytes 7864324

commit v10 on v9

--- a/solution.py
+++ b/solution.py
@@ -98,7 +98,10 @@
     acc_ref,
     top_ref,
     total_ref,
-    gate_ref,
+    logits_ref,
+    pick0_ref,
+    pick1_ref,
+    live_ref,
     out_ref,
     score_ref,
     *,
@@ -118,9 +121,14 @@
         wv_ref, score_ref, top, total_ref[:, 0:1] * factor, acc_ref[...] * factor
     )
     attended = acc / total
-    gate = gate_ref[...]
-    out_ref[:, :HEAD_DIM] = (attended[:rows] * gate[:, 0:1]).astype(out_ref.dtype)
-    out_ref[:, HEAD_DIM:] = (attended[rows:] * gate[:, 1:2]).astype(out_ref.dtype)
+    logits = logits_ref[...]
+    chosen0 = jnp.sum(jnp.where(pick0_ref[...] != 0, logits, 0.0), axis=1, keepdims=True)
+    chosen1 = jnp.sum(jnp.where(pick1_ref[...] != 0, logits, 0.0), axis=1, keepdims=True)
+    live = live_ref[...] != 0
+    gate0 = jnp.where(live, jax.nn.sigmoid(chosen0 - chosen1), 0.0)
+    gate1 = jnp.where(live, jax.nn.sigmoid(chosen1 - chosen0), 0.0)
+    out_ref[:, :HEAD_DIM] = (attended[:rows] * gate0).astype(out_ref.dtype)
+    out_ref[:, HEAD_DIM:] = (attended[rows:] * gate1).astype(out_ref.dtype)
 
 
 def attend_first(queries, key_pos, parts, plane_rows, extra, head_count, extra_sinks, per_device):
@@ -162,7 +170,7 @@
     return acc, top, total
 
 
-def attend_second(queries, key_pos, parts, plane_rows, state, gate_live, head_count, per_device):
+def attend_second(queries, key_pos, parts, plane_rows, state, gate_inputs, head_count, per_device):
     rows = queries.shape[0]
     stacked = PICKS * rows
     first, second = parts
@@ -190,12 +198,12 @@
             state_spec,
             state_spec,
             state_spec,
-            pl.BlockSpec((rows, PICKS), lambda h: (0, 0)),
-        ],
+        ]
+        + [pl.BlockSpec(value.shape, lambda h: (0, 0)) for value in gate_inputs],
         out_specs=q_spec,
         scratch_shapes=[pltpu.VMEM((stacked, second_rows), jnp.float32)],
         out_shape=jax.ShapeDtypeStruct((rows, head_count * PICKS * HEAD_DIM), jnp.bfloat16),
-    )(queries, second_pos, second, second, acc, top, total, gate_live)
+    )(queries, second_pos, second, second, acc, top, total, *gate_inputs)
 
 
 def body(queries, suffix_kv, window_kv, sink_kv, lengths, group_ids, hidden_in, router, picks):
@@ -267,14 +275,12 @@
     state, partial_value = lax.optimization_barrier((state, partial_value))
     logits = lax.psum(partial_value, "tp")
     experts = jnp.arange(logits.shape[1], dtype=jnp.int32)
-    chosen = jnp.sum(
-        jnp.where(picks[:, :, None] == experts[None, None, :], logits[:, None, :], 0.0), axis=2
-    )
-    gate_values = jax.nn.sigmoid(chosen - chosen[:, ::-1])
-    is_live = jnp.arange(row_count, dtype=jnp.int32) < lengths[0]
-    gate_live = jnp.where(is_live[:, None], gate_values, 0.0)
+    pick0 = (picks[:, 0:1] == experts[None, :]).astype(jnp.int32)
+    pick1 = (picks[:, 1:2] == experts[None, :]).astype(jnp.int32)
+    is_live = (jnp.arange(row_count, dtype=jnp.int32) < lengths[0]).astype(jnp.int32)
+    gate_inputs = (logits, pick0, pick1, is_live[:, None])
     return attend_second(
-        queries, key_pos, parts, plane_rows, state, gate_live, head_count, per_device
+        queries, key_pos, parts, plane_rows, state, gate_inputs, head_count, per_device
     )
 
 

time: 110 us -> 123 us (1.12)
  blocking collectives: 30.4 us -> 43 us
    psum x1, blocking collectives: 30.4 us -> 43 us  [body(): logits = lax.psum(partial_value, 'tp')]
    convert_element_type x0 -> x2, other arithmetic: none -> 1.4 us  [the longest x1 0.78 us: body(): pick0 = (picks[:, 0:1] == experts[None, :]).astype(jnp.int32)]
  transfers between devices with their start and end apart: 6 -> 6, of which waited for: 3 -> 3; matrix products, arithmetic and copies ran while one was open for 7% -> 6% of each run, Pallas kernels for 4% -> 3%
where the time goes in v10:
time: 123 us
  blocking collectives  43 us (35%)
  starting transfers between devices  29.1 us (24%)
  waiting for transfers between devices  26 us (21%)
  Pallas kernels  9.2 us (7%)
  other arithmetic  6.68 us (5%)
  local copies, waits for them, and re-layouts  6.06 us (5%)
  between operations  2.59 us (2%)
    psum x1, blocking collectives, body(): logits = lax.psum(partial_value, 'tp')  43 us
    ppermute x4, waiting for transfers between devices, shifted(): return lax.ppermute(value, 'z', pairs)  26 us
    ppermute x4, starting transfers between devices, shifted(): return lax.ppermute(value, 'z', pairs)  17.2 us
    all_to_all x2, starting transfers between devices, body(): lax.all_to_all(outgoing, ('ylo', 'x'), split_axis=0, concat_axis=0, tiled...  12 us
    pallas_call x1, Pallas kernels, attend_second(): pl.pallas_call(functools.partial(second_kernel, per_device=per_device, st...  5.2 us
    pallas_call x1, Pallas kernels, attend_first(): pl.pallas_call(functools.partial(first_kernel, extra_sinks=extra_sinks, p...  4 us
    select_n x2, other arithmetic, body(): jnp.where((peer_groups == 0)[:, None, None], data[None, 0], data[None, 1])  3.19 us
    unnamed x22, local copies, waits for them, and re-layouts  2.73 us
  transfers between devices with their start and end apart: 6, of which 3 were waited for; matrix products, arithmetic and copies ran while one was open for 6% of the time, Pallas kernels for 3%

profile of v10, /device:TPU:142, one launch (start us, length us, event | category | flops | bytes accessed | tf_op | source)
XLA Modules:
  0.0 122.8 jit_solution(15857070443993492863)
XLA Ops:
  0.0 0.0 copy-start
  0.0 1.0 reshape.99
  1.0 1.9 %collective-permute-start = (bf16[2,64,512]{2,1,0:T(8,128)(2,1)S(1)}, bf16[2,64,512]{2,1,0:T(8,128)(2,1)S(1)}, u32[]{:S(2)}, u32[]{:S(2)}) collective-permute-start(bf16[2,64,512]{2,1,0:T(8,128)(2,1)S(1)} %reshape.99), channel_id=1, source_target_pairs={{0,448},{64,0},{128,64},{192,128},{256,192},{320,256},{384,320},{4... | collective-permute-start | bytes 393224 | tf_op jit(solution)/shard_map/ppermute | solution.py:224
  3.0 4.3 %collective-permute-start.1 = (bf16[2,64,512]{2,1,0:T(8,128)(2,1)S(1)}, bf16[2,64,512]{2,1,0:T(8,128)(2,1)S(1)}, u32[]{:S(2)}, u32[]{:S(2)}) collective-permute-start(bf16[2,64,512]{2,1,0:T(8,128)(2,1)S(1)} %reshape.99), channel_id=1, source_target_pairs={{0,64},{64,128},{128,192},{192,256},{256,320},{320,384},{384,448},... | collective-permute-start | bytes 393224 | tf_op jit(solution)/shard_map/ppermute | solution.py:224
  7.3 0.7 dynamic-slice_compare_fusion
  8.0 2.1 %collective-permute-done.1 = bf16[2,64,512]{2,1,0:T(8,128)(2,1)S(1)} collective-permute-done((bf16[2,64,512]{2,1,0:T(8,128)(2,1)S(1)}, bf16[2,64,512]{2,1,0:T(8,128)(2,1)S(1)}, u32[]{:S(2)}, u32[]{:S(2)}) %collective-permute-start.1) | collective-permute-done | bytes 131104 | tf_op jit(solution)/shard_map/ppermute | solution.py:224
  10.1 0.0 collective-permute-done
  10.2 1.3 %broadcast_select_fusion.1 = bf16[8,192,512]{2,1,0:T(8,128)(2,1)} fusion(pred[8]{0:T(512)(128)(4,1)S(1)} %dynamic-slice_compare_fusion, bf16[192,512]{1,0:T(8,128)(2,1)S(1)} %get-tuple-element.22, bf16[192,512]{1,0:T(8,128)(2,1)S(1)} %get-tuple-element.21), kind=kLoop, calls=%fused_computation.1 | loop fusion | flops 786432 | bytes 1966088 | tf_op jit(solution)/shard_map/jit(_where)/select_n | solution.py:247
  11.5 6.3 %all-to-all-start.1 = ((bf16[8,192,512]{2,1,0:T(8,128)(2,1)}), bf16[8,192,512]{2,1,0:T(8,128)(2,1)S(1)}, u32[]{:S(2)}, u32[]{:S(2)}) async-start(bf16[8,192,512]{2,1,0:T(8,128)(2,1)} %broadcast_select_fusion.1), calls=%async_computation.1 | async-start | bytes 3145728 | tf_op jit(solution)/shard_map/all_to_all | solution.py:248
  17.8 0.1 pad_maximum_fusion.1
  17.9 7.9 %collective-permute-start.2 = (bf16[2,160,512]{2,1,0:T(8,128)(2,1)S(1)}, bf16[2,160,512]{2,1,0:T(8,128)(2,1)S(1)}, u32[]{:S(2)}, u32[]{:S(2)}) collective-permute-start(bf16[2,160,512]{2,1,0:T(8,128)(2,1)S(1)} %get-tuple-element.24), channel_id=1, source_target_pairs={{0,192},{64,256},{128,320},{192,384},{256,448},{320,0},{384,64},{4... | collective-permute-start | bytes 983048 | tf_op jit(solution)/shard_map/ppermute | solution.py:224
  25.8 3.1 %collective-permute-start.3 = (bf16[2,160,512]{2,1,0:T(8,128)(2,1)S(1)}, bf16[2,160,512]{2,1,0:T(8,128)(2,1)S(1)}, u32[]{:S(2)}, u32[]{:S(2)}) collective-permute-start(bf16[2,160,512]{2,1,0:T(8,128)(2,1)S(1)} %get-tuple-element.23), channel_id=1, source_target_pairs={{0,320},{64,384},{128,448},{192,0},{256,64},{320,128},{384,192},{4... | collective-permute-start | bytes 983048 | tf_op jit(solution)/shard_map/ppermute | solution.py:224
  28.8 14.4 %collective-permute-done.2 = bf16[2,160,512]{2,1,0:T(8,128)(2,1)S(1)} collective-permute-done((bf16[2,160,512]{2,1,0:T(8,128)(2,1)S(1)}, bf16[2,160,512]{2,1,0:T(8,128)(2,1)S(1)}, u32[]{:S(2)}, u32[]{:S(2)}) %collective-permute-start.2) | collective-permute-done | bytes 327712 | tf_op jit(solution)/shard_map/ppermute | solution.py:224
  43.3 9.5 %collective-permute-done.3 = bf16[2,160,512]{2,1,0:T(8,128)(2,1)S(1)} collective-permute-done((bf16[2,160,512]{2,1,0:T(8,128)(2,1)S(1)}, bf16[2,160,512]{2,1,0:T(8,128)(2,1)S(1)}, u32[]{:S(2)}, u32[]{:S(2)}) %collective-permute-start.3) | collective-permute-done | bytes 327712 | tf_op jit(solution)/shard_map/ppermute | solution.py:224
  52.9 1.9 %broadcast_select_fusion = bf16[8,320,512]{2,1,0:T(8,128)(2,1)} fusion(pred[8]{0:T(512)(128)(4,1)S(1)} %dynamic-slice_compare_fusion, bf16[320,512]{1,0:T(8,128)(2,1)S(1)} %get-tuple-element.20, bf16[320,512]{1,0:T(8,128)(2,1)S(1)} %get-tuple-element.19), kind=kLoop, calls=%fused_computation | loop fusion | flops 1310720 | bytes 3276808 | tf_op jit(solution)/shard_map/jit(_where)/select_n | solution.py:247
  54.7 0.0 copy-start.7
  54.7 0.0 copy-start.5
  54.7 0.0 copy-start.3
  54.7 0.0 copy-start.6
  54.7 0.0 copy-start.4
  54.7 0.0 all-to-all-done.1
  54.8 0.0 copy-start.2
  54.8 1.1 copy-done.2
  55.9 5.7 %all-to-all-start = ((bf16[8,320,512]{2,1,0:T(8,128)(2,1)}), bf16[8,320,512]{2,1,0:T(8,128)(2,1)S(1)}, u32[]{:S(2)}, u32[]{:S(2)}) async-start(bf16[8,320,512]{2,1,0:T(8,128)(2,1)} %broadcast_select_fusion), calls=%async_computation | async-start | bytes 5242880 | tf_op jit(solution)/shard_map/all_to_all | solution.py:248
  61.7 0.1 iota_add_fusion.3
  61.7 0.1 broadcast_add_fusion
  61.8 0.1 iota_add_fusion
  61.9 0.1 concatenate.25
  62.0 0.1 reshape.97
  62.1 0.1 iota_add_fusion.7
  62.1 0.1 iota_add_fusion.5
  62.2 0.1 pad_add_fusion.1
  62.3 0.1 reshape.96
  62.4 0.6 slice.40.pos_ref
  63.0 0.6 slice.45.pos_ref
  63.6 0.0 copy-done.7
  63.6 0.6 dynamic_slice.11
  65.8 0.0 copy-done.5
  65.9 0.0 copy-done.3
  66.6 0.1 pad.2.clone
  66.7 0.6 fusion.2.live_ref
  67.3 0.0 copy-done.6
  67.3 0.0 copy-done
  67.3 0.0 copy-done.4
  67.3 0.1 fusion.3
  67.4 0.8 fusion
  68.2 0.8 maximum_maximum_fusion.xk_ref.xv_ref
  69.0 4.0 %shard_map.91 = (f32[2,256,128]{2,1,0:T(8,128)}, f32[2,256,128]{2,1,0:T(8,128)}, f32[2,256,128]{2,1,0:T(8,128)}) custom-call(bf16[128,512]{1,0:T(8,128)(2,1)} %q_ref.3, s32[1,1536]{1,0:T(1,128)} %slice.45.pos_ref, bf16[1536,512]{1,0:T(8,128)(2,1)} %bitcast.28, bf16[1536,512]{1,0:T(8,128)(2,1)} %bitcast.29, ...), custom_call_target="tpu_custom_call" | custom-call | tf_op jit(solution)/shard_map/pallas_call | solution.py:153
  73.0 0.1 copy.10
  73.1 43.0 %psum.7.logits_ref = f32[128,8]{1,0:T(8,128)} all-reduce(f32[128,8]{1,0:T(8,128)S(1)} %copy.10), channel_id=1, replica_groups=mesh['z'=8,'ylo'=2,'x'=4,'tp'=8] {'tp'}, use_global_device_ids=true, to_apply=%region_0.1 | all-reduce | flops 1024 | bytes 8192 | tf_op jit(solution)/shard_map/psum | solution.py:276
  116.1 0.0 all-to-all-done
  116.1 0.0 copy-start.1
  116.1 1.5 %copy-done.1 = bf16[8,320,512]{2,1,0:T(8,128)(2,1)} copy-done((bf16[8,320,512]{2,1,0:T(8,128)(2,1)}, bf16[8,320,512]{2,1,0:T(8,128)(2,1)S(1)}, u32[]{:S(2)}) %copy-start.1) | copy-done | bytes 2621464
  117.6 5.2 %shard_map.92 = bf16[128,512]{1,0:T(8,128)(2,1)} custom-call(bf16[128,512]{1,0:T(8,128)(2,1)} %q_ref.3, s32[1,2560]{1,0:T(1,128)} %slice.40.pos_ref, bf16[2560,512]{1,0:T(8,128)(2,1)} %bitcast.26, bf16[2560,512]{1,0:T(8,128)(2,1)} %bitcast.27, f32[2,256,128]{2,1,0:T(8,128)} %get-tuple-element.15.acc_ref, f32[2,256,128]{2,1,0:T(8,128)} %get-tuple-element.16.top_ref, ...), custom_call_target="tpu_custom_call" | custom-call | tf_op jit(solution)/shard_map/pallas_call | solution.py:190
  (24 shorter events, 0.3 us)
Async XLA Ops:
  0.0 67.3 %copy-start = (bf16[128,256]{1,0:T(8,128)(2,1)S(1)}, bf16[128,256]{1,0:T(8,128)(2,1)}, u32[]{:S(2)}) copy-start(bf16[128,256]{1,0:T(8,128)(2,1)} %param.15) | copy-start | bytes 196612
  1.0 9.1 %collective-permute-start = (bf16[2,64,512]{2,1,0:T(8,128)(2,1)S(1)}, bf16[2,64,512]{2,1,0:T(8,128)(2,1)S(1)}, u32[]{:S(2)}, u32[]{:S(2)}) collective-permute-start(bf16[2,64,512]{2,1,0:T(8,128)(2,1)S(1)} %reshape.99), channel_id=1, source_target_pairs={{0,448},{64,0},{128,64},{192,128},{256,192},{320,256},{384,320},{4... | collective-permute-start | bytes 393224 | tf_op jit(solution)/shard_map/ppermute | solution.py:224
  3.0 7.1 %collective-permute-start.1 = (bf16[2,64,512]{2,1,0:T(8,128)(2,1)S(1)}, bf16[2,64,512]{2,1,0:T(8,128)(2,1)S(1)}, u32[]{:S(2)}, u32[]{:S(2)}) collective-permute-start(bf16[2,64,512]{2,1,0:T(8,128)(2,1)S(1)} %reshape.99), channel_id=1, source_target_pairs={{0,64},{64,128},{128,192},{192,256},{256,320},{320,384},{384,448},... | collective-permute-start | bytes 393224 | tf_op jit(solution)/shard_map/ppermute | solution.py:224
  11.5 43.2 %all-to-all-start.1 = ((bf16[8,192,512]{2,1,0:T(8,128)(2,1)}), bf16[8,192,512]{2,1,0:T(8,128)(2,1)S(1)}, u32[]{:S(2)}, u32[]{:S(2)}) async-start(bf16[8,192,512]{2,1,0:T(8,128)(2,1)} %broadcast_select_fusion.1), calls=%async_computation.1 | async-start | bytes 3145728 | tf_op jit(solution)/shard_map/all_to_all | solution.py:248
  17.9 25.4 %collective-permute-start.2 = (bf16[2,160,512]{2,1,0:T(8,128)(2,1)S(1)}, bf16[2,160,512]{2,1,0:T(8,128)(2,1)S(1)}, u32[]{:S(2)}, u32[]{:S(2)}) collective-permute-start(bf16[2,160,512]{2,1,0:T(8,128)(2,1)S(1)} %get-tuple-element.24), channel_id=1, source_target_pairs={{0,192},{64,256},{128,320},{192,384},{256,448},{320,0},{384,64},{4... | collective-permute-start | bytes 983048 | tf_op jit(solution)/shard_map/ppermute | solution.py:224
  25.8 27.0 %collective-permute-start.3 = (bf16[2,160,512]{2,1,0:T(8,128)(2,1)S(1)}, bf16[2,160,512]{2,1,0:T(8,128)(2,1)S(1)}, u32[]{:S(2)}, u32[]{:S(2)}) collective-permute-start(bf16[2,160,512]{2,1,0:T(8,128)(2,1)S(1)} %get-tuple-element.23), channel_id=1, source_target_pairs={{0,320},{64,384},{128,448},{192,0},{256,64},{320,128},{384,192},{4... | collective-permute-start | bytes 983048 | tf_op jit(solution)/shard_map/ppermute | solution.py:224
  54.7 8.9 %copy-start.7 = (s32[64]{0:T(128)S(1)}, s32[64]{0:T(128)}, u32[]{:S(2)}) copy-start(s32[64]{0:T(128)} %param.14) | copy-start | bytes 772
  54.7 11.1 %copy-start.5 = (bf16[2,4,2,256]{3,2,1,0:T(2,128)(2,1)S(1)}, bf16[2,4,2,256]{3,2,1,0:T(2,128)(2,1)}, u32[]{:S(2)}) copy-start(bf16[2,4,2,256]{3,2,1,0:T(2,128)(2,1)} %param.12) | copy-start | bytes 24580
  54.7 11.2 %copy-start.3 = (bf16[128,2,256]{2,1,0:T(2,128)(2,1)S(1)}, bf16[128,2,256]{2,1,0:T(2,128)(2,1)}, u32[]{:S(2)}) copy-start(bf16[128,2,256]{2,1,0:T(2,128)(2,1)} %param.10) | copy-start | bytes 393220
  54.7 12.6 %copy-start.6 = (s32[128,2]{0,1:T(2,128)S(1)}, s32[128,2]{0,1:T(2,128)}, u32[]{:S(2)}) copy-start(s32[128,2]{0,1:T(2,128)} %param.17) | copy-start | bytes 3076
  54.7 12.6 %copy-start.4 = (bf16[256,8]{0,1:T(8,128)(2,1)S(1)}, bf16[256,8]{0,1:T(8,128)(2,1)}, u32[]{:S(2)}) copy-start(bf16[256,8]{0,1:T(8,128)(2,1)} %param.16) | copy-start | bytes 12292
  54.8 1.1 copy-start.2
  55.9 60.2 %all-to-all-start = ((bf16[8,320,512]{2,1,0:T(8,128)(2,1)}), bf16[8,320,512]{2,1,0:T(8,128)(2,1)S(1)}, u32[]{:S(2)}, u32[]{:S(2)}) async-start(bf16[8,320,512]{2,1,0:T(8,128)(2,1)} %broadcast_select_fusion), calls=%async_computation | async-start | bytes 5242880 | tf_op jit(solution)/shard_map/all_to_all | solution.py:248
  116.1 1.5 %copy-start.1 = (bf16[8,320,512]{2,1,0:T(8,128)(2,1)}, bf16[8,320,512]{2,1,0:T(8,128)(2,1)S(1)}, u32[]{:S(2)}) copy-start(bf16[8,320,512]{2,1,0:T(8,128)(2,1)S(1)} %all-to-all-done) | copy-start | bytes 7864324

commit v11 on v10

--- a/solution.py
+++ b/solution.py
@@ -122,11 +122,20 @@
     )
     attended = acc / total
     logits = logits_ref[...]
-    chosen0 = jnp.sum(jnp.where(pick0_ref[...] != 0, logits, 0.0), axis=1, keepdims=True)
-    chosen1 = jnp.sum(jnp.where(pick1_ref[...] != 0, logits, 0.0), axis=1, keepdims=True)
+    chosen0 = jnp.sum(jnp.where(pick0_ref[...] != 0, logits, 0.0), axis=0, keepdims=True)
+    chosen1 = jnp.sum(jnp.where(pick1_ref[...] != 0, logits, 0.0), axis=0, keepdims=True)
     live = live_ref[...] != 0
-    gate0 = jnp.where(live, jax.nn.sigmoid(chosen0 - chosen1), 0.0)
-    gate1 = jnp.where(live, jax.nn.sigmoid(chosen1 - chosen0), 0.0)
+    gate_rows = jnp.concatenate(
+        [
+            jnp.where(live, jax.nn.sigmoid(chosen0 - chosen1), 0.0),
+            jnp.where(live, jax.nn.sigmoid(chosen1 - chosen0), 0.0),
+            jnp.zeros((logits.shape[0] - PICKS, logits.shape[1]), jnp.float32),
+        ],
+        axis=0,
+    )
+    gate_cols = jnp.transpose(gate_rows)
+    gate0 = gate_cols[:, 0:1]
+    gate1 = gate_cols[:, 1:2]
     out_ref[:, :HEAD_DIM] = (attended[:rows] * gate0).astype(out_ref.dtype)
     out_ref[:, HEAD_DIM:] = (attended[rows:] * gate1).astype(out_ref.dtype)
 
@@ -275,10 +284,10 @@
     state, partial_value = lax.optimization_barrier((state, partial_value))
     logits = lax.psum(partial_value, "tp")
     experts = jnp.arange(logits.shape[1], dtype=jnp.int32)
-    pick0 = (picks[:, 0:1] == experts[None, :]).astype(jnp.int32)
-    pick1 = (picks[:, 1:2] == experts[None, :]).astype(jnp.int32)
+    pick0 = (picks[:, 0][None, :] == experts[:, None]).astype(jnp.int32)
+    pick1 = (picks[:, 1][None, :] == experts[:, None]).astype(jnp.int32)
     is_live = (jnp.arange(row_count, dtype=jnp.int32) < lengths[0]).astype(jnp.int32)
-    gate_inputs = (logits, pick0, pick1, is_live[:, None])
+    gate_inputs = (jnp.transpose(logits), pick0, pick1, is_live[None, :])
     return attend_second(
         queries, key_pos, parts, plane_rows, state, gate_inputs, head_count, per_device
     )

time: 123 us -> 110 us (0.89)
  blocking collectives: 43 us -> 30.1 us
    psum x1, blocking collectives: 43 us -> 30.1 us  [body(): logits = lax.psum(partial_value, 'tp')]
  transfers between devices with their start and end apart: 6 -> 6, of which waited for: 3 -> 3; matrix products, arithmetic and copies ran while one was open for 6% -> 7% of each run, Pallas kernels for 3% -> 4%
where the time goes in v11:
time: 110 us
  blocking collectives  30.1 us (27%)
  starting transfers between devices  29.1 us (26%)
  waiting for transfers between devices  26 us (24%)
  Pallas kernels  9.18 us (8%)
  other arithmetic  6.43 us (6%)
  local copies, waits for them, and re-layouts  5.98 us (5%)
  between operations  2.58 us (2%)
    psum x1, blocking collectives, body(): logits = lax.psum(partial_value, 'tp')  30.1 us
    ppermute x4, waiting for transfers between devices, shifted(): return lax.ppermute(value, 'z', pairs)  26 us
    ppermute x4, starting transfers between devices, shifted(): return lax.ppermute(value, 'z', pairs)  17.2 us
    all_to_all x2, starting transfers between devices, body(): lax.all_to_all(outgoing, ('ylo', 'x'), split_axis=0, concat_axis=0, tiled...  12 us
    pallas_call x1, Pallas kernels, attend_second(): pl.pallas_call(functools.partial(second_kernel, per_device=per_device, st...  5.18 us
    pallas_call x1, Pallas kernels, attend_first(): pl.pallas_call(functools.partial(first_kernel, extra_sinks=extra_sinks, p...  4 us
    select_n x2, other arithmetic, body(): jnp.where((peer_groups == 0)[:, None, None], data[None, 0], data[None, 1])  3.19 us
    unnamed x22, local copies, waits for them, and re-layouts  2.73 us
  transfers between devices with their start and end apart: 6, of which 3 were waited for; matrix products, arithmetic and copies ran while one was open for 7% of the time, Pallas kernels for 4%

profile of v11, /device:TPU:142, one launch (start us, length us, event | category | flops | bytes accessed | tf_op | source)
XLA Modules:
  0.0 109.6 jit_solution(11830209823963199164)
XLA Ops:
  0.0 0.0 copy-start
  0.0 1.0 reshape.101
  1.0 1.9 %collective-permute-start = (bf16[2,64,512]{2,1,0:T(8,128)(2,1)S(1)}, bf16[2,64,512]{2,1,0:T(8,128)(2,1)S(1)}, u32[]{:S(2)}, u32[]{:S(2)}) collective-permute-start(bf16[2,64,512]{2,1,0:T(8,128)(2,1)S(1)} %reshape.101), channel_id=1, source_target_pairs={{0,448},{64,0},{128,64},{192,128},{256,192},{320,256},{384,320},{4... | collective-permute-start | bytes 393224 | tf_op jit(solution)/shard_map/ppermute | solution.py:233
  3.0 4.3 %collective-permute-start.1 = (bf16[2,64,512]{2,1,0:T(8,128)(2,1)S(1)}, bf16[2,64,512]{2,1,0:T(8,128)(2,1)S(1)}, u32[]{:S(2)}, u32[]{:S(2)}) collective-permute-start(bf16[2,64,512]{2,1,0:T(8,128)(2,1)S(1)} %reshape.101), channel_id=1, source_target_pairs={{0,64},{64,128},{128,192},{192,256},{256,320},{320,384},{384,448},... | collective-permute-start | bytes 393224 | tf_op jit(solution)/shard_map/ppermute | solution.py:233
  7.3 0.7 dynamic-slice_compare_fusion
  8.0 2.1 %collective-permute-done.1 = bf16[2,64,512]{2,1,0:T(8,128)(2,1)S(1)} collective-permute-done((bf16[2,64,512]{2,1,0:T(8,128)(2,1)S(1)}, bf16[2,64,512]{2,1,0:T(8,128)(2,1)S(1)}, u32[]{:S(2)}, u32[]{:S(2)}) %collective-permute-start.1) | collective-permute-done | bytes 131104 | tf_op jit(solution)/shard_map/ppermute | solution.py:233
  10.1 0.0 collective-permute-done
  10.2 1.3 %broadcast_select_fusion.1 = bf16[8,192,512]{2,1,0:T(8,128)(2,1)} fusion(pred[8]{0:T(512)(128)(4,1)S(1)} %dynamic-slice_compare_fusion, bf16[192,512]{1,0:T(8,128)(2,1)S(1)} %get-tuple-element.22, bf16[192,512]{1,0:T(8,128)(2,1)S(1)} %get-tuple-element.21), kind=kLoop, calls=%fused_computation.1 | loop fusion | flops 786432 | bytes 1966088 | tf_op jit(solution)/shard_map/jit(_where)/select_n | solution.py:256
  11.5 6.3 %all-to-all-start.1 = ((bf16[8,192,512]{2,1,0:T(8,128)(2,1)}), bf16[8,192,512]{2,1,0:T(8,128)(2,1)S(1)}, u32[]{:S(2)}, u32[]{:S(2)}) async-start(bf16[8,192,512]{2,1,0:T(8,128)(2,1)} %broadcast_select_fusion.1), calls=%async_computation.1 | async-start | bytes 3145728 | tf_op jit(solution)/shard_map/all_to_all | solution.py:257
  17.8 0.1 pad_maximum_fusion.1
  17.9 7.9 %collective-permute-start.2 = (bf16[2,160,512]{2,1,0:T(8,128)(2,1)S(1)}, bf16[2,160,512]{2,1,0:T(8,128)(2,1)S(1)}, u32[]{:S(2)}, u32[]{:S(2)}) collective-permute-start(bf16[2,160,512]{2,1,0:T(8,128)(2,1)S(1)} %get-tuple-element.24), channel_id=1, source_target_pairs={{0,192},{64,256},{128,320},{192,384},{256,448},{320,0},{384,64},{4... | collective-permute-start | bytes 983048 | tf_op jit(solution)/shard_map/ppermute | solution.py:233
  25.8 3.1 %collective-permute-start.3 = (bf16[2,160,512]{2,1,0:T(8,128)(2,1)S(1)}, bf16[2,160,512]{2,1,0:T(8,128)(2,1)S(1)}, u32[]{:S(2)}, u32[]{:S(2)}) collective-permute-start(bf16[2,160,512]{2,1,0:T(8,128)(2,1)S(1)} %get-tuple-element.23), channel_id=1, source_target_pairs={{0,320},{64,384},{128,448},{192,0},{256,64},{320,128},{384,192},{4... | collective-permute-start | bytes 983048 | tf_op jit(solution)/shard_map/ppermute | solution.py:233
  28.8 14.4 %collective-permute-done.2 = bf16[2,160,512]{2,1,0:T(8,128)(2,1)S(1)} collective-permute-done((bf16[2,160,512]{2,1,0:T(8,128)(2,1)S(1)}, bf16[2,160,512]{2,1,0:T(8,128)(2,1)S(1)}, u32[]{:S(2)}, u32[]{:S(2)}) %collective-permute-start.2) | collective-permute-done | bytes 327712 | tf_op jit(solution)/shard_map/ppermute | solution.py:233
  43.3 9.5 %collective-permute-done.3 = bf16[2,160,512]{2,1,0:T(8,128)(2,1)S(1)} collective-permute-done((bf16[2,160,512]{2,1,0:T(8,128)(2,1)S(1)}, bf16[2,160,512]{2,1,0:T(8,128)(2,1)S(1)}, u32[]{:S(2)}, u32[]{:S(2)}) %collective-permute-start.3) | collective-permute-done | bytes 327712 | tf_op jit(solution)/shard_map/ppermute | solution.py:233
  52.9 1.9 %broadcast_select_fusion = bf16[8,320,512]{2,1,0:T(8,128)(2,1)} fusion(pred[8]{0:T(512)(128)(4,1)S(1)} %dynamic-slice_compare_fusion, bf16[320,512]{1,0:T(8,128)(2,1)S(1)} %get-tuple-element.20, bf16[320,512]{1,0:T(8,128)(2,1)S(1)} %get-tuple-element.19), kind=kLoop, calls=%fused_computation | loop fusion | flops 1310720 | bytes 3276808 | tf_op jit(solution)/shard_map/jit(_where)/select_n | solution.py:256
  54.7 0.0 copy-start.7
  54.7 0.0 copy-start.5
  54.7 0.0 copy-start.3
  54.7 0.0 copy-start.6
  54.7 0.0 copy-start.4
  54.7 0.0 all-to-all-done.1
  54.8 0.0 copy-start.2
  54.8 1.1 %copy-done.2 = bf16[8,192,512]{2,1,0:T(8,128)(2,1)} copy-done((bf16[8,192,512]{2,1,0:T(8,128)(2,1)}, bf16[8,192,512]{2,1,0:T(8,128)(2,1)S(1)}, u32[]{:S(2)}) %copy-start.2) | copy-done | bytes 1572888
  55.9 5.7 %all-to-all-start = ((bf16[8,320,512]{2,1,0:T(8,128)(2,1)}), bf16[8,320,512]{2,1,0:T(8,128)(2,1)S(1)}, u32[]{:S(2)}, u32[]{:S(2)}) async-start(bf16[8,320,512]{2,1,0:T(8,128)(2,1)} %broadcast_select_fusion), calls=%async_computation | async-start | bytes 5242880 | tf_op jit(solution)/shard_map/all_to_all | solution.py:257
  61.7 0.1 iota_add_fusion.3
  61.7 0.1 broadcast_add_fusion
  61.8 0.1 iota_add_fusion
  61.9 0.1 concatenate.25
  62.0 0.1 reshape.99
  62.1 0.1 iota_add_fusion.7
  62.1 0.1 iota_add_fusion.5
  62.2 0.1 pad_add_fusion.1
  62.3 0.1 reshape.98
  62.4 0.6 slice.40.pos_ref
  63.0 0.6 slice.45.pos_ref
  63.6 0.0 copy-done.7
  63.6 0.6 dynamic_slice.11
  65.9 0.0 copy-done.5
  65.9 0.0 copy-done.3
  66.6 0.1 pad.2.clone
  66.7 0.5 compare_convert_fusion.live_ref
  67.2 0.0 copy-done.6
  67.2 0.6 fusion
  67.8 0.0 copy-done
  67.8 0.0 copy-done.4
  67.8 0.1 fusion.2
  67.9 0.8 maximum_maximum_fusion.xk_ref.xv_ref
  68.8 4.0 %shard_map.91 = (f32[2,256,128]{2,1,0:T(8,128)}, f32[2,256,128]{2,1,0:T(8,128)}, f32[2,256,128]{2,1,0:T(8,128)}) custom-call(bf16[128,512]{1,0:T(8,128)(2,1)} %q_ref.3, s32[1,1536]{1,0:T(1,128)} %slice.45.pos_ref, bf16[1536,512]{1,0:T(8,128)(2,1)} %bitcast.29, bf16[1536,512]{1,0:T(8,128)(2,1)} %bitcast.30, ...), custom_call_target="tpu_custom_call" | custom-call | tf_op jit(solution)/shard_map/pallas_call | solution.py:162
  72.8 30.1 %psum.7.logits_ref = f32[8,128]{1,0:T(8,128)} all-reduce(f32[8,128]{1,0:T(8,128)S(1)} %bitcast.36), channel_id=1, replica_groups=mesh['z'=8,'ylo'=2,'x'=4,'tp'=8] {'tp'}, use_global_device_ids=true, to_apply=%region_0.1 | all-reduce | flops 1024 | bytes 8192 | tf_op jit(solution)/shard_map/psum | solution.py:285
  102.9 0.0 all-to-all-done
  102.9 0.0 copy-start.1
  102.9 1.5 %copy-done.1 = bf16[8,320,512]{2,1,0:T(8,128)(2,1)} copy-done((bf16[8,320,512]{2,1,0:T(8,128)(2,1)}, bf16[8,320,512]{2,1,0:T(8,128)(2,1)S(1)}, u32[]{:S(2)}) %copy-start.1) | copy-done | bytes 2621464
  104.4 5.2 %shard_map.92 = bf16[128,512]{1,0:T(8,128)(2,1)} custom-call(bf16[128,512]{1,0:T(8,128)(2,1)} %q_ref.3, s32[1,2560]{1,0:T(1,128)} %slice.40.pos_ref, bf16[2560,512]{1,0:T(8,128)(2,1)} %bitcast.27, bf16[2560,512]{1,0:T(8,128)(2,1)} %bitcast.28, f32[2,256,128]{2,1,0:T(8,128)} %get-tuple-element.15.acc_ref, f32[2,256,128]{2,1,0:T(8,128)} %get-tuple-element.16.top_ref, ...), custom_call_target="tpu_custom_call" | custom-call | tf_op jit(solution)/shard_map/pallas_call | solution.py:199
  (24 shorter events, 0.3 us)
Async XLA Ops:
  0.0 67.8 %copy-start = (bf16[128,256]{1,0:T(8,128)(2,1)S(1)}, bf16[128,256]{1,0:T(8,128)(2,1)}, u32[]{:S(2)}) copy-start(bf16[128,256]{1,0:T(8,128)(2,1)} %param.15) | copy-start | bytes 196612
  1.0 9.1 %collective-permute-start = (bf16[2,64,512]{2,1,0:T(8,128)(2,1)S(1)}, bf16[2,64,512]{2,1,0:T(8,128)(2,1)S(1)}, u32[]{:S(2)}, u32[]{:S(2)}) collective-permute-start(bf16[2,64,512]{2,1,0:T(8,128)(2,1)S(1)} %reshape.101), channel_id=1, source_target_pairs={{0,448},{64,0},{128,64},{192,128},{256,192},{320,256},{384,320},{4... | collective-permute-start | bytes 393224 | tf_op jit(solution)/shard_map/ppermute | solution.py:233
  3.0 7.1 %collective-permute-start.1 = (bf16[2,64,512]{2,1,0:T(8,128)(2,1)S(1)}, bf16[2,64,512]{2,1,0:T(8,128)(2,1)S(1)}, u32[]{:S(2)}, u32[]{:S(2)}) collective-permute-start(bf16[2,64,512]{2,1,0:T(8,128)(2,1)S(1)} %reshape.101), channel_id=1, source_target_pairs={{0,64},{64,128},{128,192},{192,256},{256,320},{320,384},{384,448},... | collective-permute-start | bytes 393224 | tf_op jit(solution)/shard_map/ppermute | solution.py:233
  11.5 43.2 %all-to-all-start.1 = ((bf16[8,192,512]{2,1,0:T(8,128)(2,1)}), bf16[8,192,512]{2,1,0:T(8,128)(2,1)S(1)}, u32[]{:S(2)}, u32[]{:S(2)}) async-start(bf16[8,192,512]{2,1,0:T(8,128)(2,1)} %broadcast_select_fusion.1), calls=%async_computation.1 | async-start | bytes 3145728 | tf_op jit(solution)/shard_map/all_to_all | solution.py:257
  17.9 25.4 %collective-permute-start.2 = (bf16[2,160,512]{2,1,0:T(8,128)(2,1)S(1)}, bf16[2,160,512]{2,1,0:T(8,128)(2,1)S(1)}, u32[]{:S(2)}, u32[]{:S(2)}) collective-permute-start(bf16[2,160,512]{2,1,0:T(8,128)(2,1)S(1)} %get-tuple-element.24), channel_id=1, source_target_pairs={{0,192},{64,256},{128,320},{192,384},{256,448},{320,0},{384,64},{4... | collective-permute-start | bytes 983048 | tf_op jit(solution)/shard_map/ppermute | solution.py:233
  25.8 27.0 %collective-permute-start.3 = (bf16[2,160,512]{2,1,0:T(8,128)(2,1)S(1)}, bf16[2,160,512]{2,1,0:T(8,128)(2,1)S(1)}, u32[]{:S(2)}, u32[]{:S(2)}) collective-permute-start(bf16[2,160,512]{2,1,0:T(8,128)(2,1)S(1)} %get-tuple-element.23), channel_id=1, source_target_pairs={{0,320},{64,384},{128,448},{192,0},{256,64},{320,128},{384,192},{4... | collective-permute-start | bytes 983048 | tf_op jit(solution)/shard_map/ppermute | solution.py:233
  54.7 8.9 %copy-start.7 = (s32[64]{0:T(128)S(1)}, s32[64]{0:T(128)}, u32[]{:S(2)}) copy-start(s32[64]{0:T(128)} %param.14) | copy-start | bytes 772
  54.7 11.1 %copy-start.5 = (bf16[2,4,2,256]{3,2,1,0:T(2,128)(2,1)S(1)}, bf16[2,4,2,256]{3,2,1,0:T(2,128)(2,1)}, u32[]{:S(2)}) copy-start(bf16[2,4,2,256]{3,2,1,0:T(2,128)(2,1)} %param.12) | copy-start | bytes 24580
  54.7 11.2 %copy-start.3 = (bf16[128,2,256]{2,1,0:T(2,128)(2,1)S(1)}, bf16[128,2,256]{2,1,0:T(2,128)(2,1)}, u32[]{:S(2)}) copy-start(bf16[128,2,256]{2,1,0:T(2,128)(2,1)} %param.10) | copy-start | bytes 393220
  54.7 12.5 %copy-start.6 = (s32[128,2]{0,1:T(2,128)S(1)}, s32[128,2]{0,1:T(2,128)}, u32[]{:S(2)}) copy-start(s32[128,2]{0,1:T(2,128)} %param.17) | copy-start | bytes 3076
  54.7 13.1 %copy-start.4 = (bf16[256,8]{0,1:T(8,128)(2,1)S(1)}, bf16[256,8]{0,1:T(8,128)(2,1)}, u32[]{:S(2)}) copy-start(bf16[256,8]{0,1:T(8,128)(2,1)} %param.16) | copy-start | bytes 12292
  54.8 1.1 %copy-start.2 = (bf16[8,192,512]{2,1,0:T(8,128)(2,1)}, bf16[8,192,512]{2,1,0:T(8,128)(2,1)S(1)}, u32[]{:S(2)}) copy-start(bf16[8,192,512]{2,1,0:T(8,128)(2,1)S(1)} %all-to-all-done.1) | copy-start | bytes 4718596
  55.9 47.0 %all-to-all-start = ((bf16[8,320,512]{2,1,0:T(8,128)(2,1)}), bf16[8,320,512]{2,1,0:T(8,128)(2,1)S(1)}, u32[]{:S(2)}, u32[]{:S(2)}) async-start(bf16[8,320,512]{2,1,0:T(8,128)(2,1)} %broadcast_select_fusion), calls=%async_computation | async-start | bytes 5242880 | tf_op jit(solution)/shard_map/all_to_all | solution.py:257
  102.9 1.5 %copy-start.1 = (bf16[8,320,512]{2,1,0:T(8,128)(2,1)}, bf16[8,320,512]{2,1,0:T(8,128)(2,1)S(1)}, u32[]{:S(2)}) copy-start(bf16[8,320,512]{2,1,0:T(8,128)(2,1)S(1)} %all-to-all-done) | copy-start | bytes 7864324

commit v12 on v11

--- a/solution.py
+++ b/solution.py
@@ -26,7 +26,7 @@
     for c in range(wk_ref.shape[0] // CHUNK):
         keys = wk_ref[pl.ds(c * CHUNK, CHUNK), :]
         s = lax.dot_general(q_stack, keys, nt, preferred_element_type=jnp.float32) * scale
-        if (c * CHUNK) // stride * per_device < rows:
+        if stride is None or (c * CHUNK) // stride * per_device < rows:
             key_pos = pos_ref[:, pl.ds(c * CHUNK, CHUNK)]
             s = jnp.where(key_pos > query_pos, s, -jnp.inf)
         score_ref[:, pl.ds(c * CHUNK, CHUNK)] = s
@@ -161,7 +161,7 @@
 
     acc, top, total = pl.pallas_call(
         functools.partial(
-            first_kernel, extra_sinks=extra_sinks, per_device=per_device, stride=plane_rows[0]
+            first_kernel, extra_sinks=extra_sinks, per_device=per_device, stride=None
         ),
         grid=(head_count,),
         in_specs=[
@@ -237,7 +237,8 @@
     down = shifted(local, z_count - 1)
     far_up = shifted(jnp.concatenate([down, local, up[:, :half]], axis=1), 3)
     far_down = shifted(jnp.concatenate([local, up, down[:, half:]], axis=1), z_count - 3)
-    near_pieces = ((0, 0, per_device), (1, 0, per_device), (z_count - 1, 0, per_device))
+    own_pieces = ((0, 0, per_device),)
+    near_pieces = ((1, 0, per_device), (z_count - 1, 0, per_device))
     far_pieces = (
         (2, 0, per_device),
         (3, 0, per_device),
@@ -246,8 +247,12 @@
         (z_count - 2, 0, per_device),
         (4, half, per_device - half),
     )
-    part_pieces = (near_pieces, far_pieces)
-    part_data = (jnp.concatenate([local, up, down], axis=1), jnp.concatenate([far_up, far_down], axis=1))
+    part_pieces = (own_pieces, near_pieces, far_pieces)
+    part_data = (
+        local,
+        jnp.concatenate([up, down], axis=1),
+        jnp.concatenate([far_up, far_down], axis=1),
+    )
     peer_groups = lax.dynamic_slice_in_dim(group_ids, z_me * plane_count, plane_count)
     plane_ids = jnp.arange(plane_count, dtype=jnp.int32)
     parts = []
@@ -279,7 +284,8 @@
         axis=0,
     )
     key_pos = jnp.concatenate(positions).reshape(1, -1)
-    plane_rows = tuple(data.shape[1] for data in part_data)
+    parts = [jnp.concatenate(parts[:2], axis=0), parts[2]]
+    plane_rows = (None, part_data[2].shape[1])
     state = attend_first(queries, key_pos, parts, plane_rows, extra, head_count, sink_count, per_device)
     state, partial_value = lax.optimization_barrier((state, partial_value))
     logits = lax.psum(partial_value, "tp")

time: 110 us -> 113 us (1.027)
  the two profiles are of different devices: /device:TPU:142 before, /device:TPU:14 now
where the time goes in v12:
time: 113 us
  starting transfers between devices  38.8 us (34%)
  blocking collectives  23.3 us (21%)
  waiting for transfers between devices  22.5 us (20%)
  other arithmetic  9.59 us (8%)
  Pallas kernels  9.15 us (8%)
  local copies, waits for them, and re-layouts  6.81 us (6%)
  between operations  2.61 us (2%)
    psum x1, blocking collectives, body(): logits = lax.psum(partial_value, 'tp')  23.3 us
    ppermute x4, waiting for transfers between devices, shifted(): return lax.ppermute(value, 'z', pairs)  22.5 us
    all_to_all x3, starting transfers between devices, body(): lax.all_to_all(outgoing, ('ylo', 'x'), split_axis=0, concat_axis=0, tiled...  20.6 us
    ppermute x4, starting transfers between devices, shifted(): return lax.ppermute(value, 'z', pairs)  18.2 us
    pallas_call x1, Pallas kernels, attend_second(): pl.pallas_call(functools.partial(second_kernel, per_device=per_device, st...  5.2 us
    pallas_call x1, Pallas kernels, attend_first(): pl.pallas_call(functools.partial(first_kernel, extra_sinks=extra_sinks, p...  3.94 us
    select_n x3, other arithmetic, body(): jnp.where((peer_groups == 0)[:, None, None], data[None, 0], data[None, 1])  3.86 us
    unnamed x23, local copies, waits for them, and re-layouts  2.61 us
  transfers between devices with their start and end apart: 7, of which 4 were waited for; matrix products, arithmetic and copies ran while one was open for 10% of the time, Pallas kernels for 3%

profile of v12, /device:TPU:14, one launch (start us, length us, event | category | flops | bytes accessed | tf_op | source)
XLA Modules:
  0.0 112.9 jit_solution(8127525511476450491)
XLA Ops:
  0.0 0.0 copy-start
  0.0 1.0 fusion.2
  1.0 0.7 dynamic-slice_compare_fusion
  1.8 0.9 broadcast_select_fusion.2
  2.7 9.2 %all-to-all-start.1 = ((bf16[8,64,512]{2,1,0:T(8,128)(2,1)}), bf16[8,64,512]{2,1,0:T(8,128)(2,1)S(1)}, u32[]{:S(2)}, u32[]{:S(2)}) async-start(bf16[8,64,512]{2,1,0:T(8,128)(2,1)} %broadcast_select_fusion.2), calls=%async_computation.1 | async-start | bytes 1048576 | tf_op jit(solution)/shard_map/all_to_all | solution.py:262
  11.9 1.0 reshape.112
  12.9 1.9 %collective-permute-start.1 = (bf16[2,64,512]{2,1,0:T(8,128)(2,1)S(1)}, bf16[2,64,512]{2,1,0:T(8,128)(2,1)S(1)}, u32[]{:S(2)}, u32[]{:S(2)}) collective-permute-start(bf16[2,64,512]{2,1,0:T(8,128)(2,1)S(1)} %reshape.112), channel_id=1, source_target_pairs={{0,64},{64,128},{128,192},{192,256},{256,320},{320,384},{384,448},... | collective-permute-start | bytes 393224 | tf_op jit(solution)/shard_map/ppermute | solution.py:233
  14.8 7.5 %collective-permute-start = (bf16[2,64,512]{2,1,0:T(8,128)(2,1)S(1)}, bf16[2,64,512]{2,1,0:T(8,128)(2,1)S(1)}, u32[]{:S(2)}, u32[]{:S(2)}) collective-permute-start(bf16[2,64,512]{2,1,0:T(8,128)(2,1)S(1)} %reshape.112), channel_id=1, source_target_pairs={{0,448},{64,0},{128,64},{192,128},{256,192},{320,256},{384,320},{4... | collective-permute-start | bytes 393224 | tf_op jit(solution)/shard_map/ppermute | solution.py:233
  22.2 1.0 collective-permute-done.1
  23.3 1.5 %collective-permute-done = bf16[2,64,512]{2,1,0:T(8,128)(2,1)S(1)} collective-permute-done((bf16[2,64,512]{2,1,0:T(8,128)(2,1)S(1)}, bf16[2,64,512]{2,1,0:T(8,128)(2,1)S(1)}, u32[]{:S(2)}, u32[]{:S(2)}) %collective-permute-start) | collective-permute-done | bytes 131104 | tf_op jit(solution)/shard_map/ppermute | solution.py:233
  24.8 1.1 broadcast_select_fusion.1
  25.9 0.0 all-to-all-done.1
  25.9 5.7 %all-to-all-start.2 = ((bf16[8,128,512]{2,1,0:T(8,128)(2,1)}), bf16[8,128,512]{2,1,0:T(8,128)(2,1)S(1)}, u32[]{:S(2)}, u32[]{:S(2)}) async-start(bf16[8,128,512]{2,1,0:T(8,128)(2,1)} %broadcast_select_fusion.1), calls=%async_computation.2 | async-start | bytes 2097152 | tf_op jit(solution)/shard_map/all_to_all | solution.py:262
  31.6 0.1 pad_maximum_fusion.2
  31.7 6.1 %collective-permute-start.2 = (bf16[2,160,512]{2,1,0:T(8,128)(2,1)S(1)}, bf16[2,160,512]{2,1,0:T(8,128)(2,1)S(1)}, u32[]{:S(2)}, u32[]{:S(2)}) collective-permute-start(bf16[2,160,512]{2,1,0:T(8,128)(2,1)S(1)} %get-tuple-element.26), channel_id=1, source_target_pairs={{0,192},{64,256},{128,320},{192,384},{256,448},{320,0},{384,64},{4... | collective-permute-start | bytes 983048 | tf_op jit(solution)/shard_map/ppermute | solution.py:233
  37.8 2.8 %collective-permute-start.3 = (bf16[2,160,512]{2,1,0:T(8,128)(2,1)S(1)}, bf16[2,160,512]{2,1,0:T(8,128)(2,1)S(1)}, u32[]{:S(2)}, u32[]{:S(2)}) collective-permute-start(bf16[2,160,512]{2,1,0:T(8,128)(2,1)S(1)} %get-tuple-element.25), channel_id=1, source_target_pairs={{0,320},{64,384},{128,448},{192,0},{256,64},{320,128},{384,192},{4... | collective-permute-start | bytes 983048 | tf_op jit(solution)/shard_map/ppermute | solution.py:233
  40.6 15.8 %collective-permute-done.2 = bf16[2,160,512]{2,1,0:T(8,128)(2,1)S(1)} collective-permute-done((bf16[2,160,512]{2,1,0:T(8,128)(2,1)S(1)}, bf16[2,160,512]{2,1,0:T(8,128)(2,1)S(1)}, u32[]{:S(2)}, u32[]{:S(2)}) %collective-permute-start.2) | collective-permute-done | bytes 327712 | tf_op jit(solution)/shard_map/ppermute | solution.py:233
  56.4 4.2 %collective-permute-done.3 = bf16[2,160,512]{2,1,0:T(8,128)(2,1)S(1)} collective-permute-done((bf16[2,160,512]{2,1,0:T(8,128)(2,1)S(1)}, bf16[2,160,512]{2,1,0:T(8,128)(2,1)S(1)}, u32[]{:S(2)}, u32[]{:S(2)}) %collective-permute-start.3) | collective-permute-done | bytes 327712 | tf_op jit(solution)/shard_map/ppermute | solution.py:233
  60.6 1.8 %broadcast_select_fusion = bf16[8,320,512]{2,1,0:T(8,128)(2,1)} fusion(pred[8]{0:T(512)(128)(4,1)S(1)} %dynamic-slice_compare_fusion, bf16[320,512]{1,0:T(8,128)(2,1)S(1)} %get-tuple-element.20, bf16[320,512]{1,0:T(8,128)(2,1)S(1)} %get-tuple-element.19), kind=kLoop, calls=%fused_computation | loop fusion | flops 1310720 | bytes 3276808 | tf_op jit(solution)/shard_map/jit(_where)/select_n | solution.py:261
  62.5 0.0 copy-start.7
  62.5 0.0 copy-start.5
  62.5 0.0 copy-start.3
  62.5 0.0 copy-start.6
  62.5 0.0 copy-start.4
  62.5 0.0 all-to-all-done.2
  62.5 0.0 copy-start.2
  62.5 1.0 copy-done.2
  63.5 5.7 %all-to-all-start = ((bf16[8,320,512]{2,1,0:T(8,128)(2,1)}), bf16[8,320,512]{2,1,0:T(8,128)(2,1)S(1)}, u32[]{:S(2)}, u32[]{:S(2)}) async-start(bf16[8,320,512]{2,1,0:T(8,128)(2,1)} %broadcast_select_fusion), calls=%async_computation | async-start | bytes 5242880 | tf_op jit(solution)/shard_map/all_to_all | solution.py:262
  69.3 0.1 iota_add_fusion.3
  69.4 0.1 broadcast_add_fusion
  69.4 0.1 iota_add_fusion
  69.5 0.1 concatenate.28
  69.6 0.1 reshape.110
  69.7 0.1 iota_add_fusion.7
  69.7 0.1 add.276
  69.8 0.1 iota_add_fusion.5
  69.9 0.1 add_bitcast_fusion
  70.0 0.6 slice.50.pos_ref
  70.6 0.6 slice.55.pos_ref
  71.2 0.0 copy-done.7
  71.2 0.6 dynamic_slice.11
  73.5 0.0 copy-done.5
  73.6 0.0 copy-done.3
  74.3 0.1 pad.2.clone
  74.3 0.5 compare_convert_fusion.live_ref
  74.9 0.0 copy-done.6
  74.9 0.6 fusion
  75.5 0.0 copy-done
  75.5 0.0 copy-done.4
  75.5 0.1 fusion.3
  75.6 0.8 maximum_maximum_fusion.xk_ref.xv_ref
  76.4 2.5 %pad_maximum_fusion.wk_ref.wv_ref = bf16[1536,512]{1,0:T(8,128)(2,1)} fusion(bf16[1024,512]{1,0:T(8,128)(2,1)} %bitcast.38, bf16[512,512]{1,0:T(8,128)(2,1)S(1)} %bitcast.39), kind=kLoop, calls=%fused_computation.1 | loop fusion | flops 3145728 | bytes 3145728 | tf_op jit(solution)/shard_map/concatenate | solution.py:287
  78.9 3.9 %shard_map.91 = (f32[2,256,128]{2,1,0:T(8,128)}, f32[2,256,128]{2,1,0:T(8,128)}, f32[2,256,128]{2,1,0:T(8,128)}) custom-call(bf16[128,512]{1,0:T(8,128)(2,1)} %q_ref.3, s32[1,1536]{1,0:T(1,128)} %slice.55.pos_ref, bf16[1536,512]{1,0:T(8,128)(2,1)} %pad_maximum_fusion.wk_ref.wv_ref, bf16[1536,512]{1,0:T(8,128)(2,1)} %pad_maximum_fusion.wk_ref.wv_ref, ...), custom_call_target="tpu_custom_call" | custom-call | tf_op jit(solution)/shard_map/pallas_call | solution.py:162
  82.8 23.3 %psum.7.logits_ref = f32[8,128]{1,0:T(8,128)} all-reduce(f32[8,128]{1,0:T(8,128)S(1)} %bitcast.49), channel_id=1, replica_groups=mesh['z'=8,'ylo'=2,'x'=4,'tp'=8] {'tp'}, use_global_device_ids=true, to_apply=%region_0.1 | all-reduce | flops 1024 | bytes 8192 | tf_op jit(solution)/shard_map/psum | solution.py:291
  106.2 0.0 all-to-all-done
  106.2 0.0 copy-start.1
  106.2 1.5 %copy-done.1 = bf16[8,320,512]{2,1,0:T(8,128)(2,1)} copy-done((bf16[8,320,512]{2,1,0:T(8,128)(2,1)}, bf16[8,320,512]{2,1,0:T(8,128)(2,1)S(1)}, u32[]{:S(2)}) %copy-start.1) | copy-done | bytes 2621464
  107.7 5.2 %shard_map.92 = bf16[128,512]{1,0:T(8,128)(2,1)} custom-call(bf16[128,512]{1,0:T(8,128)(2,1)} %q_ref.3, s32[1,2560]{1,0:T(1,128)} %slice.50.pos_ref, bf16[2560,512]{1,0:T(8,128)(2,1)} %bitcast.36, bf16[2560,512]{1,0:T(8,128)(2,1)} %bitcast.37, f32[2,256,128]{2,1,0:T(8,128)} %get-tuple-element.15.acc_ref, f32[2,256,128]{2,1,0:T(8,128)} %get-tuple-element.16.top_ref, ...), custom_call_target="tpu_custom_call" | custom-call | tf_op jit(solution)/shard_map/pallas_call | solution.py:199
  (25 shorter events, 0.3 us)
Async XLA Ops:
  0.0 75.5 %copy-start = (bf16[128,256]{1,0:T(8,128)(2,1)S(1)}, bf16[128,256]{1,0:T(8,128)(2,1)}, u32[]{:S(2)}) copy-start(bf16[128,256]{1,0:T(8,128)(2,1)} %param.15) | copy-start | bytes 196612
  2.7 23.2 %all-to-all-start.1 = ((bf16[8,64,512]{2,1,0:T(8,128)(2,1)}), bf16[8,64,512]{2,1,0:T(8,128)(2,1)S(1)}, u32[]{:S(2)}, u32[]{:S(2)}) async-start(bf16[8,64,512]{2,1,0:T(8,128)(2,1)} %broadcast_select_fusion.2), calls=%async_computation.1 | async-start | bytes 1048576 | tf_op jit(solution)/shard_map/all_to_all | solution.py:262
  12.9 10.4 %collective-permute-start.1 = (bf16[2,64,512]{2,1,0:T(8,128)(2,1)S(1)}, bf16[2,64,512]{2,1,0:T(8,128)(2,1)S(1)}, u32[]{:S(2)}, u32[]{:S(2)}) collective-permute-start(bf16[2,64,512]{2,1,0:T(8,128)(2,1)S(1)} %reshape.112), channel_id=1, source_target_pairs={{0,64},{64,128},{128,192},{192,256},{256,320},{320,384},{384,448},... | collective-permute-start | bytes 393224 | tf_op jit(solution)/shard_map/ppermute | solution.py:233
  14.8 10.0 %collective-permute-start = (bf16[2,64,512]{2,1,0:T(8,128)(2,1)S(1)}, bf16[2,64,512]{2,1,0:T(8,128)(2,1)S(1)}, u32[]{:S(2)}, u32[]{:S(2)}) collective-permute-start(bf16[2,64,512]{2,1,0:T(8,128)(2,1)S(1)} %reshape.112), channel_id=1, source_target_pairs={{0,448},{64,0},{128,64},{192,128},{256,192},{320,256},{384,320},{4... | collective-permute-start | bytes 393224 | tf_op jit(solution)/shard_map/ppermute | solution.py:233
  25.9 36.6 %all-to-all-start.2 = ((bf16[8,128,512]{2,1,0:T(8,128)(2,1)}), bf16[8,128,512]{2,1,0:T(8,128)(2,1)S(1)}, u32[]{:S(2)}, u32[]{:S(2)}) async-start(bf16[8,128,512]{2,1,0:T(8,128)(2,1)} %broadcast_select_fusion.1), calls=%async_computation.2 | async-start | bytes 2097152 | tf_op jit(solution)/shard_map/all_to_all | solution.py:262
  31.7 24.7 %collective-permute-start.2 = (bf16[2,160,512]{2,1,0:T(8,128)(2,1)S(1)}, bf16[2,160,512]{2,1,0:T(8,128)(2,1)S(1)}, u32[]{:S(2)}, u32[]{:S(2)}) collective-permute-start(bf16[2,160,512]{2,1,0:T(8,128)(2,1)S(1)} %get-tuple-element.26), channel_id=1, source_target_pairs={{0,192},{64,256},{128,320},{192,384},{256,448},{320,0},{384,64},{4... | collective-permute-start | bytes 983048 | tf_op jit(solution)/shard_map/ppermute | solution.py:233
  37.8 22.8 %collective-permute-start.3 = (bf16[2,160,512]{2,1,0:T(8,128)(2,1)S(1)}, bf16[2,160,512]{2,1,0:T(8,128)(2,1)S(1)}, u32[]{:S(2)}, u32[]{:S(2)}) collective-permute-start(bf16[2,160,512]{2,1,0:T(8,128)(2,1)S(1)} %get-tuple-element.25), channel_id=1, source_target_pairs={{0,320},{64,384},{128,448},{192,0},{256,64},{320,128},{384,192},{4... | collective-permute-start | bytes 983048 | tf_op jit(solution)/shard_map/ppermute | solution.py:233
  62.5 8.7 %copy-start.7 = (s32[64]{0:T(128)S(1)}, s32[64]{0:T(128)}, u32[]{:S(2)}) copy-start(s32[64]{0:T(128)} %param.14) | copy-start | bytes 772
  62.5 11.0 %copy-start.5 = (bf16[2,4,2,256]{3,2,1,0:T(2,128)(2,1)S(1)}, bf16[2,4,2,256]{3,2,1,0:T(2,128)(2,1)}, u32[]{:S(2)}) copy-start(bf16[2,4,2,256]{3,2,1,0:T(2,128)(2,1)} %param.12) | copy-start | bytes 24580
  62.5 11.1 %copy-start.3 = (bf16[128,2,256]{2,1,0:T(2,128)(2,1)S(1)}, bf16[128,2,256]{2,1,0:T(2,128)(2,1)}, u32[]{:S(2)}) copy-start(bf16[128,2,256]{2,1,0:T(2,128)(2,1)} %param.10) | copy-start | bytes 393220
  62.5 12.4 %copy-start.6 = (s32[128,2]{0,1:T(2,128)S(1)}, s32[128,2]{0,1:T(2,128)}, u32[]{:S(2)}) copy-start(s32[128,2]{0,1:T(2,128)} %param.17) | copy-start | bytes 3076
  62.5 13.0 %copy-start.4 = (bf16[256,8]{0,1:T(8,128)(2,1)S(1)}, bf16[256,8]{0,1:T(8,128)(2,1)}, u32[]{:S(2)}) copy-start(bf16[256,8]{0,1:T(8,128)(2,1)} %param.16) | copy-start | bytes 12292
  62.5 1.0 copy-start.2
  63.5 42.7 %all-to-all-start = ((bf16[8,320,512]{2,1,0:T(8,128)(2,1)}), bf16[8,320,512]{2,1,0:T(8,128)(2,1)S(1)}, u32[]{:S(2)}, u32[]{:S(2)}) async-start(bf16[8,320,512]{2,1,0:T(8,128)(2,1)} %broadcast_select_fusion), calls=%async_computation | async-start | bytes 5242880 | tf_op jit(solution)/shard_map/all_to_all | solution.py:262
  106.2 1.5 %copy-start.1 = (bf16[8,320,512]{2,1,0:T(8,128)(2,1)}, bf16[8,320,512]{2,1,0:T(8,128)(2,1)S(1)}, u32[]{:S(2)}) copy-start(bf16[8,320,512]{2,1,0:T(8,128)(2,1)S(1)} %all-to-all-done) | copy-start | bytes 7864324

commit v13 on v11

--- a/solution.py
+++ b/solution.py
@@ -22,7 +22,7 @@
     stacked = q_stack.shape[0]
     query_pos = lax.broadcasted_iota(jnp.int32, (stacked, 1), 0) % rows
     nt = (((1,), (1,)), ((), ()))
-    top = jnp.full((stacked, 1), -jnp.inf, jnp.float32)
+    lane_top = jnp.full((stacked, HEAD_DIM), -jnp.inf, jnp.float32)
     for c in range(wk_ref.shape[0] // CHUNK):
         keys = wk_ref[pl.ds(c * CHUNK, CHUNK), :]
         s = lax.dot_general(q_stack, keys, nt, preferred_element_type=jnp.float32) * scale
@@ -30,20 +30,23 @@
             key_pos = pos_ref[:, pl.ds(c * CHUNK, CHUNK)]
             s = jnp.where(key_pos > query_pos, s, -jnp.inf)
         score_ref[:, pl.ds(c * CHUNK, CHUNK)] = s
-        top = jnp.maximum(top, jnp.max(s, axis=1, keepdims=True))
-    return top
+        for j in range(CHUNK // HEAD_DIM):
+            lane_top = jnp.maximum(lane_top, s[:, j * HEAD_DIM : (j + 1) * HEAD_DIM])
+    return jnp.max(lane_top, axis=1, keepdims=True)
 
 
 def window_sums(wv_ref, score_ref, top, total, acc):
+    lane_total = jnp.zeros((top.shape[0], HEAD_DIM), jnp.float32)
     for c in range(wv_ref.shape[0] // CHUNK):
         e = jnp.exp(score_ref[:, pl.ds(c * CHUNK, CHUNK)] - top)
-        total = total + jnp.sum(e, axis=1, keepdims=True)
+        for j in range(CHUNK // HEAD_DIM):
+            lane_total = lane_total + e[:, j * HEAD_DIM : (j + 1) * HEAD_DIM]
         acc = acc + jnp.dot(
             e.astype(jnp.bfloat16),
             wv_ref[pl.ds(c * CHUNK, CHUNK), :],
             preferred_element_type=jnp.float32,
         )
-    return total, acc
+    return total + jnp.sum(lane_total, axis=1, keepdims=True), acc
 
 
 def first_kernel(

time: 110 us -> 110 us (level)
  no operation moved by 1% of the time
where the time goes in v13:
time: 110 us
  blocking collectives  30 us (27%)
  starting transfers between devices  29.1 us (26%)
  waiting for transfers between devices  26 us (24%)
  Pallas kernels  9.38 us (9%)
  other arithmetic  6.43 us (6%)
  local copies, waits for them, and re-layouts  5.98 us (5%)
  between operations  2.58 us (2%)
    psum x1, blocking collectives, body(): logits = lax.psum(partial_value, 'tp')  30 us
    ppermute x4, waiting for transfers between devices, shifted(): return lax.ppermute(value, 'z', pairs)  26 us
    ppermute x4, starting transfers between devices, shifted(): return lax.ppermute(value, 'z', pairs)  17.2 us
    all_to_all x2, starting transfers between devices, body(): lax.all_to_all(outgoing, ('ylo', 'x'), split_axis=0, concat_axis=0, tiled...  12 us
    pallas_call x1, Pallas kernels, attend_second(): pl.pallas_call(functools.partial(second_kernel, per_device=per_device, st...  5.27 us
    pallas_call x1, Pallas kernels, attend_first(): pl.pallas_call(functools.partial(first_kernel, extra_sinks=extra_sinks, p...  4.12 us
    select_n x2, other arithmetic, body(): jnp.where((peer_groups == 0)[:, None, None], data[None, 0], data[None, 1])  3.19 us
    unnamed x22, local copies, waits for them, and re-layouts  2.73 us
  transfers between devices with their start and end apart: 6, of which 3 were waited for; matrix products, arithmetic and copies ran while one was open for 7% of the time, Pallas kernels for 4%

profile of v13, /device:TPU:142, one launch (start us, length us, event | category | flops | bytes accessed | tf_op | source)
XLA Modules:
  0.0 109.7 jit_solution(919608792408853020)
XLA Ops:
  0.0 0.0 copy-start
  0.0 1.0 reshape.101
  1.0 1.9 %collective-permute-start = (bf16[2,64,512]{2,1,0:T(8,128)(2,1)S(1)}, bf16[2,64,512]{2,1,0:T(8,128)(2,1)S(1)}, u32[]{:S(2)}, u32[]{:S(2)}) collective-permute-start(bf16[2,64,512]{2,1,0:T(8,128)(2,1)S(1)} %reshape.101), channel_id=1, source_target_pairs={{0,448},{64,0},{128,64},{192,128},{256,192},{320,256},{384,320},{4... | collective-permute-start | bytes 393224 | tf_op jit(solution)/shard_map/ppermute | solution.py:236
  3.0 4.3 %collective-permute-start.1 = (bf16[2,64,512]{2,1,0:T(8,128)(2,1)S(1)}, bf16[2,64,512]{2,1,0:T(8,128)(2,1)S(1)}, u32[]{:S(2)}, u32[]{:S(2)}) collective-permute-start(bf16[2,64,512]{2,1,0:T(8,128)(2,1)S(1)} %reshape.101), channel_id=1, source_target_pairs={{0,64},{64,128},{128,192},{192,256},{256,320},{320,384},{384,448},... | collective-permute-start | bytes 393224 | tf_op jit(solution)/shard_map/ppermute | solution.py:236
  7.3 0.7 dynamic-slice_compare_fusion
  8.0 2.1 %collective-permute-done.1 = bf16[2,64,512]{2,1,0:T(8,128)(2,1)S(1)} collective-permute-done((bf16[2,64,512]{2,1,0:T(8,128)(2,1)S(1)}, bf16[2,64,512]{2,1,0:T(8,128)(2,1)S(1)}, u32[]{:S(2)}, u32[]{:S(2)}) %collective-permute-start.1) | collective-permute-done | bytes 131104 | tf_op jit(solution)/shard_map/ppermute | solution.py:236
  10.1 0.0 collective-permute-done
  10.2 1.3 %broadcast_select_fusion.1 = bf16[8,192,512]{2,1,0:T(8,128)(2,1)} fusion(pred[8]{0:T(512)(128)(4,1)S(1)} %dynamic-slice_compare_fusion, bf16[192,512]{1,0:T(8,128)(2,1)S(1)} %get-tuple-element.22, bf16[192,512]{1,0:T(8,128)(2,1)S(1)} %get-tuple-element.21), kind=kLoop, calls=%fused_computation.1 | loop fusion | flops 786432 | bytes 1966088 | tf_op jit(solution)/shard_map/jit(_where)/select_n | solution.py:259
  11.5 6.3 %all-to-all-start.1 = ((bf16[8,192,512]{2,1,0:T(8,128)(2,1)}), bf16[8,192,512]{2,1,0:T(8,128)(2,1)S(1)}, u32[]{:S(2)}, u32[]{:S(2)}) async-start(bf16[8,192,512]{2,1,0:T(8,128)(2,1)} %broadcast_select_fusion.1), calls=%async_computation.1 | async-start | bytes 3145728 | tf_op jit(solution)/shard_map/all_to_all | solution.py:260
  17.8 0.1 pad_maximum_fusion.1
  17.9 7.9 %collective-permute-start.2 = (bf16[2,160,512]{2,1,0:T(8,128)(2,1)S(1)}, bf16[2,160,512]{2,1,0:T(8,128)(2,1)S(1)}, u32[]{:S(2)}, u32[]{:S(2)}) collective-permute-start(bf16[2,160,512]{2,1,0:T(8,128)(2,1)S(1)} %get-tuple-element.24), channel_id=1, source_target_pairs={{0,192},{64,256},{128,320},{192,384},{256,448},{320,0},{384,64},{4... | collective-permute-start | bytes 983048 | tf_op jit(solution)/shard_map/ppermute | solution.py:236
  25.8 3.1 %collective-permute-start.3 = (bf16[2,160,512]{2,1,0:T(8,128)(2,1)S(1)}, bf16[2,160,512]{2,1,0:T(8,128)(2,1)S(1)}, u32[]{:S(2)}, u32[]{:S(2)}) collective-permute-start(bf16[2,160,512]{2,1,0:T(8,128)(2,1)S(1)} %get-tuple-element.23), channel_id=1, source_target_pairs={{0,320},{64,384},{128,448},{192,0},{256,64},{320,128},{384,192},{4... | collective-permute-start | bytes 983048 | tf_op jit(solution)/shard_map/ppermute | solution.py:236
  28.8 14.4 %collective-permute-done.2 = bf16[2,160,512]{2,1,0:T(8,128)(2,1)S(1)} collective-permute-done((bf16[2,160,512]{2,1,0:T(8,128)(2,1)S(1)}, bf16[2,160,512]{2,1,0:T(8,128)(2,1)S(1)}, u32[]{:S(2)}, u32[]{:S(2)}) %collective-permute-start.2) | collective-permute-done | bytes 327712 | tf_op jit(solution)/shard_map/ppermute | solution.py:236
  43.3 9.5 %collective-permute-done.3 = bf16[2,160,512]{2,1,0:T(8,128)(2,1)S(1)} collective-permute-done((bf16[2,160,512]{2,1,0:T(8,128)(2,1)S(1)}, bf16[2,160,512]{2,1,0:T(8,128)(2,1)S(1)}, u32[]{:S(2)}, u32[]{:S(2)}) %collective-permute-start.3) | collective-permute-done | bytes 327712 | tf_op jit(solution)/shard_map/ppermute | solution.py:236
  52.9 1.9 %broadcast_select_fusion = bf16[8,320,512]{2,1,0:T(8,128)(2,1)} fusion(pred[8]{0:T(512)(128)(4,1)S(1)} %dynamic-slice_compare_fusion, bf16[320,512]{1,0:T(8,128)(2,1)S(1)} %get-tuple-element.20, bf16[320,512]{1,0:T(8,128)(2,1)S(1)} %get-tuple-element.19), kind=kLoop, calls=%fused_computation | loop fusion | flops 1310720 | bytes 3276808 | tf_op jit(solution)/shard_map/jit(_where)/select_n | solution.py:259
  54.7 0.0 copy-start.7
  54.7 0.0 copy-start.5
  54.7 0.0 copy-start.3
  54.7 0.0 copy-start.6
  54.7 0.0 copy-start.4
  54.7 0.0 all-to-all-done.1
  54.8 0.0 copy-start.2
  54.8 1.1 %copy-done.2 = bf16[8,192,512]{2,1,0:T(8,128)(2,1)} copy-done((bf16[8,192,512]{2,1,0:T(8,128)(2,1)}, bf16[8,192,512]{2,1,0:T(8,128)(2,1)S(1)}, u32[]{:S(2)}) %copy-start.2) | copy-done | bytes 1572888
  55.9 5.7 %all-to-all-start = ((bf16[8,320,512]{2,1,0:T(8,128)(2,1)}), bf16[8,320,512]{2,1,0:T(8,128)(2,1)S(1)}, u32[]{:S(2)}, u32[]{:S(2)}) async-start(bf16[8,320,512]{2,1,0:T(8,128)(2,1)} %broadcast_select_fusion), calls=%async_computation | async-start | bytes 5242880 | tf_op jit(solution)/shard_map/all_to_all | solution.py:260
  61.7 0.1 iota_add_fusion.3
  61.7 0.1 broadcast_add_fusion
  61.8 0.1 iota_add_fusion
  61.9 0.1 concatenate.25
  62.0 0.1 reshape.99
  62.1 0.1 iota_add_fusion.7
  62.1 0.1 iota_add_fusion.5
  62.2 0.1 pad_add_fusion.1
  62.3 0.1 reshape.98
  62.4 0.6 slice.40.pos_ref
  63.0 0.6 slice.45.pos_ref
  63.6 0.0 copy-done.7
  63.6 0.6 dynamic_slice.11
  65.9 0.0 copy-done.5
  65.9 0.0 copy-done.3
  66.6 0.1 pad.2.clone
  66.7 0.5 compare_convert_fusion.live_ref
  67.2 0.0 copy-done.6
  67.2 0.6 fusion
  67.8 0.0 copy-done
  67.8 0.0 copy-done.4
  67.8 0.1 fusion.2
  67.9 0.8 maximum_maximum_fusion.xk_ref.xv_ref
  68.8 4.1 %shard_map.91 = (f32[2,256,128]{2,1,0:T(8,128)}, f32[2,256,128]{2,1,0:T(8,128)}, f32[2,256,128]{2,1,0:T(8,128)}) custom-call(bf16[128,512]{1,0:T(8,128)(2,1)} %q_ref.3, s32[1,1536]{1,0:T(1,128)} %slice.45.pos_ref, bf16[1536,512]{1,0:T(8,128)(2,1)} %bitcast.29, bf16[1536,512]{1,0:T(8,128)(2,1)} %bitcast.30, ...), custom_call_target="tpu_custom_call" | custom-call | tf_op jit(solution)/shard_map/pallas_call | solution.py:165
  72.9 30.0 %psum.7.logits_ref = f32[8,128]{1,0:T(8,128)} all-reduce(f32[8,128]{1,0:T(8,128)S(1)} %bitcast.36), channel_id=1, replica_groups=mesh['z'=8,'ylo'=2,'x'=4,'tp'=8] {'tp'}, use_global_device_ids=true, to_apply=%region_0.1 | all-reduce | flops 1024 | bytes 8192 | tf_op jit(solution)/shard_map/psum | solution.py:288
  102.9 0.0 all-to-all-done
  102.9 0.0 copy-start.1
  102.9 1.5 %copy-done.1 = bf16[8,320,512]{2,1,0:T(8,128)(2,1)} copy-done((bf16[8,320,512]{2,1,0:T(8,128)(2,1)}, bf16[8,320,512]{2,1,0:T(8,128)(2,1)S(1)}, u32[]{:S(2)}) %copy-start.1) | copy-done | bytes 2621464
  104.4 5.3 %shard_map.92 = bf16[128,512]{1,0:T(8,128)(2,1)} custom-call(bf16[128,512]{1,0:T(8,128)(2,1)} %q_ref.3, s32[1,2560]{1,0:T(1,128)} %slice.40.pos_ref, bf16[2560,512]{1,0:T(8,128)(2,1)} %bitcast.27, bf16[2560,512]{1,0:T(8,128)(2,1)} %bitcast.28, f32[2,256,128]{2,1,0:T(8,128)} %get-tuple-element.15.acc_ref, f32[2,256,128]{2,1,0:T(8,128)} %get-tuple-element.16.top_ref, ...), custom_call_target="tpu_custom_call" | custom-call | tf_op jit(solution)/shard_map/pallas_call | solution.py:202
  (24 shorter events, 0.3 us)
Async XLA Ops:
  0.0 67.8 %copy-start = (bf16[128,256]{1,0:T(8,128)(2,1)S(1)}, bf16[128,256]{1,0:T(8,128)(2,1)}, u32[]{:S(2)}) copy-start(bf16[128,256]{1,0:T(8,128)(2,1)} %param.15) | copy-start | bytes 196612
  1.0 9.1 %collective-permute-start = (bf16[2,64,512]{2,1,0:T(8,128)(2,1)S(1)}, bf16[2,64,512]{2,1,0:T(8,128)(2,1)S(1)}, u32[]{:S(2)}, u32[]{:S(2)}) collective-permute-start(bf16[2,64,512]{2,1,0:T(8,128)(2,1)S(1)} %reshape.101), channel_id=1, source_target_pairs={{0,448},{64,0},{128,64},{192,128},{256,192},{320,256},{384,320},{4... | collective-permute-start | bytes 393224 | tf_op jit(solution)/shard_map/ppermute | solution.py:236
  3.0 7.1 %collective-permute-start.1 = (bf16[2,64,512]{2,1,0:T(8,128)(2,1)S(1)}, bf16[2,64,512]{2,1,0:T(8,128)(2,1)S(1)}, u32[]{:S(2)}, u32[]{:S(2)}) collective-permute-start(bf16[2,64,512]{2,1,0:T(8,128)(2,1)S(1)} %reshape.101), channel_id=1, source_target_pairs={{0,64},{64,128},{128,192},{192,256},{256,320},{320,384},{384,448},... | collective-permute-start | bytes 393224 | tf_op jit(solution)/shard_map/ppermute | solution.py:236
  11.5 43.2 %all-to-all-start.1 = ((bf16[8,192,512]{2,1,0:T(8,128)(2,1)}), bf16[8,192,512]{2,1,0:T(8,128)(2,1)S(1)}, u32[]{:S(2)}, u32[]{:S(2)}) async-start(bf16[8,192,512]{2,1,0:T(8,128)(2,1)} %broadcast_select_fusion.1), calls=%async_computation.1 | async-start | bytes 3145728 | tf_op jit(solution)/shard_map/all_to_all | solution.py:260
  17.9 25.4 %collective-permute-start.2 = (bf16[2,160,512]{2,1,0:T(8,128)(2,1)S(1)}, bf16[2,160,512]{2,1,0:T(8,128)(2,1)S(1)}, u32[]{:S(2)}, u32[]{:S(2)}) collective-permute-start(bf16[2,160,512]{2,1,0:T(8,128)(2,1)S(1)} %get-tuple-element.24), channel_id=1, source_target_pairs={{0,192},{64,256},{128,320},{192,384},{256,448},{320,0},{384,64},{4... | collective-permute-start | bytes 983048 | tf_op jit(solution)/shard_map/ppermute | solution.py:236
  25.8 27.0 %collective-permute-start.3 = (bf16[2,160,512]{2,1,0:T(8,128)(2,1)S(1)}, bf16[2,160,512]{2,1,0:T(8,128)(2,1)S(1)}, u32[]{:S(2)}, u32[]{:S(2)}) collective-permute-start(bf16[2,160,512]{2,1,0:T(8,128)(2,1)S(1)} %get-tuple-element.23), channel_id=1, source_target_pairs={{0,320},{64,384},{128,448},{192,0},{256,64},{320,128},{384,192},{4... | collective-permute-start | bytes 983048 | tf_op jit(solution)/shard_map/ppermute | solution.py:236
  54.7 8.9 %copy-start.7 = (s32[64]{0:T(128)S(1)}, s32[64]{0:T(128)}, u32[]{:S(2)}) copy-start(s32[64]{0:T(128)} %param.14) | copy-start | bytes 772
  54.7 11.1 %copy-start.5 = (bf16[2,4,2,256]{3,2,1,0:T(2,128)(2,1)S(1)}, bf16[2,4,2,256]{3,2,1,0:T(2,128)(2,1)}, u32[]{:S(2)}) copy-start(bf16[2,4,2,256]{3,2,1,0:T(2,128)(2,1)} %param.12) | copy-start | bytes 24580
  54.7 11.2 %copy-start.3 = (bf16[128,2,256]{2,1,0:T(2,128)(2,1)S(1)}, bf16[128,2,256]{2,1,0:T(2,128)(2,1)}, u32[]{:S(2)}) copy-start(bf16[128,2,256]{2,1,0:T(2,128)(2,1)} %param.10) | copy-start | bytes 393220
  54.7 12.5 %copy-start.6 = (s32[128,2]{0,1:T(2,128)S(1)}, s32[128,2]{0,1:T(2,128)}, u32[]{:S(2)}) copy-start(s32[128,2]{0,1:T(2,128)} %param.17) | copy-start | bytes 3076
  54.7 13.1 %copy-start.4 = (bf16[256,8]{0,1:T(8,128)(2,1)S(1)}, bf16[256,8]{0,1:T(8,128)(2,1)}, u32[]{:S(2)}) copy-start(bf16[256,8]{0,1:T(8,128)(2,1)} %param.16) | copy-start | bytes 12292
  54.8 1.1 %copy-start.2 = (bf16[8,192,512]{2,1,0:T(8,128)(2,1)}, bf16[8,192,512]{2,1,0:T(8,128)(2,1)S(1)}, u32[]{:S(2)}) copy-start(bf16[8,192,512]{2,1,0:T(8,128)(2,1)S(1)} %all-to-all-done.1) | copy-start | bytes 4718596
  55.9 47.0 %all-to-all-start = ((bf16[8,320,512]{2,1,0:T(8,128)(2,1)}), bf16[8,320,512]{2,1,0:T(8,128)(2,1)S(1)}, u32[]{:S(2)}, u32[]{:S(2)}) async-start(bf16[8,320,512]{2,1,0:T(8,128)(2,1)} %broadcast_select_fusion), calls=%async_computation | async-start | bytes 5242880 | tf_op jit(solution)/shard_map/all_to_all | solution.py:260
  102.9 1.5 %copy-start.1 = (bf16[8,320,512]{2,1,0:T(8,128)(2,1)}, bf16[8,320,512]{2,1,0:T(8,128)(2,1)S(1)}, u32[]{:S(2)}) copy-start(bf16[8,320,512]{2,1,0:T(8,128)(2,1)S(1)} %all-to-all-done) | copy-start | bytes 7864324

commit v14 on v13

--- a/solution.py
+++ b/solution.py
@@ -114,15 +114,27 @@
     rows = q_ref.shape[0]
     scale = 1.0 / math.sqrt(HEAD_DIM)
     q_stack = stacked_queries(q_ref)
-    first_top = top_ref[:, 0:1]
-    top = jnp.maximum(
-        first_top,
-        window_scores(q_stack, pos_ref, wk_ref, score_ref, rows, per_device, stride, scale),
-    )
-    factor = jnp.exp(first_top - top)
-    total, acc = window_sums(
-        wv_ref, score_ref, top, total_ref[:, 0:1] * factor, acc_ref[...] * factor
-    )
+    query_pos = lax.broadcasted_iota(jnp.int32, (q_stack.shape[0], 1), 0) % rows
+    nt = (((1,), (1,)), ((), ()))
+    top = top_ref[:, 0:1]
+    total = total_ref[:, 0:1]
+    acc = acc_ref[...]
+    for c in range(wk_ref.shape[0] // CHUNK):
+        keys = wk_ref[pl.ds(c * CHUNK, CHUNK), :]
+        s = lax.dot_general(q_stack, keys, nt, preferred_element_type=jnp.float32) * scale
+        if (c * CHUNK) // stride * per_device < rows:
+            key_pos = pos_ref[:, pl.ds(c * CHUNK, CHUNK)]
+            s = jnp.where(key_pos > query_pos, s, -jnp.inf)
+        new_top = jnp.maximum(top, jnp.max(s, axis=1, keepdims=True))
+        factor = jnp.exp(top - new_top)
+        e = jnp.exp(s - new_top)
+        total = total * factor + jnp.sum(e, axis=1, keepdims=True)
+        acc = acc * factor + jnp.dot(
+            e.astype(jnp.bfloat16),
+            wv_ref[pl.ds(c * CHUNK, CHUNK), :],
+            preferred_element_type=jnp.float32,
+        )
+        top = new_top
     attended = acc / total
     logits = logits_ref[...]
     chosen0 = jnp.sum(jnp.where(pick0_ref[...] != 0, logits, 0.0), axis=0, keepdims=True)

time: 110 us -> 112 us (1.018)
  Pallas kernels: 9.38 us -> 11 us
    pallas_call x1, Pallas kernels: 5.27 us -> 6.9 us  [attend_second(): pl.pallas_call(functools.partial(second_kernel, per_device=per_device, st...]
where the time goes in v14:
time: 112 us; the launch traced here: 111 us
  blocking collectives  30 us (27%)
  starting transfers between devices  29.1 us (26%)
  waiting for transfers between devices  26 us (23%)
  Pallas kernels  11 us (10%)
  other arithmetic  6.43 us (6%)
  local copies, waits for them, and re-layouts  5.98 us (5%)
  between operations  2.58 us (2%)
    psum x1, blocking collectives, body(): logits = lax.psum(partial_value, 'tp')  30 us
    ppermute x4, waiting for transfers between devices, shifted(): return lax.ppermute(value, 'z', pairs)  26 us
    ppermute x4, starting transfers between devices, shifted(): return lax.ppermute(value, 'z', pairs)  17.2 us
    all_to_all x2, starting transfers between devices, body(): lax.all_to_all(outgoing, ('ylo', 'x'), split_axis=0, concat_axis=0, tiled...  12 us
    pallas_call x1, Pallas kernels, attend_second(): pl.pallas_call(functools.partial(second_kernel, per_device=per_device, st...  6.9 us
    pallas_call x1, Pallas kernels, attend_first(): pl.pallas_call(functools.partial(first_kernel, extra_sinks=extra_sinks, p...  4.12 us
    select_n x2, other arithmetic, body(): jnp.where((peer_groups == 0)[:, None, None], data[None, 0], data[None, 1])  3.19 us
    unnamed x22, local copies, waits for them, and re-layouts  2.73 us
  transfers between devices with their start and end apart: 6, of which 3 were waited for; matrix products, arithmetic and copies ran while one was open for 7% of the time, Pallas kernels for 4%

profile of v14, /device:TPU:142, one launch (start us, length us, event | category | flops | bytes accessed | tf_op | source)
XLA Modules:
  0.0 111.3 jit_solution(17857650906860074814)
XLA Ops:
  0.0 0.0 copy-start
  0.0 1.0 reshape.101
  1.0 1.9 %collective-permute-start = (bf16[2,64,512]{2,1,0:T(8,128)(2,1)S(1)}, bf16[2,64,512]{2,1,0:T(8,128)(2,1)S(1)}, u32[]{:S(2)}, u32[]{:S(2)}) collective-permute-start(bf16[2,64,512]{2,1,0:T(8,128)(2,1)S(1)} %reshape.101), channel_id=1, source_target_pairs={{0,448},{64,0},{128,64},{192,128},{256,192},{320,256},{384,320},{4... | collective-permute-start | bytes 393224 | tf_op jit(solution)/shard_map/ppermute | solution.py:248
  3.0 4.3 %collective-permute-start.1 = (bf16[2,64,512]{2,1,0:T(8,128)(2,1)S(1)}, bf16[2,64,512]{2,1,0:T(8,128)(2,1)S(1)}, u32[]{:S(2)}, u32[]{:S(2)}) collective-permute-start(bf16[2,64,512]{2,1,0:T(8,128)(2,1)S(1)} %reshape.101), channel_id=1, source_target_pairs={{0,64},{64,128},{128,192},{192,256},{256,320},{320,384},{384,448},... | collective-permute-start | bytes 393224 | tf_op jit(solution)/shard_map/ppermute | solution.py:248
  7.3 0.7 dynamic-slice_compare_fusion
  8.0 2.1 %collective-permute-done.1 = bf16[2,64,512]{2,1,0:T(8,128)(2,1)S(1)} collective-permute-done((bf16[2,64,512]{2,1,0:T(8,128)(2,1)S(1)}, bf16[2,64,512]{2,1,0:T(8,128)(2,1)S(1)}, u32[]{:S(2)}, u32[]{:S(2)}) %collective-permute-start.1) | collective-permute-done | bytes 131104 | tf_op jit(solution)/shard_map/ppermute | solution.py:248
  10.1 0.0 collective-permute-done
  10.2 1.3 %broadcast_select_fusion.1 = bf16[8,192,512]{2,1,0:T(8,128)(2,1)} fusion(pred[8]{0:T(512)(128)(4,1)S(1)} %dynamic-slice_compare_fusion, bf16[192,512]{1,0:T(8,128)(2,1)S(1)} %get-tuple-element.22, bf16[192,512]{1,0:T(8,128)(2,1)S(1)} %get-tuple-element.21), kind=kLoop, calls=%fused_computation.1 | loop fusion | flops 786432 | bytes 1966088 | tf_op jit(solution)/shard_map/jit(_where)/select_n | solution.py:271
  11.5 6.3 %all-to-all-start.1 = ((bf16[8,192,512]{2,1,0:T(8,128)(2,1)}), bf16[8,192,512]{2,1,0:T(8,128)(2,1)S(1)}, u32[]{:S(2)}, u32[]{:S(2)}) async-start(bf16[8,192,512]{2,1,0:T(8,128)(2,1)} %broadcast_select_fusion.1), calls=%async_computation.1 | async-start | bytes 3145728 | tf_op jit(solution)/shard_map/all_to_all | solution.py:272
  17.8 0.1 pad_maximum_fusion.1
  17.9 7.9 %collective-permute-start.2 = (bf16[2,160,512]{2,1,0:T(8,128)(2,1)S(1)}, bf16[2,160,512]{2,1,0:T(8,128)(2,1)S(1)}, u32[]{:S(2)}, u32[]{:S(2)}) collective-permute-start(bf16[2,160,512]{2,1,0:T(8,128)(2,1)S(1)} %get-tuple-element.24), channel_id=1, source_target_pairs={{0,192},{64,256},{128,320},{192,384},{256,448},{320,0},{384,64},{4... | collective-permute-start | bytes 983048 | tf_op jit(solution)/shard_map/ppermute | solution.py:248
  25.8 3.1 %collective-permute-start.3 = (bf16[2,160,512]{2,1,0:T(8,128)(2,1)S(1)}, bf16[2,160,512]{2,1,0:T(8,128)(2,1)S(1)}, u32[]{:S(2)}, u32[]{:S(2)}) collective-permute-start(bf16[2,160,512]{2,1,0:T(8,128)(2,1)S(1)} %get-tuple-element.23), channel_id=1, source_target_pairs={{0,320},{64,384},{128,448},{192,0},{256,64},{320,128},{384,192},{4... | collective-permute-start | bytes 983048 | tf_op jit(solution)/shard_map/ppermute | solution.py:248
  28.8 14.4 %collective-permute-done.2 = bf16[2,160,512]{2,1,0:T(8,128)(2,1)S(1)} collective-permute-done((bf16[2,160,512]{2,1,0:T(8,128)(2,1)S(1)}, bf16[2,160,512]{2,1,0:T(8,128)(2,1)S(1)}, u32[]{:S(2)}, u32[]{:S(2)}) %collective-permute-start.2) | collective-permute-done | bytes 327712 | tf_op jit(solution)/shard_map/ppermute | solution.py:248
  43.3 9.5 %collective-permute-done.3 = bf16[2,160,512]{2,1,0:T(8,128)(2,1)S(1)} collective-permute-done((bf16[2,160,512]{2,1,0:T(8,128)(2,1)S(1)}, bf16[2,160,512]{2,1,0:T(8,128)(2,1)S(1)}, u32[]{:S(2)}, u32[]{:S(2)}) %collective-permute-start.3) | collective-permute-done | bytes 327712 | tf_op jit(solution)/shard_map/ppermute | solution.py:248
  52.9 1.9 %broadcast_select_fusion = bf16[8,320,512]{2,1,0:T(8,128)(2,1)} fusion(pred[8]{0:T(512)(128)(4,1)S(1)} %dynamic-slice_compare_fusion, bf16[320,512]{1,0:T(8,128)(2,1)S(1)} %get-tuple-element.20, bf16[320,512]{1,0:T(8,128)(2,1)S(1)} %get-tuple-element.19), kind=kLoop, calls=%fused_computation | loop fusion | flops 1310720 | bytes 3276808 | tf_op jit(solution)/shard_map/jit(_where)/select_n | solution.py:271
  54.7 0.0 copy-start.7
  54.7 0.0 copy-start.5
  54.7 0.0 copy-start.3
  54.7 0.0 copy-start.6
  54.7 0.0 copy-start.4
  54.7 0.0 all-to-all-done.1
  54.8 0.0 copy-start.2
  54.8 1.1 %copy-done.2 = bf16[8,192,512]{2,1,0:T(8,128)(2,1)} copy-done((bf16[8,192,512]{2,1,0:T(8,128)(2,1)}, bf16[8,192,512]{2,1,0:T(8,128)(2,1)S(1)}, u32[]{:S(2)}) %copy-start.2) | copy-done | bytes 1572888
  55.9 5.7 %all-to-all-start = ((bf16[8,320,512]{2,1,0:T(8,128)(2,1)}), bf16[8,320,512]{2,1,0:T(8,128)(2,1)S(1)}, u32[]{:S(2)}, u32[]{:S(2)}) async-start(bf16[8,320,512]{2,1,0:T(8,128)(2,1)} %broadcast_select_fusion), calls=%async_computation | async-start | bytes 5242880 | tf_op jit(solution)/shard_map/all_to_all | solution.py:272
  61.7 0.1 iota_add_fusion.3
  61.7 0.1 broadcast_add_fusion
  61.8 0.1 iota_add_fusion
  61.9 0.1 concatenate.25
  62.0 0.1 reshape.99
  62.1 0.1 iota_add_fusion.7
  62.1 0.1 iota_add_fusion.5
  62.2 0.1 pad_add_fusion.1
  62.3 0.1 reshape.98
  62.4 0.6 slice.40.pos_ref
  63.0 0.6 slice.45.pos_ref
  63.6 0.0 copy-done.7
  63.6 0.6 dynamic_slice.11
  65.9 0.0 copy-done.5
  65.9 0.0 copy-done.3
  66.6 0.1 pad.2.clone
  66.7 0.5 compare_convert_fusion.live_ref
  67.2 0.0 copy-done.6
  67.2 0.6 fusion
  67.8 0.0 copy-done
  67.8 0.0 copy-done.4
  67.8 0.1 fusion.2
  67.9 0.8 maximum_maximum_fusion.xk_ref.xv_ref
  68.8 4.1 %shard_map.91 = (f32[2,256,128]{2,1,0:T(8,128)}, f32[2,256,128]{2,1,0:T(8,128)}, f32[2,256,128]{2,1,0:T(8,128)}) custom-call(bf16[128,512]{1,0:T(8,128)(2,1)} %q_ref.3, s32[1,1536]{1,0:T(1,128)} %slice.45.pos_ref, bf16[1536,512]{1,0:T(8,128)(2,1)} %bitcast.29, bf16[1536,512]{1,0:T(8,128)(2,1)} %bitcast.30, ...), custom_call_target="tpu_custom_call" | custom-call | tf_op jit(solution)/shard_map/pallas_call | solution.py:177
  72.9 30.0 %psum.7.logits_ref = f32[8,128]{1,0:T(8,128)} all-reduce(f32[8,128]{1,0:T(8,128)S(1)} %bitcast.36), channel_id=1, replica_groups=mesh['z'=8,'ylo'=2,'x'=4,'tp'=8] {'tp'}, use_global_device_ids=true, to_apply=%region_0.1 | all-reduce | flops 1024 | bytes 8192 | tf_op jit(solution)/shard_map/psum | solution.py:300
  102.9 0.0 all-to-all-done
  102.9 0.0 copy-start.1
  102.9 1.5 %copy-done.1 = bf16[8,320,512]{2,1,0:T(8,128)(2,1)} copy-done((bf16[8,320,512]{2,1,0:T(8,128)(2,1)}, bf16[8,320,512]{2,1,0:T(8,128)(2,1)S(1)}, u32[]{:S(2)}) %copy-start.1) | copy-done | bytes 2621464
  104.4 6.9 %shard_map.92 = bf16[128,512]{1,0:T(8,128)(2,1)} custom-call(bf16[128,512]{1,0:T(8,128)(2,1)} %q_ref.3, s32[1,2560]{1,0:T(1,128)} %slice.40.pos_ref, bf16[2560,512]{1,0:T(8,128)(2,1)} %bitcast.27, bf16[2560,512]{1,0:T(8,128)(2,1)} %bitcast.28, f32[2,256,128]{2,1,0:T(8,128)} %get-tuple-element.15.acc_ref, f32[2,256,128]{2,1,0:T(8,128)} %get-tuple-element.16.top_ref, ...), custom_call_target="tpu_custom_call" | custom-call | tf_op jit(solution)/shard_map/pallas_call | solution.py:214
  (24 shorter events, 0.3 us)
Async XLA Ops:
  0.0 67.8 %copy-start = (bf16[128,256]{1,0:T(8,128)(2,1)S(1)}, bf16[128,256]{1,0:T(8,128)(2,1)}, u32[]{:S(2)}) copy-start(bf16[128,256]{1,0:T(8,128)(2,1)} %param.15) | copy-start | bytes 196612
  1.0 9.1 %collective-permute-start = (bf16[2,64,512]{2,1,0:T(8,128)(2,1)S(1)}, bf16[2,64,512]{2,1,0:T(8,128)(2,1)S(1)}, u32[]{:S(2)}, u32[]{:S(2)}) collective-permute-start(bf16[2,64,512]{2,1,0:T(8,128)(2,1)S(1)} %reshape.101), channel_id=1, source_target_pairs={{0,448},{64,0},{128,64},{192,128},{256,192},{320,256},{384,320},{4... | collective-permute-start | bytes 393224 | tf_op jit(solution)/shard_map/ppermute | solution.py:248
  3.0 7.1 %collective-permute-start.1 = (bf16[2,64,512]{2,1,0:T(8,128)(2,1)S(1)}, bf16[2,64,512]{2,1,0:T(8,128)(2,1)S(1)}, u32[]{:S(2)}, u32[]{:S(2)}) collective-permute-start(bf16[2,64,512]{2,1,0:T(8,128)(2,1)S(1)} %reshape.101), channel_id=1, source_target_pairs={{0,64},{64,128},{128,192},{192,256},{256,320},{320,384},{384,448},... | collective-permute-start | bytes 393224 | tf_op jit(solution)/shard_map/ppermute | solution.py:248
  11.5 43.2 %all-to-all-start.1 = ((bf16[8,192,512]{2,1,0:T(8,128)(2,1)}), bf16[8,192,512]{2,1,0:T(8,128)(2,1)S(1)}, u32[]{:S(2)}, u32[]{:S(2)}) async-start(bf16[8,192,512]{2,1,0:T(8,128)(2,1)} %broadcast_select_fusion.1), calls=%async_computation.1 | async-start | bytes 3145728 | tf_op jit(solution)/shard_map/all_to_all | solution.py:272
  17.9 25.4 %collective-permute-start.2 = (bf16[2,160,512]{2,1,0:T(8,128)(2,1)S(1)}, bf16[2,160,512]{2,1,0:T(8,128)(2,1)S(1)}, u32[]{:S(2)}, u32[]{:S(2)}) collective-permute-start(bf16[2,160,512]{2,1,0:T(8,128)(2,1)S(1)} %get-tuple-element.24), channel_id=1, source_target_pairs={{0,192},{64,256},{128,320},{192,384},{256,448},{320,0},{384,64},{4... | collective-permute-start | bytes 983048 | tf_op jit(solution)/shard_map/ppermute | solution.py:248
  25.8 27.0 %collective-permute-start.3 = (bf16[2,160,512]{2,1,0:T(8,128)(2,1)S(1)}, bf16[2,160,512]{2,1,0:T(8,128)(2,1)S(1)}, u32[]{:S(2)}, u32[]{:S(2)}) collective-permute-start(bf16[2,160,512]{2,1,0:T(8,128)(2,1)S(1)} %get-tuple-element.23), channel_id=1, source_target_pairs={{0,320},{64,384},{128,448},{192,0},{256,64},{320,128},{384,192},{4... | collective-permute-start | bytes 983048 | tf_op jit(solution)/shard_map/ppermute | solution.py:248
  54.7 8.9 %copy-start.7 = (s32[64]{0:T(128)S(1)}, s32[64]{0:T(128)}, u32[]{:S(2)}) copy-start(s32[64]{0:T(128)} %param.14) | copy-start | bytes 772
  54.7 11.1 %copy-start.5 = (bf16[2,4,2,256]{3,2,1,0:T(2,128)(2,1)S(1)}, bf16[2,4,2,256]{3,2,1,0:T(2,128)(2,1)}, u32[]{:S(2)}) copy-start(bf16[2,4,2,256]{3,2,1,0:T(2,128)(2,1)} %param.12) | copy-start | bytes 24580
  54.7 11.2 %copy-start.3 = (bf16[128,2,256]{2,1,0:T(2,128)(2,1)S(1)}, bf16[128,2,256]{2,1,0:T(2,128)(2,1)}, u32[]{:S(2)}) copy-start(bf16[128,2,256]{2,1,0:T(2,128)(2,1)} %param.10) | copy-start | bytes 393220
  54.7 12.5 %copy-start.6 = (s32[128,2]{0,1:T(2,128)S(1)}, s32[128,2]{0,1:T(2,128)}, u32[]{:S(2)}) copy-start(s32[128,2]{0,1:T(2,128)} %param.17) | copy-start | bytes 3076
  54.7 13.1 %copy-start.4 = (bf16[256,8]{0,1:T(8,128)(2,1)S(1)}, bf16[256,8]{0,1:T(8,128)(2,1)}, u32[]{:S(2)}) copy-start(bf16[256,8]{0,1:T(8,128)(2,1)} %param.16) | copy-start | bytes 12292
  54.8 1.1 %copy-start.2 = (bf16[8,192,512]{2,1,0:T(8,128)(2,1)}, bf16[8,192,512]{2,1,0:T(8,128)(2,1)S(1)}, u32[]{:S(2)}) copy-start(bf16[8,192,512]{2,1,0:T(8,128)(2,1)S(1)} %all-to-all-done.1) | copy-start | bytes 4718596
  55.9 47.0 %all-to-all-start = ((bf16[8,320,512]{2,1,0:T(8,128)(2,1)}), bf16[8,320,512]{2,1,0:T(8,128)(2,1)S(1)}, u32[]{:S(2)}, u32[]{:S(2)}) async-start(bf16[8,320,512]{2,1,0:T(8,128)(2,1)} %broadcast_select_fusion), calls=%async_computation | async-start | bytes 5242880 | tf_op jit(solution)/shard_map/all_to_all | solution.py:272
  102.9 1.5 %copy-start.1 = (bf16[8,320,512]{2,1,0:T(8,128)(2,1)}, bf16[8,320,512]{2,1,0:T(8,128)(2,1)S(1)}, u32[]{:S(2)}) copy-start(bf16[8,320,512]{2,1,0:T(8,128)(2,1)S(1)} %all-to-all-done) | copy-start | bytes 7864324

commit v15 on v13

--- a/solution.py
+++ b/solution.py
@@ -10,7 +10,7 @@
 
 HEAD_DIM = 128
 PICKS = 2
-CHUNK = 512
+CHUNK = 256
 
 
 def stacked_queries(q_ref):

time: 110 us -> 110 us (level)
  no operation moved by 1% of the time
where the time goes in v15:
time: 110 us
  blocking collectives  30 us (27%)
  starting transfers between devices  29.1 us (26%)
  waiting for transfers between devices  26 us (24%)
  Pallas kernels  9.41 us (9%)
  other arithmetic  6.43 us (6%)
  local copies, waits for them, and re-layouts  5.98 us (5%)
  between operations  2.58 us (2%)
    psum x1, blocking collectives, body(): logits = lax.psum(partial_value, 'tp')  30 us
    ppermute x4, waiting for transfers between devices, shifted(): return lax.ppermute(value, 'z', pairs)  26 us
    ppermute x4, starting transfers between devices, shifted(): return lax.ppermute(value, 'z', pairs)  17.2 us
    all_to_all x2, starting transfers between devices, body(): lax.all_to_all(outgoing, ('ylo', 'x'), split_axis=0, concat_axis=0, tiled...  12 us
    pallas_call x1, Pallas kernels, attend_second(): pl.pallas_call(functools.partial(second_kernel, per_device=per_device, st...  5.26 us
    pallas_call x1, Pallas kernels, attend_first(): pl.pallas_call(functools.partial(first_kernel, extra_sinks=extra_sinks, p...  4.15 us
    select_n x2, other arithmetic, body(): jnp.where((peer_groups == 0)[:, None, None], data[None, 0], data[None, 1])  3.19 us
    unnamed x22, local copies, waits for them, and re-layouts  2.73 us
  transfers between devices with their start and end apart: 6, of which 3 were waited for; matrix products, arithmetic and copies ran while one was open for 7% of the time, Pallas kernels for 4%

profile of v15, /device:TPU:142, one launch (start us, length us, event | category | flops | bytes accessed | tf_op | source)
XLA Modules:
  0.0 109.7 jit_solution(7321180456199856381)
XLA Ops:
  0.0 0.0 copy-start
  0.0 1.0 reshape.101
  1.0 1.9 %collective-permute-start = (bf16[2,64,512]{2,1,0:T(8,128)(2,1)S(1)}, bf16[2,64,512]{2,1,0:T(8,128)(2,1)S(1)}, u32[]{:S(2)}, u32[]{:S(2)}) collective-permute-start(bf16[2,64,512]{2,1,0:T(8,128)(2,1)S(1)} %reshape.101), channel_id=1, source_target_pairs={{0,448},{64,0},{128,64},{192,128},{256,192},{320,256},{384,320},{4... | collective-permute-start | bytes 393224 | tf_op jit(solution)/shard_map/ppermute | solution.py:236
  3.0 4.3 %collective-permute-start.1 = (bf16[2,64,512]{2,1,0:T(8,128)(2,1)S(1)}, bf16[2,64,512]{2,1,0:T(8,128)(2,1)S(1)}, u32[]{:S(2)}, u32[]{:S(2)}) collective-permute-start(bf16[2,64,512]{2,1,0:T(8,128)(2,1)S(1)} %reshape.101), channel_id=1, source_target_pairs={{0,64},{64,128},{128,192},{192,256},{256,320},{320,384},{384,448},... | collective-permute-start | bytes 393224 | tf_op jit(solution)/shard_map/ppermute | solution.py:236
  7.3 0.7 dynamic-slice_compare_fusion
  8.0 2.1 %collective-permute-done.1 = bf16[2,64,512]{2,1,0:T(8,128)(2,1)S(1)} collective-permute-done((bf16[2,64,512]{2,1,0:T(8,128)(2,1)S(1)}, bf16[2,64,512]{2,1,0:T(8,128)(2,1)S(1)}, u32[]{:S(2)}, u32[]{:S(2)}) %collective-permute-start.1) | collective-permute-done | bytes 131104 | tf_op jit(solution)/shard_map/ppermute | solution.py:236
  10.1 0.0 collective-permute-done
  10.2 1.3 %broadcast_select_fusion.1 = bf16[8,192,512]{2,1,0:T(8,128)(2,1)} fusion(pred[8]{0:T(512)(128)(4,1)S(1)} %dynamic-slice_compare_fusion, bf16[192,512]{1,0:T(8,128)(2,1)S(1)} %get-tuple-element.22, bf16[192,512]{1,0:T(8,128)(2,1)S(1)} %get-tuple-element.21), kind=kLoop, calls=%fused_computation.1 | loop fusion | flops 786432 | bytes 1966088 | tf_op jit(solution)/shard_map/jit(_where)/select_n | solution.py:259
  11.5 6.3 %all-to-all-start.1 = ((bf16[8,192,512]{2,1,0:T(8,128)(2,1)}), bf16[8,192,512]{2,1,0:T(8,128)(2,1)S(1)}, u32[]{:S(2)}, u32[]{:S(2)}) async-start(bf16[8,192,512]{2,1,0:T(8,128)(2,1)} %broadcast_select_fusion.1), calls=%async_computation.1 | async-start | bytes 3145728 | tf_op jit(solution)/shard_map/all_to_all | solution.py:260
  17.8 0.1 pad_maximum_fusion.1
  17.9 7.9 %collective-permute-start.2 = (bf16[2,160,512]{2,1,0:T(8,128)(2,1)S(1)}, bf16[2,160,512]{2,1,0:T(8,128)(2,1)S(1)}, u32[]{:S(2)}, u32[]{:S(2)}) collective-permute-start(bf16[2,160,512]{2,1,0:T(8,128)(2,1)S(1)} %get-tuple-element.24), channel_id=1, source_target_pairs={{0,192},{64,256},{128,320},{192,384},{256,448},{320,0},{384,64},{4... | collective-permute-start | bytes 983048 | tf_op jit(solution)/shard_map/ppermute | solution.py:236
  25.8 3.1 %collective-permute-start.3 = (bf16[2,160,512]{2,1,0:T(8,128)(2,1)S(1)}, bf16[2,160,512]{2,1,0:T(8,128)(2,1)S(1)}, u32[]{:S(2)}, u32[]{:S(2)}) collective-permute-start(bf16[2,160,512]{2,1,0:T(8,128)(2,1)S(1)} %get-tuple-element.23), channel_id=1, source_target_pairs={{0,320},{64,384},{128,448},{192,0},{256,64},{320,128},{384,192},{4... | collective-permute-start | bytes 983048 | tf_op jit(solution)/shard_map/ppermute | solution.py:236
  28.8 14.4 %collective-permute-done.2 = bf16[2,160,512]{2,1,0:T(8,128)(2,1)S(1)} collective-permute-done((bf16[2,160,512]{2,1,0:T(8,128)(2,1)S(1)}, bf16[2,160,512]{2,1,0:T(8,128)(2,1)S(1)}, u32[]{:S(2)}, u32[]{:S(2)}) %collective-permute-start.2) | collective-permute-done | bytes 327712 | tf_op jit(solution)/shard_map/ppermute | solution.py:236
  43.3 9.5 %collective-permute-done.3 = bf16[2,160,512]{2,1,0:T(8,128)(2,1)S(1)} collective-permute-done((bf16[2,160,512]{2,1,0:T(8,128)(2,1)S(1)}, bf16[2,160,512]{2,1,0:T(8,128)(2,1)S(1)}, u32[]{:S(2)}, u32[]{:S(2)}) %collective-permute-start.3) | collective-permute-done | bytes 327712 | tf_op jit(solution)/shard_map/ppermute | solution.py:236
  52.9 1.9 %broadcast_select_fusion = bf16[8,320,512]{2,1,0:T(8,128)(2,1)} fusion(pred[8]{0:T(512)(128)(4,1)S(1)} %dynamic-slice_compare_fusion, bf16[320,512]{1,0:T(8,128)(2,1)S(1)} %get-tuple-element.20, bf16[320,512]{1,0:T(8,128)(2,1)S(1)} %get-tuple-element.19), kind=kLoop, calls=%fused_computation | loop fusion | flops 1310720 | bytes 3276808 | tf_op jit(solution)/shard_map/jit(_where)/select_n | solution.py:259
  54.7 0.0 copy-start.7
  54.7 0.0 copy-start.5
  54.7 0.0 copy-start.3
  54.7 0.0 copy-start.6
  54.7 0.0 copy-start.4
  54.7 0.0 all-to-all-done.1
  54.8 0.0 copy-start.2
  54.8 1.1 %copy-done.2 = bf16[8,192,512]{2,1,0:T(8,128)(2,1)} copy-done((bf16[8,192,512]{2,1,0:T(8,128)(2,1)}, bf16[8,192,512]{2,1,0:T(8,128)(2,1)S(1)}, u32[]{:S(2)}) %copy-start.2) | copy-done | bytes 1572888
  55.9 5.7 %all-to-all-start = ((bf16[8,320,512]{2,1,0:T(8,128)(2,1)}), bf16[8,320,512]{2,1,0:T(8,128)(2,1)S(1)}, u32[]{:S(2)}, u32[]{:S(2)}) async-start(bf16[8,320,512]{2,1,0:T(8,128)(2,1)} %broadcast_select_fusion), calls=%async_computation | async-start | bytes 5242880 | tf_op jit(solution)/shard_map/all_to_all | solution.py:260
  61.7 0.1 iota_add_fusion.3
  61.7 0.1 broadcast_add_fusion
  61.8 0.1 iota_add_fusion
  61.9 0.1 concatenate.25
  62.0 0.1 reshape.99
  62.1 0.1 iota_add_fusion.7
  62.1 0.1 iota_add_fusion.5
  62.2 0.1 pad_add_fusion.1
  62.3 0.1 reshape.98
  62.4 0.6 slice.40.pos_ref
  63.0 0.6 slice.45.pos_ref
  63.6 0.0 copy-done.7
  63.6 0.6 dynamic_slice.11
  65.9 0.0 copy-done.5
  65.9 0.0 copy-done.3
  66.6 0.1 pad.2.clone
  66.7 0.5 compare_convert_fusion.live_ref
  67.2 0.0 copy-done.6
  67.2 0.6 fusion
  67.8 0.0 copy-done
  67.8 0.0 copy-done.4
  67.8 0.1 fusion.2
  67.9 0.8 maximum_maximum_fusion.xk_ref.xv_ref
  68.8 4.1 %shard_map.91 = (f32[2,256,128]{2,1,0:T(8,128)}, f32[2,256,128]{2,1,0:T(8,128)}, f32[2,256,128]{2,1,0:T(8,128)}) custom-call(bf16[128,512]{1,0:T(8,128)(2,1)} %q_ref.3, s32[1,1536]{1,0:T(1,128)} %slice.45.pos_ref, bf16[1536,512]{1,0:T(8,128)(2,1)} %bitcast.29, bf16[1536,512]{1,0:T(8,128)(2,1)} %bitcast.30, ...), custom_call_target="tpu_custom_call" | custom-call | tf_op jit(solution)/shard_map/pallas_call | solution.py:165
  72.9 30.0 %psum.7.logits_ref = f32[8,128]{1,0:T(8,128)} all-reduce(f32[8,128]{1,0:T(8,128)S(1)} %bitcast.36), channel_id=1, replica_groups=mesh['z'=8,'ylo'=2,'x'=4,'tp'=8] {'tp'}, use_global_device_ids=true, to_apply=%region_0.1 | all-reduce | flops 1024 | bytes 8192 | tf_op jit(solution)/shard_map/psum | solution.py:288
  102.9 0.0 all-to-all-done
  102.9 0.0 copy-start.1
  102.9 1.5 %copy-done.1 = bf16[8,320,512]{2,1,0:T(8,128)(2,1)} copy-done((bf16[8,320,512]{2,1,0:T(8,128)(2,1)}, bf16[8,320,512]{2,1,0:T(8,128)(2,1)S(1)}, u32[]{:S(2)}) %copy-start.1) | copy-done | bytes 2621464
  104.4 5.3 %shard_map.92 = bf16[128,512]{1,0:T(8,128)(2,1)} custom-call(bf16[128,512]{1,0:T(8,128)(2,1)} %q_ref.3, s32[1,2560]{1,0:T(1,128)} %slice.40.pos_ref, bf16[2560,512]{1,0:T(8,128)(2,1)} %bitcast.27, bf16[2560,512]{1,0:T(8,128)(2,1)} %bitcast.28, f32[2,256,128]{2,1,0:T(8,128)} %get-tuple-element.15.acc_ref, f32[2,256,128]{2,1,0:T(8,128)} %get-tuple-element.16.top_ref, ...), custom_call_target="tpu_custom_call" | custom-call | tf_op jit(solution)/shard_map/pallas_call | solution.py:202
  (24 shorter events, 0.3 us)
Async XLA Ops:
  0.0 67.8 %copy-start = (bf16[128,256]{1,0:T(8,128)(2,1)S(1)}, bf16[128,256]{1,0:T(8,128)(2,1)}, u32[]{:S(2)}) copy-start(bf16[128,256]{1,0:T(8,128)(2,1)} %param.15) | copy-start | bytes 196612
  1.0 9.1 %collective-permute-start = (bf16[2,64,512]{2,1,0:T(8,128)(2,1)S(1)}, bf16[2,64,512]{2,1,0:T(8,128)(2,1)S(1)}, u32[]{:S(2)}, u32[]{:S(2)}) collective-permute-start(bf16[2,64,512]{2,1,0:T(8,128)(2,1)S(1)} %reshape.101), channel_id=1, source_target_pairs={{0,448},{64,0},{128,64},{192,128},{256,192},{320,256},{384,320},{4... | collective-permute-start | bytes 393224 | tf_op jit(solution)/shard_map/ppermute | solution.py:236
  3.0 7.1 %collective-permute-start.1 = (bf16[2,64,512]{2,1,0:T(8,128)(2,1)S(1)}, bf16[2,64,512]{2,1,0:T(8,128)(2,1)S(1)}, u32[]{:S(2)}, u32[]{:S(2)}) collective-permute-start(bf16[2,64,512]{2,1,0:T(8,128)(2,1)S(1)} %reshape.101), channel_id=1, source_target_pairs={{0,64},{64,128},{128,192},{192,256},{256,320},{320,384},{384,448},... | collective-permute-start | bytes 393224 | tf_op jit(solution)/shard_map/ppermute | solution.py:236
  11.5 43.2 %all-to-all-start.1 = ((bf16[8,192,512]{2,1,0:T(8,128)(2,1)}), bf16[8,192,512]{2,1,0:T(8,128)(2,1)S(1)}, u32[]{:S(2)}, u32[]{:S(2)}) async-start(bf16[8,192,512]{2,1,0:T(8,128)(2,1)} %broadcast_select_fusion.1), calls=%async_computation.1 | async-start | bytes 3145728 | tf_op jit(solution)/shard_map/all_to_all | solution.py:260
  17.9 25.4 %collective-permute-start.2 = (bf16[2,160,512]{2,1,0:T(8,128)(2,1)S(1)}, bf16[2,160,512]{2,1,0:T(8,128)(2,1)S(1)}, u32[]{:S(2)}, u32[]{:S(2)}) collective-permute-start(bf16[2,160,512]{2,1,0:T(8,128)(2,1)S(1)} %get-tuple-element.24), channel_id=1, source_target_pairs={{0,192},{64,256},{128,320},{192,384},{256,448},{320,0},{384,64},{4... | collective-permute-start | bytes 983048 | tf_op jit(solution)/shard_map/ppermute | solution.py:236
  25.8 27.0 %collective-permute-start.3 = (bf16[2,160,512]{2,1,0:T(8,128)(2,1)S(1)}, bf16[2,160,512]{2,1,0:T(8,128)(2,1)S(1)}, u32[]{:S(2)}, u32[]{:S(2)}) collective-permute-start(bf16[2,160,512]{2,1,0:T(8,128)(2,1)S(1)} %get-tuple-element.23), channel_id=1, source_target_pairs={{0,320},{64,384},{128,448},{192,0},{256,64},{320,128},{384,192},{4... | collective-permute-start | bytes 983048 | tf_op jit(solution)/shard_map/ppermute | solution.py:236
  54.7 8.9 %copy-start.7 = (s32[64]{0:T(128)S(1)}, s32[64]{0:T(128)}, u32[]{:S(2)}) copy-start(s32[64]{0:T(128)} %param.14) | copy-start | bytes 772
  54.7 11.1 %copy-start.5 = (bf16[2,4,2,256]{3,2,1,0:T(2,128)(2,1)S(1)}, bf16[2,4,2,256]{3,2,1,0:T(2,128)(2,1)}, u32[]{:S(2)}) copy-start(bf16[2,4,2,256]{3,2,1,0:T(2,128)(2,1)} %param.12) | copy-start | bytes 24580
  54.7 11.2 %copy-start.3 = (bf16[128,2,256]{2,1,0:T(2,128)(2,1)S(1)}, bf16[128,2,256]{2,1,0:T(2,128)(2,1)}, u32[]{:S(2)}) copy-start(bf16[128,2,256]{2,1,0:T(2,128)(2,1)} %param.10) | copy-start | bytes 393220
  54.7 12.5 %copy-start.6 = (s32[128,2]{0,1:T(2,128)S(1)}, s32[128,2]{0,1:T(2,128)}, u32[]{:S(2)}) copy-start(s32[128,2]{0,1:T(2,128)} %param.17) | copy-start | bytes 3076
  54.7 13.1 %copy-start.4 = (bf16[256,8]{0,1:T(8,128)(2,1)S(1)}, bf16[256,8]{0,1:T(8,128)(2,1)}, u32[]{:S(2)}) copy-start(bf16[256,8]{0,1:T(8,128)(2,1)} %param.16) | copy-start | bytes 12292
  54.8 1.1 %copy-start.2 = (bf16[8,192,512]{2,1,0:T(8,128)(2,1)}, bf16[8,192,512]{2,1,0:T(8,128)(2,1)S(1)}, u32[]{:S(2)}) copy-start(bf16[8,192,512]{2,1,0:T(8,128)(2,1)S(1)} %all-to-all-done.1) | copy-start | bytes 4718596
  55.9 47.0 %all-to-all-start = ((bf16[8,320,512]{2,1,0:T(8,128)(2,1)}), bf16[8,320,512]{2,1,0:T(8,128)(2,1)S(1)}, u32[]{:S(2)}, u32[]{:S(2)}) async-start(bf16[8,320,512]{2,1,0:T(8,128)(2,1)} %broadcast_select_fusion), calls=%async_computation | async-start | bytes 5242880 | tf_op jit(solution)/shard_map/all_to_all | solution.py:260
  102.9 1.5 %copy-start.1 = (bf16[8,320,512]{2,1,0:T(8,128)(2,1)}, bf16[8,320,512]{2,1,0:T(8,128)(2,1)S(1)}, u32[]{:S(2)}) copy-start(bf16[8,320,512]{2,1,0:T(8,128)(2,1)S(1)} %all-to-all-done) | copy-start | bytes 7864324
